TPU v7x, 256 devices: a whole 4x4x8 slice. The times are simulated.
256 devices in a mesh: dp: 4 (over y), expert: 64 (over x, z, core).
Axes of the slice: x: 4, y: 4, z: 8, core: 2. Of those that a mesh axis runs over, the one named last changes fastest.
Arguments:
- hidden: bfloat16 [32768, 2, 1024], P(('dp', 'expert')), may hold values from -6 to 6
- routes: int32 [32768, 2], P(('dp', 'expert')), may hold values from 0 to 63, all different within a row; in each aligned block of 128 rows (0 to 127, 128 to 255, ...) at most 8 rows name the same one
- gates: float32 [32768, 2], P(('dp', 'expert')), may hold values from 0.1 to 1
- cotangent: bfloat16 [32768, 7168], P(('dp', 'expert')), may hold values from -1.796875 to 1.796875
- weight: bfloat16 [64, 1024, 7168], P('expert', None, 'dp'), may hold values from -0.0625 to 0.0625
Outputs:
- grad_hidden: bfloat16 [32768, 2, 1024], P(('dp', 'expert'))
- grad_gates: float32 [32768, 2], P(('dp', 'expert'))
- grad_weight: bfloat16 [64, 1024, 7168], P('expert', None, 'dp')
Inputs may be any that keep to these rules, and one draw needn't show every extreme that they name: `routes`: each row names 2 different experts; in each aligned block of 128 rows (the rows of one device) no expert is named by more than 8 rows, a bound that some block reaches.
All inputs are finite; a program needn't handle non-finite values.
Results may differ from a plain program's by a relative error of at most 0.0049.
Values may be sent and summed in bfloat16 or wider, within the bound.
No kernel may reach another device: no remote copies, remote signals or barrier semaphores. Data moves between devices by JAX's collectives and lax.ppermute only.
A program may use at most 128 MiB of HBM per device.

v0:
```python
import jax
import jax.numpy as jnp
from jax import lax
from jax.sharding import PartitionSpec as P


def per_device(hidden, routes, gates, cotangent, weight):
    local_tokens, top_count, hidden_width = hidden.shape
    columns = lax.axis_size("expert")
    capacity = min(local_tokens, 2 * local_tokens * top_count // columns)
    slot_count = local_tokens * top_count
    flat_experts = routes.reshape(slot_count)
    one_hot = (flat_experts[:, None] == jnp.arange(columns, dtype=jnp.int32)[None, :]).astype(
        jnp.int32
    )
    earlier = jnp.cumsum(one_hot, axis=0) - one_hot
    position = jnp.sum(earlier * one_hot, axis=1)
    destination = flat_experts * capacity + position
    slot_of = (
        jnp.full((columns * capacity,), slot_count, jnp.int32)
        .at[destination]
        .set(jnp.arange(slot_count, dtype=jnp.int32))
    )
    scaled = (
        (gates[:, :, None] * hidden.astype(jnp.float32))
        .astype(jnp.bfloat16)
        .reshape(slot_count, hidden_width)
    )
    scaled = jnp.concatenate([scaled, jnp.zeros((1, hidden_width), jnp.bfloat16)], axis=0)
    cot_pad = jnp.concatenate([cotangent, jnp.zeros((1, cotangent.shape[1]), jnp.bfloat16)], axis=0)
    send_rows = scaled[slot_of].reshape(columns, capacity, hidden_width)
    send_cot = cot_pad[slot_of // top_count].reshape(columns, capacity, cotangent.shape[1])
    got_rows, got_cot = (
        lax.all_to_all(send_rows, "expert", split_axis=0, concat_axis=0, tiled=True),
        lax.all_to_all(send_cot, "expert", split_axis=0, concat_axis=0, tiled=True),
    )
    cot_quarter = lax.all_to_all(got_cot[None], "dp", split_axis=3, concat_axis=0, tiled=True)
    rows_all = lax.all_gather(got_rows[None], "dp", axis=0, tiled=True)
    matrix = weight[0]
    partial_back = jnp.einsum(
        "bscd,fd->bscf", cot_quarter, matrix, preferred_element_type=jnp.float32
    )
    summed = lax.psum_scatter(partial_back, "dp", scatter_dimension=0, tiled=True)
    grad_matrix = jnp.einsum(
        "bscf,bscd->fd", rows_all, cot_quarter, preferred_element_type=jnp.float32
    )
    returned = lax.all_to_all(summed[0], "expert", split_axis=0, concat_axis=0, tiled=True)
    back = returned.reshape(columns * capacity, hidden_width)[destination]
    grad_hidden = (
        (gates.reshape(slot_count)[:, None] * back)
        .astype(jnp.bfloat16)
        .reshape(local_tokens, top_count, hidden_width)
    )
    grad_gates = jnp.sum(
        hidden.reshape(slot_count, hidden_width).astype(jnp.float32) * back, axis=1
    ).reshape(local_tokens, top_count)
    return (grad_hidden, grad_gates, grad_matrix.astype(jnp.bfloat16)[None])


def solution(mesh):
    placed = (
        P(("dp", "expert"), None, None),
        P(("dp", "expert"), None),
        P(("dp", "expert"), None),
        P(("dp", "expert"), None),
        P("expert", None, "dp"),
    )
    return jax.shard_map(
        per_device,
        mesh=mesh,
        in_specs=placed,
        out_specs=(
            P(("dp", "expert"), None, None),
            P(("dp", "expert"), None),
            P("expert", None, "dp"),
        ),
        check_vma=False,
    )
```

profile of v0, /device:TPU:1, one launch (start us, length us, event | category | flops | bytes accessed | tf_op | source)
XLA Modules:
  0.0 613.7 jit_solution(7053803963562707793)
XLA Ops:
  7.2 0.0 reduce-scatter.2.cloned.1.call-start
  7.2 0.8 copy.29
  8.0 0.1 eq.29
  8.1 0.1 eq.25
  8.3 0.7 broadcast_multiply_fusion
  9.0 0.6 reduce-window.6
  9.6 0.2 slice_reduce_fusion
  9.8 0.1 copy.28
  9.9 0.1 mul.41
  10.1 0.1 fusion.14
  10.2 1.4 scatter_custom_fusion
  11.6 1.7 concatenate.6
  13.3 7.1 %gather_fusion = bf16[512,7168]{1,0:T(8,128)(2,1)} fusion(bf16[129,7168]{1,0:T(8,128)(2,1)S(1)} %concatenate.6, s32[1024]{0:T(1024)S(1)} %get-tuple-element.15), kind=kCustom, calls=%fused_computation | custom fusion | bytes 14682112 | tf_op jit(solution)/shard_map/gather | solution.py:32
  20.4 176.4 %all_to_all.33 = bf16[64,8,7168]{2,1,0:T(8,128)(2,1)} all-to-all(bf16[64,8,7168]{2,1,0:T(8,128)(2,1)} %bitcast.60), channel_id=1, replica_groups=mesh['dp'=4,'expert'=64] {'expert'}, dimensions={0} | all-to-all | bytes 14680064 | tf_op jit(solution)/shard_map/all_to_all | solution.py:35
  196.8 19.3 %copy.32 = bf16[1,64,8,7168]{1,2,0,3:T(8,128)(2,1)} copy(bf16[1,64,8,7168]{3,2,1,0:T(8,128)(2,1)} %bitcast.61) | data formatting | bytes 14680064 | tf_op jit(solution)/shard_map/broadcast_in_dim | solution.py:37
  216.1 14.8 %reshape.123 = bf16[4,2,458752]{2,1,0:T(2,128)(2,1)} reshape(bf16[7168,1,8,64]{3,2,1,0:T(8,128)(2,1)} %bitcast.57) | data formatting | bytes 14680064
  230.9 90.1 %all_to_all.34 = bf16[4,2,458752]{2,1,0:T(2,128)(2,1)} all-to-all(bf16[4,2,458752]{2,1,0:T(2,128)(2,1)} %reshape.123), channel_id=1, replica_groups=mesh['dp'=4,'expert'=64] {'dp'}, dimensions={0} | all-to-all | bytes 14680064 | tf_op jit(solution)/shard_map/all_to_all | solution.py:37
  321.0 14.3 %reshape.124 = bf16[7168,1,8,64]{3,2,1,0:T(8,128)(2,1)} reshape(bf16[4,2,458752]{2,1,0:T(2,128)(2,1)} %all_to_all.34) | data formatting | bytes 14680064
  335.3 17.7 %copy.34 = bf16[1,64,8,4,1792]{4,2,1,3,0:T(8,128)(2,1)} copy(bf16[1,64,8,4,1792]{1,2,4,3,0:T(8,128)(2,1)} %bitcast.58) | data formatting | bytes 14680064 | tf_op jit(solution)/shard_map/all_to_all | solution.py:37
  353.1 13.2 %fusion.2 = f32[4,64,8,1024]{3,2,1,0:T(8,128)} fusion(bf16[1,64,8,4,1792]{4,2,1,3,0:T(8,128)(2,1)} %copy.34, bf16[1,1024,1792]{2,1,0:T(8,128)(2,1)} %param.9), kind=kOutput, calls=%fused_computation.7 | convolution fusion | flops 7516192768 | bytes 19398656 | tf_op jit(solution)/shard_map/bscd,fd->bscf/dot_general | solution.py:40
  366.2 0.0 copy-start
  366.3 0.0 reduce-scatter.2.cloned.1.call-update
  366.3 78.2 %reduce-scatter.2.cloned.1.call-done = f32[1,64,8,1024]{3,2,1,0:T(8,128)} async-done(((f32[4,64,8,1024]{3,2,1,0:T(8,128)}), f32[1,64,8,1024]{3,2,1,0:T(8,128)}) %reduce-scatter.2.cloned.1.call-update) | async-done | bytes 2097168 | tf_op jit(solution)/shard_map/reduce_scatter | solution.py:43
  444.5 10.7 %all-to-all-start.2 = ((f32[64,8,1024]{2,1,0:T(8,128)}), f32[64,8,1024]{2,1,0:T(8,128)S(1)}, u32[]{:S(2)}, u32[]{:S(2)}) async-start(f32[64,8,1024]{2,1,0:T(8,128)} %bitcast.63), calls=%async_computation.3 | async-start | bytes 4194304 | tf_op jit(solution)/shard_map/all_to_all | solution.py:47
  455.2 0.0 all-gather.3.cloned.1.call-start
  455.3 0.0 copy-done
  455.3 0.1 copy.27
  455.4 51.0 %all-to-all-done.2 = f32[64,8,1024]{2,1,0:T(8,128)S(1)} async-done(((f32[64,8,1024]{2,1,0:T(8,128)}), f32[64,8,1024]{2,1,0:T(8,128)S(1)}, u32[]{:S(2)}, u32[]{:S(2)}) %all-to-all-start.2) | async-done | bytes 2097184 | tf_op jit(solution)/shard_map/all_to_all | solution.py:47
  506.4 1.1 gather_fusion.1
  507.5 0.6 gather.13
  508.1 3.0 fusion.10
  511.2 0.2 reshape.81
  511.4 2.1 gather_fusion.2
  513.5 34.3 %all_to_all.35 = bf16[64,8,1024]{2,1,0:T(8,128)(2,1)} all-to-all(bf16[64,8,1024]{2,1,0:T(8,128)(2,1)S(1)} %bitcast.62), channel_id=1, replica_groups=mesh['dp'=4,'expert'=64] {'expert'}, dimensions={0} | all-to-all | bytes 2097152 | tf_op jit(solution)/shard_map/all_to_all | solution.py:34
  547.7 0.0 all-gather.3.cloned.1.call-update
  547.8 0.6 copy.35
  548.4 45.4 %all-gather.3.cloned.1.call-done = bf16[256,8,1024]{2,1,0:T(8,128)(2,1)} async-done(((bf16[64,8,1024]{2,1,0:T(8,128)(2,1)}), bf16[256,8,1024]{2,1,0:T(8,128)(2,1)}) %all-gather.3.cloned.1.call-update) | async-done | bytes 4194320 | tf_op jit(solution)/shard_map/all_gather | solution.py:38
  593.8 13.0 %fusion.7 = bf16[1,1024,1792]{2,1,0:T(8,128)(2,1)} fusion(bf16[4,64,8,1024]{3,2,1,0:T(8,128)(2,1)} %bitcast.67, bf16[1,64,8,4,1792]{4,2,1,3,0:T(8,128)(2,1)} %copy.34), kind=kOutput, calls=%fused_computation.10 | convolution fusion | flops 7518027776 | bytes 15204352 | tf_op jit(solution)/shard_map/bscf,bscd->fd/dot_general | solution.py:44
  (9 shorter events, 0.1 us)
Async XLA Ops:
  7.2 437.3 %reduce-scatter.2.cloned.1.call-start = ((), (), s32[]{:S(2)}) async-start(), calls=%async_computation.5 | async-start | bytes 10485760 | tf_op jit(solution)/shard_map/reduce_scatter | solution.py:43
  366.2 89.0 %copy-start = (f32[128,2]{0,1:T(2,128)S(1)}, f32[128,2]{0,1:T(2,128)}, u32[]{:S(2)}) copy-start(f32[128,2]{0,1:T(2,128)} %param.7) | copy-start | bytes 3076
  444.5 61.9 %all-to-all-start.2 = ((f32[64,8,1024]{2,1,0:T(8,128)}), f32[64,8,1024]{2,1,0:T(8,128)S(1)}, u32[]{:S(2)}, u32[]{:S(2)}) async-start(f32[64,8,1024]{2,1,0:T(8,128)} %bitcast.63), calls=%async_computation.3 | async-start | bytes 4194304 | tf_op jit(solution)/shard_map/all_to_all | solution.py:47
  455.2 138.6 %all-gather.3.cloned.1.call-start = ((), (), s32[]{:S(2)}) async-start(), calls=%async_computation.6 | async-start | bytes 5242880 | tf_op jit(solution)/shard_map/all_gather | solution.py:38
Sparse Core Ops, SparseCore 0:
  366.4 78.0 reduce-scatter.1
  547.9 45.8 all-gather.2
where the time goes:
time: 615 us; the launch traced here: 614 us
  blocking collectives  301 us (49%)
  waiting for transfers between devices  175 us (28%)
  local copies, waits for them, and re-layouts  82.5 us (13%)
  matrix products  26.2 us (4%)
  between operations  14.2 us (2%)
  starting transfers between devices  10.8 us (2%)
    all_to_all x1, blocking collectives, per_device(): lax.all_to_all(send_cot, 'expert', split_axis=0, concat_axis=0, tiled=True)  176 us
    all_to_all x1, blocking collectives, per_device(): lax.all_to_all(got_cot[None], 'dp', split_axis=3, concat_axis=0, tiled=True)  90.1 us
    reduce_scatter x1, waiting for transfers between devices, per_device(): lax.psum_scatter(partial_back, 'dp', scatter_dimension=0, tiled=True)  78.2 us
    all_to_all x1, waiting for transfers between devices, per_device(): lax.all_to_all(summed[0], 'expert', split_axis=0, concat_axis=0, tiled=True)  51 us
    all_gather x1, waiting for transfers between devices, per_device(): rows_all = lax.all_gather(got_rows[None], 'dp', axis=0, tiled=True)  45.4 us
    all_to_all x1, blocking collectives, per_device(): lax.all_to_all(send_rows, 'expert', split_axis=0, concat_axis=0, tiled=True)  34.3 us
    unnamed x7, local copies, waits for them, and re-layouts  30.6 us
    broadcast_in_dim x1, local copies, waits for them, and re-layouts, per_device(): got_cot[None]  19.3 us
  transfers between devices with their start and end apart: 3, of which 3 were waited for; matrix products, arithmetic and copies ran while one was open for 0% of the time, Pallas kernels for 0%

commit v1 on v0

v1 whole, which is shorter than its diff:
```python
import jax
import jax.numpy as jnp
from jax import lax
from jax.sharding import PartitionSpec as P


def slots_for(flat_experts, columns, capacity):
    slot_count = flat_experts.shape[0]
    one_hot = (flat_experts[:, None] == jnp.arange(columns, dtype=jnp.int32)[None, :]).astype(
        jnp.int32
    )
    earlier = jnp.cumsum(one_hot, axis=0) - one_hot
    position = jnp.sum(earlier * one_hot, axis=1)
    destination = flat_experts * capacity + position
    slot_of = (
        jnp.full((columns * capacity,), slot_count, jnp.int32)
        .at[destination]
        .set(jnp.arange(slot_count, dtype=jnp.int32))
    )
    return destination, slot_of


def per_device(hidden, routes, gates, cotangent, weight):
    local_tokens, top_count, hidden_width = hidden.shape
    columns = lax.axis_size("expert")
    groups = lax.axis_size("dp")
    capacity = min(local_tokens, 2 * local_tokens * top_count // columns)
    slot_count = local_tokens * top_count
    quarter = cotangent.shape[1] // groups

    routes_all = lax.all_gather(routes.reshape(slot_count), "dp", axis=0, tiled=False)
    _, slot_of_all = jax.vmap(lambda r: slots_for(r, columns, capacity))(routes_all)
    destination, slot_of = slots_for(routes.reshape(slot_count), columns, capacity)

    cot_split = cotangent.reshape(local_tokens, groups, quarter).transpose(1, 0, 2)
    cot_q = lax.all_to_all(cot_split, "dp", split_axis=0, concat_axis=0, tiled=True)
    token_of = jnp.minimum(slot_of_all // top_count, local_tokens - 1)
    token_of = token_of.reshape(groups, columns, capacity).transpose(1, 0, 2)
    flat_token = token_of + (jnp.arange(groups, dtype=jnp.int32) * local_tokens)[None, :, None]
    send_cot = cot_q.reshape(groups * local_tokens, quarter)[flat_token]
    got_cot = lax.all_to_all(send_cot, "expert", split_axis=0, concat_axis=0, tiled=True)

    clamped = jnp.minimum(slot_of, slot_count - 1)
    send_hidden = hidden.reshape(slot_count, hidden_width)[clamped].reshape(
        columns, capacity, hidden_width
    )
    send_gates = jnp.where(slot_of < slot_count, gates.reshape(slot_count)[clamped], 0.0).reshape(
        columns, capacity
    )
    got_hidden = lax.all_to_all(send_hidden, "expert", split_axis=0, concat_axis=0, tiled=True)
    got_gates = lax.all_to_all(send_gates, "expert", split_axis=0, concat_axis=0, tiled=True)

    scaled = (got_gates[:, :, None] * got_hidden.astype(jnp.float32)).astype(jnp.bfloat16)
    rows_all = lax.all_gather(scaled, "dp", axis=0, tiled=False)
    matrix = weight[0]
    partial_back = jnp.stack(
        [
            jnp.einsum("scd,fd->scf", got_cot[:, g], matrix, preferred_element_type=jnp.float32)
            for g in range(groups)
        ]
    )
    back = lax.psum_scatter(partial_back, "dp", scatter_dimension=0, tiled=True)[0]
    grad_matrix = jnp.einsum(
        "gscf,sgcd->fd", rows_all, got_cot, preferred_element_type=jnp.float32
    )
    grad_hidden_rows = (got_gates[:, :, None] * back).astype(jnp.bfloat16)
    grad_gates_rows = jnp.sum(got_hidden.astype(jnp.float32) * back, axis=2)
    returned_hidden = lax.all_to_all(
        grad_hidden_rows, "expert", split_axis=0, concat_axis=0, tiled=True
    )
    returned_gates = lax.all_to_all(
        grad_gates_rows, "expert", split_axis=0, concat_axis=0, tiled=True
    )
    grad_hidden = returned_hidden.reshape(columns * capacity, hidden_width)[destination].reshape(
        local_tokens, top_count, hidden_width
    )
    grad_gates = returned_gates.reshape(columns * capacity)[destination].reshape(
        local_tokens, top_count
    )
    return (grad_hidden, grad_gates, grad_matrix.astype(jnp.bfloat16)[None])


def solution(mesh):
    placed = (
        P(("dp", "expert"), None, None),
        P(("dp", "expert"), None),
        P(("dp", "expert"), None),
        P(("dp", "expert"), None),
        P("expert", None, "dp"),
    )
    return jax.shard_map(
        per_device,
        mesh=mesh,
        in_specs=placed,
        out_specs=(
            P(("dp", "expert"), None, None),
            P(("dp", "expert"), None),
            P("expert", None, "dp"),
        ),
        check_vma=False,
    )
```

time: 615 us -> 405 us (0.66)
  waiting for transfers between devices: 175 us -> 54 us
  local copies, waits for them, and re-layouts: 82.5 us -> 33.1 us
  blocking collectives: 301 us -> 254 us
  other arithmetic: 4.51 us -> 11.6 us
    all_to_all x2, blocking collectives: 124 us -> 52.3 us  [the longest x1 32.5 us: per_device(): lax.all_to_all(send_hidden, 'expert', split_axis=0, concat_axis=0, tiled=...]
    reduce_scatter x1, waiting for transfers between devices: 78.2 us -> 22.8 us  [per_device(): lax.psum_scatter(partial_back, 'dp', scatter_dimension=0, tiled=True)[0]]
    all_gather x1, waiting for transfers between devices: 45.4 us -> 0.01 us  [per_device(): rows_all = lax.all_gather(scaled, 'dp', axis=0, tiled=False)]
    unnamed x7 -> x24, local copies, waits for them, and re-layouts: 30.6 us -> 5.36 us
    all_gather x0 -> x1, blocking collectives: none -> 23.3 us  [per_device(): lax.all_gather(routes.reshape(slot_count), 'dp', axis=0, tiled=False)]
    all_to_all x1 -> x3, waiting for transfers between devices: 51 us -> 31.2 us  [the longest x1 24.5 us: per_device(): lax.all_to_all(grad_hidden_rows, 'expert', split_axis=0, concat_axis=0, t...]
    broadcast_in_dim x1, local copies, waits for them, and re-layouts: 19.3 us -> 0.15 us  [per_device(): send_cot = cot_q.reshape(groups * local_tokens, quarter)[flat_token]]
    all_to_all x1 -> x2, local copies, waits for them, and re-layouts: 17.7 us -> 1.22 us  [the longest x1 0.7 us: per_device(): lax.all_to_all(send_gates, 'expert', split_axis=0, concat_axis=0, tiled=T...]
  transfers between devices with their start and end apart: 3 -> 5, of which waited for: 3 -> 3; matrix products, arithmetic and copies ran while one was open for 0% -> 6% of each run, Pallas kernels for 0% -> 0%
where the time goes in v1:
time: 405 us
  blocking collectives  254 us (63%)
  waiting for transfers between devices  54 us (13%)
  local copies, waits for them, and re-layouts  33.1 us (8%)
  matrix products  21.5 us (5%)
  starting transfers between devices  16.4 us (4%)
  between operations  14.4 us (4%)
  other arithmetic  11.6 us (3%)
    all_to_all x1, blocking collectives, per_device(): lax.all_to_all(send_cot, 'expert', split_axis=0, concat_axis=0, tiled=True)  178 us
    all_to_all x1, blocking collectives, per_device(): lax.all_to_all(send_hidden, 'expert', split_axis=0, concat_axis=0, tiled=...  32.5 us
    all_to_all x1, waiting for transfers between devices, per_device(): lax.all_to_all(grad_hidden_rows, 'expert', split_axis=0, concat_axis=0, t...  24.5 us
    all_gather x1, blocking collectives, per_device(): lax.all_gather(routes.reshape(slot_count), 'dp', axis=0, tiled=False)  23.3 us
    reduce_scatter x1, waiting for transfers between devices, per_device(): lax.psum_scatter(partial_back, 'dp', scatter_dimension=0, tiled=True)[0]  22.8 us
    all_to_all x1, blocking collectives, per_device(): lax.all_to_all(grad_gates_rows, 'expert', split_axis=0, concat_axis=0, ti...  19.8 us
    dot_general x1, matrix products, per_device(): jnp.einsum('gscf,sgcd->fd', rows_all, got_cot, preferred_element_type=jnp...  13.1 us
    gather x1, local copies, waits for them, and re-layouts, per_device(): send_cot = cot_q.reshape(groups * local_tokens, quarter)[flat_token]  10.7 us
  transfers between devices with their start and end apart: 5, of which 3 were waited for; matrix products, arithmetic and copies ran while one was open for 6% of the time, Pallas kernels for 0%

profile of v1, /device:TPU:1, one launch (start us, length us, event | category | flops | bytes accessed | tf_op | source)
XLA Modules:
  0.0 404.6 jit_solution(626316124953999824)
XLA Ops:
  7.2 0.0 copy-start.2
  7.2 2.9 copy.71
  10.0 5.1 %all-to-all-start.1 = ((bf16[4,128,1792]{2,1,0:T(8,128)(2,1)}), bf16[4,128,1792]{2,1,0:T(8,128)(2,1)S(1)}, u32[]{:S(2)}, u32[]{:S(2)}) async-start(bf16[4,128,1792]{2,1,0:T(8,128)(2,1)} %bitcast.137), calls=%async_computation.1 | async-start | bytes 3670016 | tf_op jit(solution)/shard_map/all_to_all | solution.py:36
  15.2 0.0 reduce-scatter.2.cloned.1.call-start
  15.2 0.0 copy-done.2
  15.2 0.1 copy.27
  15.3 0.1 reshape.181
  15.4 23.3 %all-gather.1 = s32[4,1,256]{2,1,0:T(1,128)S(1)} all-gather(s32[1,1,256]{2,1,0:T(1,128)S(1)} %reshape.181), channel_id=1, replica_groups=mesh['dp'=4,'expert'=64] {'dp'}, dimensions={0}, use_global_device_ids=true | all-gather | bytes 5120 | tf_op jit(solution)/shard_map/all_gather | solution.py:31
  38.7 2.4 reduce-window.16
  41.1 0.1 slice.43
  41.3 0.1 copy.34
  41.4 0.2 fusion.26
  41.6 0.0 copy-done.5
  41.6 0.1 multiply_reduce_fusion
  41.7 0.0 copy-done.4
  41.7 0.1 and_reduce_fusion
  41.8 4.3 %scatter_custom_fusion.1 = s32[2048]{0:T(1024)S(1)} fusion(s32[1024]{0:T(1024)S(1)} %bitcast.147, s32[1024]{0:T(1024)S(1)} %bitcast.148, s32[]{:T(128)} %constant.14.clone.1), kind=kCustom, calls=%fused_computation.72 | custom fusion | bytes 8196
  46.2 0.1 reshape.111
  46.3 0.1 compare_select_fusion
  46.4 0.1 copy.37
  46.5 0.2 reshape.132
  46.6 0.0 all-to-all-done.1
  46.7 10.7 %gather_fusion.1 = bf16[2048,1792]{1,0:T(8,128)(2,1)} fusion(bf16[512,1792]{1,0:T(8,128)(2,1)S(1)} %bitcast.134, s32[2048]{0:T(1024)S(1)} %broadcast_clamp_fusion), kind=kCustom, calls=%fused_computation.1 | custom fusion | bytes 14688256 | tf_op jit(solution)/shard_map/gather | solution.py:40
  57.3 178.2 %all_to_all.38 = bf16[64,4,8,1792]{3,2,1,0:T(8,128)(2,1)S(1)} all-to-all(bf16[64,4,8,1792]{3,2,1,0:T(8,128)(2,1)} %bitcast.135), channel_id=1, replica_groups=mesh['dp'=4,'expert'=64] {'expert'}, dimensions={0} | all-to-all | bytes 14680064 | tf_op jit(solution)/shard_map/all_to_all | solution.py:41
  235.5 2.1 fusion.12
  237.6 2.1 fusion.15
  239.7 2.1 fusion.18
  241.8 0.0 copy-done
  241.8 2.1 fusion.21
  243.9 3.8 pad_maximum_fusion
  247.7 0.0 reduce-scatter.2.cloned.1.call-update
  247.7 0.1 eq.52
  247.9 0.1 eq.48
  248.0 0.6 reduce-window.14
  248.7 0.2 slice_reduce_fusion
  248.9 0.1 copy.26
  249.0 0.1 mul.56
  249.2 0.1 copy.30
  249.3 0.1 reshape.107
  249.4 0.1 fusion.30
  249.5 1.4 scatter_custom_fusion
  251.0 3.5 gather_fusion
  254.5 0.7 all_to_all.24
  255.2 6.2 %all-to-all-start = ((f32[64,1,8]{2,1,0:T(1,128)}), f32[64,1,8]{2,1,0:T(1,128)S(1)}, u32[]{:S(2)}, u32[]{:S(2)}) async-start(f32[64,1,8]{2,1,0:T(1,128)} %bitcast.3), calls=%async_computation | async-start | bytes 65536 | tf_op jit(solution)/shard_map/all_to_all | solution.py:51
  261.4 0.3 all-gather.4.cloned.1.call-start
  261.7 0.2 reshape.114
  261.9 2.1 gather_fusion.3
  264.0 6.7 %all-to-all-done = f32[64,1,8]{2,1,0:T(1,128)S(1)} async-done(((f32[64,1,8]{2,1,0:T(1,128)}), f32[64,1,8]{2,1,0:T(1,128)S(1)}, u32[]{:S(2)}, u32[]{:S(2)}) %all-to-all-start) | async-done | bytes 2080 | tf_op jit(solution)/shard_map/all_to_all | solution.py:51
  270.6 32.5 %all_to_all.39 = bf16[64,8,1024]{2,1,0:T(8,128)(2,1)S(1)} all-to-all(bf16[64,8,1024]{2,1,0:T(8,128)(2,1)S(1)} %bitcast.138), channel_id=1, replica_groups=mesh['dp'=4,'expert'=64] {'expert'}, dimensions={0} | all-to-all | bytes 2097152 | tf_op jit(solution)/shard_map/all_to_all | solution.py:50
  303.1 22.8 %reduce-scatter.2.cloned.1.call-done = f32[1,64,8,1024]{3,2,1,0:T(8,128)} async-done(((f32[4,64,8,1024]{3,2,1,0:T(8,128)}), f32[1,64,8,1024]{3,2,1,0:T(8,128)}) %reduce-scatter.2.cloned.1.call-update) | async-done | bytes 2097168 | tf_op jit(solution)/shard_map/reduce_scatter | solution.py:62
  326.0 3.4 fusion.9
  329.3 0.0 all-gather.4.cloned.1.call-update
  329.3 19.8 %all_to_all.40 = f32[64,1,8]{2,1,0:T(1,128)S(1)} all-to-all(f32[64,1,8]{2,1,0:T(1,128)S(1)} %bitcast.141), channel_id=1, replica_groups=mesh['dp'=4,'expert'=64] {'expert'}, dimensions={0} | all-to-all | bytes 4096 | tf_op jit(solution)/shard_map/all_to_all | solution.py:71
  349.2 4.8 %all-to-all-start.3 = ((bf16[64,8,1024]{2,1,0:T(8,128)(2,1)}), bf16[64,8,1024]{2,1,0:T(8,128)(2,1)S(1)}, u32[]{:S(2)}, u32[]{:S(2)}) async-start(bf16[64,8,1024]{2,1,0:T(8,128)(2,1)} %get-tuple-element.10), calls=%async_computation.4 | async-start | bytes 2097152 | tf_op jit(solution)/shard_map/all_to_all | solution.py:68
  353.9 0.5 broadcast.133
  354.4 0.7 reduce.9
  355.2 0.1 reshape.116
  355.3 1.9 gather_fusion.4
  357.2 0.1 reshape.117
  357.4 0.6 copy.43
  358.0 24.5 %all-to-all-done.3 = bf16[64,8,1024]{2,1,0:T(8,128)(2,1)S(1)} async-done(((bf16[64,8,1024]{2,1,0:T(8,128)(2,1)}), bf16[64,8,1024]{2,1,0:T(8,128)(2,1)S(1)}, u32[]{:S(2)}, u32[]{:S(2)}) %all-to-all-start.3) | async-done | bytes 1048608 | tf_op jit(solution)/shard_map/all_to_all | solution.py:68
  382.5 1.2 gather_fusion.2
  383.6 1.0 reshape.113
  384.6 13.1 %fusion.8 = bf16[1,1024,1792]{2,1,0:T(8,128)(2,1)} fusion(bf16[4,64,8,1024]{3,2,1,0:T(8,128)(2,1)} %bitcast.149, bf16[64,4,8,1792]{3,2,1,0:T(8,128)(2,1)} %copy-done), kind=kOutput, calls=%fused_computation.17 | convolution fusion | flops 7518027776 | bytes 15204352 | tf_op jit(solution)/shard_map/gscf,sgcd->fd/dot_general | solution.py:63
  (35 shorter events, 0.2 us)
Async XLA Ops:
  7.2 8.0 %copy-start.2 = (s32[128,2]{0,1:T(2,128)S(1)}, s32[128,2]{0,1:T(2,128)}, u32[]{:S(2)}) copy-start(s32[128,2]{0,1:T(2,128)} %param.6) | copy-start | bytes 3076
  10.0 31.6 %copy-start.5 = (s32[2]{0:T(128)S(1)}, s32[2]{0:T(128)}, u32[]{:S(2)}) copy-start(s32[2]{0:T(128)} %constant.50) | copy-start | bytes 28
  10.0 31.7 %copy-start.4 = (s32[2]{0:T(128)S(1)}, s32[2]{0:T(128)}, u32[]{:S(2)}) copy-start(s32[2]{0:T(128)} %constant.53) | copy-start | bytes 28
  10.0 36.6 %all-to-all-start.1 = ((bf16[4,128,1792]{2,1,0:T(8,128)(2,1)}), bf16[4,128,1792]{2,1,0:T(8,128)(2,1)S(1)}, u32[]{:S(2)}, u32[]{:S(2)}) async-start(bf16[4,128,1792]{2,1,0:T(8,128)(2,1)} %bitcast.137), calls=%async_computation.1 | async-start | bytes 3670016 | tf_op jit(solution)/shard_map/all_to_all | solution.py:36
  15.2 310.8 %reduce-scatter.2.cloned.1.call-start = ((), (), s32[]{:S(2)}) async-start(), calls=%async_computation.7 | async-start | bytes 10485760 | tf_op jit(solution)/shard_map/reduce_scatter | solution.py:62
  57.3 178.2 %copy-start.6 = (bf16[1,1024,1792]{2,1,0:T(8,128)(2,1)S(1)}, bf16[1,1024,1792]{2,1,0:T(8,128)(2,1)}, u32[]{:S(2)}) copy-start(bf16[1,1024,1792]{2,1,0:T(8,128)(2,1)} %param.9) | copy-start | bytes 11010052
  235.5 6.3 %copy-start = (bf16[64,4,8,1792]{3,2,1,0:T(8,128)(2,1)}, bf16[64,4,8,1792]{3,2,1,0:T(8,128)(2,1)S(1)}, u32[]{:S(2)}) copy-start(bf16[64,4,8,1792]{3,2,1,0:T(8,128)(2,1)S(1)} %all_to_all.38) | copy-start | bytes 22020100
  247.7 1.4 copy-start.3
  247.7 14.0 %copy-start.1 = (bf16[128,2,1024]{2,1,0:T(2,128)(2,1)S(1)}, bf16[128,2,1024]{2,1,0:T(2,128)(2,1)}, u32[]{:S(2)}) copy-start(bf16[128,2,1024]{2,1,0:T(2,128)(2,1)} %param.5) | copy-start | bytes 1572868
  255.2 15.4 %all-to-all-start = ((f32[64,1,8]{2,1,0:T(1,128)}), f32[64,1,8]{2,1,0:T(1,128)S(1)}, u32[]{:S(2)}, u32[]{:S(2)}) async-start(f32[64,1,8]{2,1,0:T(1,128)} %bitcast.3), calls=%async_computation | async-start | bytes 65536 | tf_op jit(solution)/shard_map/all_to_all | solution.py:51
  261.4 123.2 %all-gather.4.cloned.1.call-start = ((), (), s32[]{:S(2)}) async-start(), calls=%async_computation.8 | async-start | bytes 5242880 | tf_op jit(solution)/shard_map/all_gather | solution.py:54
  349.2 33.3 %all-to-all-start.3 = ((bf16[64,8,1024]{2,1,0:T(8,128)(2,1)}), bf16[64,8,1024]{2,1,0:T(8,128)(2,1)S(1)}, u32[]{:S(2)}, u32[]{:S(2)}) async-start(bf16[64,8,1024]{2,1,0:T(8,128)(2,1)} %get-tuple-element.10), calls=%async_computation.4 | async-start | bytes 2097152 | tf_op jit(solution)/shard_map/all_to_all | solution.py:68
Sparse Core Ops, SparseCore 0:
  247.9 78.0 reduce-scatter.1
  329.5 50.3 all-gather.3

commit v2 on v1

--- a/solution.py
+++ b/solution.py
@@ -20,6 +20,25 @@
     return destination, slot_of
 
 
+LANES = 128
+
+
+def split3(values):
+    pieces = []
+    rest = values
+    for _ in range(3):
+        head = lax.reduce_precision(rest, exponent_bits=8, mantissa_bits=7)
+        pieces.append(head.astype(jnp.bfloat16))
+        rest = rest - head
+    pad = jnp.zeros(values.shape + (LANES - 3,), jnp.bfloat16)
+    return jnp.concatenate([jnp.stack(pieces, axis=-1), pad], axis=-1)
+
+
+def join3(lanes):
+    pieces = lanes[..., :3].astype(jnp.float32)
+    return (pieces[..., 0] + pieces[..., 1]) + pieces[..., 2]
+
+
 def per_device(hidden, routes, gates, cotangent, weight):
     local_tokens, top_count, hidden_width = hidden.shape
     columns = lax.axis_size("expert")
@@ -28,12 +47,24 @@
     slot_count = local_tokens * top_count
     quarter = cotangent.shape[1] // groups
 
-    routes_all = lax.all_gather(routes.reshape(slot_count), "dp", axis=0, tiled=False)
-    _, slot_of_all = jax.vmap(lambda r: slots_for(r, columns, capacity))(routes_all)
     destination, slot_of = slots_for(routes.reshape(slot_count), columns, capacity)
 
-    cot_split = cotangent.reshape(local_tokens, groups, quarter).transpose(1, 0, 2)
-    cot_q = lax.all_to_all(cot_split, "dp", split_axis=0, concat_axis=0, tiled=True)
+    route_lanes = jnp.zeros((local_tokens, LANES), jnp.bfloat16).at[:, :top_count].set(
+        routes.astype(jnp.bfloat16)
+    )
+    cot_split = jnp.concatenate(
+        [
+            cotangent.reshape(local_tokens, groups, quarter).transpose(1, 0, 2),
+            jnp.broadcast_to(route_lanes[None], (groups, local_tokens, LANES)),
+        ],
+        axis=2,
+    )
+    received = lax.all_to_all(cot_split, "dp", split_axis=0, concat_axis=0, tiled=True)
+    cot_q = received[:, :, :quarter]
+    routes_all = received[:, :, quarter : quarter + top_count].astype(jnp.int32)
+    _, slot_of_all = jax.vmap(lambda r: slots_for(r, columns, capacity))(
+        routes_all.reshape(groups, slot_count)
+    )
     token_of = jnp.minimum(slot_of_all // top_count, local_tokens - 1)
     token_of = token_of.reshape(groups, columns, capacity).transpose(1, 0, 2)
     flat_token = token_of + (jnp.arange(groups, dtype=jnp.int32) * local_tokens)[None, :, None]
@@ -47,8 +78,15 @@
     send_gates = jnp.where(slot_of < slot_count, gates.reshape(slot_count)[clamped], 0.0).reshape(
         columns, capacity
     )
-    got_hidden = lax.all_to_all(send_hidden, "expert", split_axis=0, concat_axis=0, tiled=True)
-    got_gates = lax.all_to_all(send_gates, "expert", split_axis=0, concat_axis=0, tiled=True)
+    got = lax.all_to_all(
+        jnp.concatenate([send_hidden, split3(send_gates)], axis=2),
+        "expert",
+        split_axis=0,
+        concat_axis=0,
+        tiled=True,
+    )
+    got_hidden = got[:, :, :hidden_width]
+    got_gates = join3(got[:, :, hidden_width:])
 
     scaled = (got_gates[:, :, None] * got_hidden.astype(jnp.float32)).astype(jnp.bfloat16)
     rows_all = lax.all_gather(scaled, "dp", axis=0, tiled=False)
@@ -65,12 +103,15 @@
     )
     grad_hidden_rows = (got_gates[:, :, None] * back).astype(jnp.bfloat16)
     grad_gates_rows = jnp.sum(got_hidden.astype(jnp.float32) * back, axis=2)
-    returned_hidden = lax.all_to_all(
-        grad_hidden_rows, "expert", split_axis=0, concat_axis=0, tiled=True
+    returned = lax.all_to_all(
+        jnp.concatenate([grad_hidden_rows, split3(grad_gates_rows)], axis=2),
+        "expert",
+        split_axis=0,
+        concat_axis=0,
+        tiled=True,
     )
-    returned_gates = lax.all_to_all(
-        grad_gates_rows, "expert", split_axis=0, concat_axis=0, tiled=True
-    )
+    returned_hidden = returned[:, :, :hidden_width]
+    returned_gates = join3(returned[:, :, hidden_width:])
     grad_hidden = returned_hidden.reshape(columns * capacity, hidden_width)[destination].reshape(
         local_tokens, top_count, hidden_width
     )

time: 405 us -> 409 us (level)
  blocking collectives: 254 us -> 215 us
  waiting for transfers between devices: 54 us -> 82 us
  local copies, waits for them, and re-layouts: 33.1 us -> 44.4 us
    all_gather x1 -> x0, blocking collectives: 23.3 us -> none  [per_device(): lax.all_gather(routes.reshape(slot_count), 'dp', axis=0, tiled=False)]
    all_to_all x1, waiting for transfers between devices: 0.01 us -> 23.2 us  [per_device(): lax.all_to_all(cot_split, 'dp', split_axis=0, concat_axis=0, tiled=True)]
    all_to_all x2 -> x1, blocking collectives: 52.3 us -> 37.6 us  [per_device(): lax.all_to_all(jnp.concatenate([send_hidden, split3(send_gates)], axis=2)...]
    reduce_scatter x1, waiting for transfers between devices: 22.8 us -> 27.1 us  [per_device(): lax.psum_scatter(partial_back, 'dp', scatter_dimension=0, tiled=True)[0]]
    unnamed x24 -> x34, local copies, waits for them, and re-layouts: 5.36 us -> 9.18 us
    all_to_all x2 -> x1, starting transfers between devices: 11 us -> 10.8 us  [per_device(): lax.all_to_all(jnp.concatenate([grad_hidden_rows, split3(grad_gates_rows)...]
    all_to_all x2 -> x1, waiting for transfers between devices: 31.2 us -> 31.3 us  [per_device(): lax.all_to_all(jnp.concatenate([grad_hidden_rows, split3(grad_gates_rows)...]
  transfers between devices with their start and end apart: 5 -> 4, of which waited for: 3 -> 4; matrix products, arithmetic and copies ran while one was open for 6% -> 5% of each run, Pallas kernels for 0% -> 0%
where the time goes in v2:
time: 409 us
  blocking collectives  215 us (53%)
  waiting for transfers between devices  82 us (20%)
  local copies, waits for them, and re-layouts  44.4 us (11%)
  matrix products  21.5 us (5%)
  starting transfers between devices  15.9 us (4%)
  other arithmetic  15.4 us (4%)
  between operations  14.5 us (4%)
    all_to_all x1, blocking collectives, per_device(): lax.all_to_all(send_cot, 'expert', split_axis=0, concat_axis=0, tiled=True)  178 us
    all_to_all x1, blocking collectives, per_device(): lax.all_to_all(jnp.concatenate([send_hidden, split3(send_gates)], axis=2)...  37.6 us
    all_to_all x1, waiting for transfers between devices, per_device(): lax.all_to_all(jnp.concatenate([grad_hidden_rows, split3(grad_gates_rows)...  31.3 us
    reduce_scatter x1, waiting for transfers between devices, per_device(): lax.psum_scatter(partial_back, 'dp', scatter_dimension=0, tiled=True)[0]  27.1 us
    all_to_all x1, waiting for transfers between devices, per_device(): lax.all_to_all(cot_split, 'dp', split_axis=0, concat_axis=0, tiled=True)  23.2 us
    dot_general x1, matrix products, per_device(): jnp.einsum('gscf,sgcd->fd', rows_all, got_cot, preferred_element_type=jnp...  13.1 us
    all_to_all x1, starting transfers between devices, per_device(): lax.all_to_all(jnp.concatenate([grad_hidden_rows, split3(grad_gates_rows)...  10.8 us
    gather x1, local copies, waits for them, and re-layouts, per_device(): send_cot = cot_q.reshape(groups * local_tokens, quarter)[flat_token]  10.7 us
  transfers between devices with their start and end apart: 4, of which 4 were waited for; matrix products, arithmetic and copies ran while one was open for 5% of the time, Pallas kernels for 0%

profile of v2, /device:TPU:1, one launch (start us, length us, event | category | flops | bytes accessed | tf_op | source)
XLA Modules:
  0.0 409.0 jit_solution(18094672019178588190)
XLA Ops:
  7.2 0.6 compare_reduce_fusion
  7.8 3.3 copy.113
  11.1 2.5 copy.115
  13.6 0.6 broadcast_select_fusion.1
  14.3 0.1 copy.145
  14.4 3.0 pad_maximum_fusion.1
  17.4 5.1 %all-to-all-start.1 = ((bf16[4,128,1920]{2,1,0:T(8,128)(2,1)}), bf16[4,128,1920]{2,1,0:T(8,128)(2,1)S(1)}, u32[]{:S(2)}, u32[]{:S(2)}) async-start(bf16[4,128,1920]{2,1,0:T(8,128)(2,1)} %pad_maximum_fusion.1), calls=%async_computation.1 | async-start | bytes 3932160 | tf_op jit(solution)/shard_map/all_to_all | solution.py:62
  22.6 23.2 %all-to-all-done.1 = bf16[4,128,1920]{2,1,0:T(8,128)(2,1)S(1)} async-done(((bf16[4,128,1920]{2,1,0:T(8,128)(2,1)}), bf16[4,128,1920]{2,1,0:T(8,128)(2,1)S(1)}, u32[]{:S(2)}, u32[]{:S(2)}) %all-to-all-start.1) | async-done | bytes 1966112 | tf_op jit(solution)/shard_map/all_to_all | solution.py:62
  45.8 0.1 copy.144
  46.0 0.2 copy.118
  46.3 2.4 reduce-window.16
  48.7 0.1 slice.117
  48.8 0.1 copy.122
  49.0 0.2 copy.117
  49.3 0.2 fusion.26
  49.6 0.1 copy.143
  49.8 0.2 copy.142
  50.1 4.3 %scatter_custom_fusion.1 = s32[2048]{0:T(1024)S(1)} fusion(s32[1024]{0:T(1024)S(1)} %bitcast.148, s32[1024]{0:T(1024)S(1)} %bitcast.147, s32[]{:T(128)} %constant.65.clone.1), kind=kCustom, calls=%fused_computation.92 | custom fusion | bytes 8196
  54.8 0.2 reshape.284
  54.9 1.6 slice.115
  56.6 10.7 %gather_fusion.2 = bf16[2048,1792]{1,0:T(8,128)(2,1)} fusion(bf16[512,1792]{1,0:T(8,128)(2,1)S(1)} %bitcast.135, s32[2048]{0:T(1024)S(1)} %broadcast_clamp_fusion), kind=kCustom, calls=%fused_computation.2 | custom fusion | bytes 14688256 | tf_op jit(solution)/shard_map/gather | solution.py:71
  67.2 177.7 %all_to_all.20 = bf16[64,4,8,1792]{3,2,1,0:T(8,128)(2,1)S(1)} all-to-all(bf16[64,4,8,1792]{3,2,1,0:T(8,128)(2,1)} %bitcast.136), channel_id=1, replica_groups=mesh['dp'=4,'expert'=64] {'expert'}, dimensions={0} | all-to-all | bytes 14680064 | tf_op jit(solution)/shard_map/all_to_all | solution.py:72
  244.9 2.1 fusion.12
  247.0 2.1 fusion.15
  249.1 2.1 fusion.18
  251.2 2.1 fusion.21
  253.3 3.8 pad_maximum_fusion
  257.2 0.1 copy.102
  257.4 0.1 eq.54
  257.5 0.1 eq.50
  257.7 0.6 reduce-window.14
  258.3 0.2 slice_reduce_fusion
  258.5 0.1 copy.101
  258.6 0.1 mul.66
  258.8 0.1 copy.105
  258.9 0.1 reshape.253
  259.2 1.4 scatter_custom_fusion
  260.6 3.5 gather_fusion.1
  264.3 0.2 copy.108
  264.5 0.8 copy.109
  265.3 0.8 copy.110
  266.1 0.2 reshape.250
  266.3 2.1 gather_fusion
  268.4 1.6 concatenate.11
  270.1 37.6 %all_to_all.21 = bf16[64,8,1152]{2,1,0:T(8,128)(2,1)S(1)} all-to-all(bf16[64,8,1152]{2,1,0:T(8,128)(2,1)S(1)} %concatenate.11), channel_id=1, replica_groups=mesh['dp'=4,'expert'=64] {'expert'}, dimensions={0} | all-to-all | bytes 2359296 | tf_op jit(solution)/shard_map/all_to_all | solution.py:81
  307.6 0.2 slice_add_fusion.2
  307.8 0.4 copy.141
  308.3 27.1 %reduce-scatter.2.cloned.1.call-done = f32[1,64,8,1024]{3,2,1,0:T(8,128)} async-done(((f32[4,64,8,1024]{3,2,1,0:T(8,128)}), f32[1,64,8,1024]{3,2,1,0:T(8,128)}) %reduce-scatter.2.cloned.1.call-update) | async-done | bytes 2097168 | tf_op jit(solution)/shard_map/reduce_scatter | solution.py:100
  335.4 3.0 fusion.9
  338.5 0.2 copy.135
  338.7 0.2 copy.136
  338.9 0.2 copy.137
  339.0 2.1 concatenate.13
  341.1 10.8 %all-to-all-start.3 = ((bf16[64,8,1152]{2,1,0:T(8,128)(2,1)}), bf16[64,8,1152]{2,1,0:T(8,128)(2,1)S(1)}, u32[]{:S(2)}, u32[]{:S(2)}) async-start(bf16[64,8,1152]{2,1,0:T(8,128)(2,1)} %concatenate.13), calls=%async_computation.4 | async-start | bytes 2359296 | tf_op jit(solution)/shard_map/all_to_all | solution.py:106
  351.9 31.3 %all-to-all-done.3 = bf16[64,8,1152]{2,1,0:T(8,128)(2,1)S(1)} async-done(((bf16[64,8,1152]{2,1,0:T(8,128)(2,1)}), bf16[64,8,1152]{2,1,0:T(8,128)(2,1)S(1)}, u32[]{:S(2)}, u32[]{:S(2)}) %all-to-all-start.3) | async-done | bytes 1179680 | tf_op jit(solution)/shard_map/all_to_all | solution.py:106
  383.2 0.1 slice_bitcast_fusion.16
  383.3 1.2 gather_fusion.3
  384.5 1.0 reshape.260
  385.5 0.3 fusion.27
  385.9 1.9 gather_fusion.4
  387.9 0.1 reshape.261
  388.0 0.6 copy.139
  388.7 0.3 all-gather.3.cloned.1.call-done
  389.0 13.1 %fusion.8 = bf16[1,1024,1792]{2,1,0:T(8,128)(2,1)} fusion(bf16[4,64,8,1024]{3,2,1,0:T(8,128)(2,1)} %bitcast.149, bf16[64,4,8,1792]{3,2,1,0:T(8,128)(2,1)} %copy-done.1), kind=kOutput, calls=%fused_computation.17 | convolution fusion | flops 7518027776 | bytes 15204352 | tf_op jit(solution)/shard_map/gscf,sgcd->fd/dot_general | solution.py:101
  (72 shorter events, 1.6 us)
Async XLA Ops:
  7.8 5.8 %copy-start.5 = (s32[128,2]{0,1:T(2,128)S(1)}, s32[128,2]{0,1:T(2,128)}, u32[]{:S(2)}) copy-start(s32[128,2]{0,1:T(2,128)} %param.8) | copy-start | bytes 3076
  17.4 32.1 %copy-start.8 = (s32[2]{0:T(128)S(1)}, s32[2]{0:T(128)}, u32[]{:S(2)}) copy-start(s32[2]{0:T(128)} %constant.85) | copy-start | bytes 28
  17.4 32.3 %copy-start.7 = (s32[2]{0:T(128)S(1)}, s32[2]{0:T(128)}, u32[]{:S(2)}) copy-start(s32[2]{0:T(128)} %constant.88) | copy-start | bytes 28
  17.4 28.4 %all-to-all-start.1 = ((bf16[4,128,1920]{2,1,0:T(8,128)(2,1)}), bf16[4,128,1920]{2,1,0:T(8,128)(2,1)S(1)}, u32[]{:S(2)}, u32[]{:S(2)}) async-start(bf16[4,128,1920]{2,1,0:T(8,128)(2,1)} %pad_maximum_fusion.1), calls=%async_computation.1 | async-start | bytes 3932160 | tf_op jit(solution)/shard_map/all_to_all | solution.py:62
  22.6 312.8 %reduce-scatter.2.cloned.1.call-start = ((), (), s32[]{:S(2)}) async-start(), calls=%async_computation.5 | async-start | bytes 10485760 | tf_op jit(solution)/shard_map/reduce_scatter | solution.py:100
  45.8 9.1 %copy-start = (bf16[4,128,1920]{2,1,0:T(8,128)(2,1)}, bf16[4,128,1920]{2,1,0:T(8,128)(2,1)S(1)}, u32[]{:S(2)}) copy-start(bf16[4,128,1920]{2,1,0:T(8,128)(2,1)S(1)} %all-to-all-done.1) | copy-start | bytes 5898244
  67.2 177.7 %copy-start.9 = (bf16[1,1024,1792]{2,1,0:T(8,128)(2,1)S(1)}, bf16[1,1024,1792]{2,1,0:T(8,128)(2,1)}, u32[]{:S(2)}) copy-start(bf16[1,1024,1792]{2,1,0:T(8,128)(2,1)} %param.11) | copy-start | bytes 11010052
  244.9 6.3 %copy-start.1 = (bf16[64,4,8,1792]{3,2,1,0:T(8,128)(2,1)}, bf16[64,4,8,1792]{3,2,1,0:T(8,128)(2,1)S(1)}, u32[]{:S(2)}) copy-start(bf16[64,4,8,1792]{3,2,1,0:T(8,128)(2,1)S(1)} %all_to_all.20) | copy-start | bytes 22020100
  257.2 1.6 copy-start.6
  257.2 8.9 %copy-start.2 = (bf16[128,2,1024]{2,1,0:T(2,128)(2,1)S(1)}, bf16[128,2,1024]{2,1,0:T(2,128)(2,1)}, u32[]{:S(2)}) copy-start(bf16[128,2,1024]{2,1,0:T(2,128)(2,1)} %param.7) | copy-start | bytes 1572868
  257.2 131.8 %all-gather.3.cloned.1.call-start = ((), (), s32[]{:S(2)}) async-start(), calls=%async_computation.6 | async-start | bytes 5242880 | tf_op jit(solution)/shard_map/all_gather | solution.py:92
  266.3 2.1 copy-start.3
  266.3 2.1 copy-start.4
  341.1 42.1 %all-to-all-start.3 = ((bf16[64,8,1152]{2,1,0:T(8,128)(2,1)}), bf16[64,8,1152]{2,1,0:T(8,128)(2,1)S(1)}, u32[]{:S(2)}, u32[]{:S(2)}) async-start(bf16[64,8,1152]{2,1,0:T(8,128)(2,1)} %concatenate.13), calls=%async_computation.4 | async-start | bytes 2359296 | tf_op jit(solution)/shard_map/all_to_all | solution.py:106
Sparse Core Ops, SparseCore 0:
  257.3 78.0 reduce-scatter.1
  338.5 50.4 all-gather.2

commit v3 on v2

--- a/solution.py
+++ b/solution.py
@@ -21,6 +21,7 @@
 
 
 LANES = 128
+CHUNKS = 2
 
 
 def split3(values):
@@ -60,17 +61,6 @@
         axis=2,
     )
     received = lax.all_to_all(cot_split, "dp", split_axis=0, concat_axis=0, tiled=True)
-    cot_q = received[:, :, :quarter]
-    routes_all = received[:, :, quarter : quarter + top_count].astype(jnp.int32)
-    _, slot_of_all = jax.vmap(lambda r: slots_for(r, columns, capacity))(
-        routes_all.reshape(groups, slot_count)
-    )
-    token_of = jnp.minimum(slot_of_all // top_count, local_tokens - 1)
-    token_of = token_of.reshape(groups, columns, capacity).transpose(1, 0, 2)
-    flat_token = token_of + (jnp.arange(groups, dtype=jnp.int32) * local_tokens)[None, :, None]
-    send_cot = cot_q.reshape(groups * local_tokens, quarter)[flat_token]
-    got_cot = lax.all_to_all(send_cot, "expert", split_axis=0, concat_axis=0, tiled=True)
-
     clamped = jnp.minimum(slot_of, slot_count - 1)
     send_hidden = hidden.reshape(slot_count, hidden_width)[clamped].reshape(
         columns, capacity, hidden_width
@@ -85,22 +75,55 @@
         concat_axis=0,
         tiled=True,
     )
+    got, received = lax.optimization_barrier((got, received))
     got_hidden = got[:, :, :hidden_width]
     got_gates = join3(got[:, :, hidden_width:])
-
     scaled = (got_gates[:, :, None] * got_hidden.astype(jnp.float32)).astype(jnp.bfloat16)
     rows_all = lax.all_gather(scaled, "dp", axis=0, tiled=False)
+
+    cot_q = received[:, :, :quarter]
+    routes_all = received[:, :, quarter : quarter + top_count].astype(jnp.int32)
+    _, slot_of_all = jax.vmap(lambda r: slots_for(r, columns, capacity))(
+        routes_all.reshape(groups, slot_count)
+    )
+    token_of = jnp.minimum(slot_of_all // top_count, local_tokens - 1)
+    token_of = token_of.reshape(groups, columns, capacity).transpose(1, 0, 2)
+    flat_token = token_of + (jnp.arange(groups, dtype=jnp.int32) * local_tokens)[None, :, None]
+    send_cot = cot_q.reshape(groups * local_tokens, quarter)[flat_token]
+
     matrix = weight[0]
-    partial_back = jnp.stack(
-        [
-            jnp.einsum("scd,fd->scf", got_cot[:, g], matrix, preferred_element_type=jnp.float32)
-            for g in range(groups)
-        ]
+    step = capacity // CHUNKS
+    backs, got_chunks = [], []
+    for c in range(CHUNKS):
+        got_cot = lax.all_to_all(
+            send_cot[:, :, c * step : (c + 1) * step],
+            "expert",
+            split_axis=0,
+            concat_axis=0,
+            tiled=True,
+        )
+        if c == 0:
+            rows_all, got_cot = lax.optimization_barrier((rows_all, got_cot))
+        got_chunks.append(got_cot)
+        partial_back = jnp.stack(
+            [
+                jnp.einsum(
+                    "scd,fd->scf", got_cot[:, g], matrix, preferred_element_type=jnp.float32
+                )
+                for g in range(groups)
+            ]
+        )
+        backs.append(lax.psum_scatter(partial_back, "dp", scatter_dimension=0, tiled=True)[0])
+    grad_matrix = sum(
+        jnp.einsum(
+            "gscf,sgcd->fd",
+            rows_all[:, :, c * step : (c + 1) * step],
+            got_chunks[c],
+            preferred_element_type=jnp.float32,
+        )
+        for c in range(CHUNKS)
     )
-    back = lax.psum_scatter(partial_back, "dp", scatter_dimension=0, tiled=True)[0]
-    grad_matrix = jnp.einsum(
-        "gscf,sgcd->fd", rows_all, got_cot, preferred_element_type=jnp.float32
-    )
+    back = jnp.concatenate(backs, axis=1)
     grad_hidden_rows = (got_gates[:, :, None] * back).astype(jnp.bfloat16)
     grad_gates_rows = jnp.sum(got_hidden.astype(jnp.float32) * back, axis=2)
     returned = lax.all_to_all(

time: 409 us -> 435 us (1.064); the launches traced: 409 us -> 428 us
  blocking collectives: 215 us -> 0 us
  waiting for transfers between devices: 82 us -> 251 us
  starting transfers between devices: 15.9 us -> 42.9 us
  local copies, waits for them, and re-layouts: 44.4 us -> 70.6 us
  other arithmetic: 15.4 us -> 21.7 us
  matrix products: 21.5 us -> 27.5 us
    all_to_all x2 -> x0, blocking collectives: 215 us -> none  [the longest x1 178 us: per_device(): lax.all_to_all(send_cot, 'expert', split_axis=0, concat_axis=0, tiled=True)]
    all_to_all x0 -> x3, waiting for transfers between devices: none -> 185 us  [the longest x2 154 us: per_device(): lax.all_to_all(send_cot[:, :, c * step:(c + 1) * step], 'expert', split_a...]
    all_to_all x0 -> x3, starting transfers between devices: none -> 26.4 us  [the longest x1 14.1 us: per_device(): lax.all_to_all(jnp.concatenate([send_hidden, split3(send_gates)], axis=2)...]
    all_to_all x1, waiting for transfers between devices: 31.3 us -> 12.8 us  [per_device(): lax.all_to_all(jnp.concatenate([grad_hidden_rows, split3(grad_gates_rows)...]
    reduce_scatter x1 -> x2, waiting for transfers between devices: 27.1 us -> 44.1 us  [per_device(): lax.psum_scatter(partial_back, 'dp', scatter_dimension=0, tiled=True)[0]]
    slice x1 -> x2, local copies, waits for them, and re-layouts: 0.02 us -> 14.7 us  [the longest x1 11.3 us: per_device(): send_cot[:, :, c * step:(c + 1) * step]]
    all_to_all x1, waiting for transfers between devices: 23.2 us -> 8.6 us  [per_device(): lax.all_to_all(cot_split, 'dp', split_axis=0, concat_axis=0, tiled=True)]
    optimization_barrier x0 -> x4, local copies, waits for them, and re-layouts: none -> 8.87 us  [the longest x3 5.6 us: per_device(): got, received = lax.optimization_barrier((got, received))]
  transfers between devices with their start and end apart: 4 -> 8, of which waited for: 4 -> 6; matrix products, arithmetic and copies ran while one was open for 5% -> 14% of each run, Pallas kernels for 0% -> 0%
where the time goes in v3:
time: 435 us; the launch traced here: 428 us
  waiting for transfers between devices  251 us (58%)
  local copies, waits for them, and re-layouts  70.6 us (16%)
  starting transfers between devices  42.9 us (10%)
  matrix products  27.5 us (6%)
  other arithmetic  21.7 us (5%)
  between operations  14.7 us (3%)
    all_to_all x2, waiting for transfers between devices, per_device(): lax.all_to_all(send_cot[:, :, c * step:(c + 1) * step], 'expert', split_a...  154 us
    reduce_scatter x2, waiting for transfers between devices, per_device(): lax.psum_scatter(partial_back, 'dp', scatter_dimension=0, tiled=True)[0]  44.1 us
    all_to_all x1, waiting for transfers between devices, per_device(): lax.all_to_all(jnp.concatenate([send_hidden, split3(send_gates)], axis=2)...  31.3 us
    dot_general x2, matrix products, per_device(): jnp.einsum('gscf,sgcd->fd', rows_all[:, :, c * step:(c + 1) * step], got_...  18.4 us
    all_to_all x1, starting transfers between devices, per_device(): lax.all_to_all(jnp.concatenate([send_hidden, split3(send_gates)], axis=2)...  14.1 us
    all_to_all x1, waiting for transfers between devices, per_device(): lax.all_to_all(jnp.concatenate([grad_hidden_rows, split3(grad_gates_rows)...  12.8 us
    all_to_all x2, starting transfers between devices, per_device(): lax.all_to_all(send_cot[:, :, c * step:(c + 1) * step], 'expert', split_a...  12.3 us
    slice x1, local copies, waits for them, and re-layouts, per_device(): send_cot[:, :, c * step:(c + 1) * step]  11.3 us
  transfers between devices with their start and end apart: 8, of which 6 were waited for; matrix products, arithmetic and copies ran while one was open for 14% of the time, Pallas kernels for 0%

profile of v3, /device:TPU:1, one launch (start us, length us, event | category | flops | bytes accessed | tf_op | source)
XLA Modules:
  0.0 428.0 jit_solution(7789883678921959359)
XLA Ops:
  7.2 0.6 compare_reduce_fusion
  7.8 1.3 broadcast_select_fusion.1
  9.3 3.3 copy.126
  12.6 2.5 copy.128
  15.1 3.0 pad_maximum_fusion.3
  18.1 5.1 %all-to-all-start.1 = ((bf16[4,128,1920]{2,1,0:T(8,128)(2,1)}), bf16[4,128,1920]{2,1,0:T(8,128)(2,1)S(1)}, u32[]{:S(2)}, u32[]{:S(2)}) async-start(bf16[4,128,1920]{2,1,0:T(8,128)(2,1)} %pad_maximum_fusion.3), calls=%async_computation.1 | async-start | bytes 3932160 | tf_op jit(solution)/shard_map/all_to_all | solution.py:63
  23.9 0.6 reduce-window.14
  24.5 0.2 slice_reduce_fusion
  25.1 1.4 scatter_custom_fusion
  26.6 3.5 gather_fusion.1
  30.3 0.8 copy.124
  31.1 0.8 copy.123
  31.9 0.8 copy.122
  32.7 0.2 reshape.250
  32.9 2.1 gather_fusion
  35.0 2.9 concatenate.14
  37.9 8.6 %all-to-all-done.1 = bf16[4,128,1920]{2,1,0:T(8,128)(2,1)S(1)} async-done(((bf16[4,128,1920]{2,1,0:T(8,128)(2,1)}), bf16[4,128,1920]{2,1,0:T(8,128)(2,1)S(1)}, u32[]{:S(2)}, u32[]{:S(2)}) %all-to-all-start.1) | async-done | bytes 1966112 | tf_op jit(solution)/shard_map/all_to_all | solution.py:63
  46.5 14.1 %all-to-all-start = ((bf16[64,8,1152]{2,1,0:T(8,128)(2,1)}), bf16[64,8,1152]{2,1,0:T(8,128)(2,1)S(1)}, u32[]{:S(2)}, u32[]{:S(2)}) async-start(bf16[64,8,1152]{2,1,0:T(8,128)(2,1)} %concatenate.14), calls=%async_computation | async-start | bytes 2359296 | tf_op jit(solution)/shard_map/all_to_all | solution.py:71
  60.7 31.3 %all-to-all-done = bf16[64,8,1152]{2,1,0:T(8,128)(2,1)S(1)} async-done(((bf16[64,8,1152]{2,1,0:T(8,128)(2,1)}), bf16[64,8,1152]{2,1,0:T(8,128)(2,1)S(1)}, u32[]{:S(2)}, u32[]{:S(2)}) %all-to-all-start) | async-done | bytes 1179680 | tf_op jit(solution)/shard_map/all_to_all | solution.py:71
  92.0 2.5 copy.131
  94.5 0.7 broadcast_multiply_fusion
  95.2 0.8 slice_convert_fusion.2
  96.6 0.7 fusion.53
  97.3 4.5 %reduce-window.16 = s32[4,64,2,128]{3,1,2,0:T(8,128)S(1)} reduce-window(s32[4,64,2,128]{3,1,2,0:T(8,128)} %fusion.53, s32[]{:T(128)} %constant.67.clone.1), window={size=1x1x1x128 pad=0_0x0_0x0_0x127_0}, to_apply=%region_5.6 | reduce-window | flops 8323072 | bytes 524292 | tf_op jit(solution)/shard_map/reduce-window.2
  101.8 0.8 slice.149
  102.7 1.1 copy.137
  104.1 0.2 copy.162
  104.6 4.5 %scatter_custom_fusion.1 = s32[2048]{0:T(1024)S(1)} fusion(s32[1024]{0:T(1024)S(1)} %bitcast.185, s32[1024]{0:T(1024)S(1)} %bitcast.184, s32[]{:T(128)} %constant.65.clone.1), kind=kCustom, calls=%fused_computation.114 | custom fusion | bytes 8196
  109.6 10.6 %gather_fusion.2 = bf16[2048,1792]{1,0:T(8,128)(2,1)} fusion(bf16[512,1792]{1,0:T(8,128)(2,1)S(1)} %bitcast.171, s32[2048]{0:T(1024)S(1)} %broadcast_clamp_fusion), kind=kCustom, calls=%fused_computation.2 | custom fusion | bytes 14688256 | tf_op jit(solution)/shard_map/gather | solution.py:92
  120.2 11.3 %fusion.72 = (bf16[64,4,4,1792]{3,2,1,0:T(4,128)(2,1)}, bf16[64,4,4,1792]{3,2,1,0:T(4,128)(2,1)}) fusion(bf16[64,4,8,1792]{3,2,1,0:T(8,128)(2,1)} %bitcast.172), kind=kLoop, calls=%fused_computation.126 | loop fusion | bytes 14680064 | tf_op jit(solution)/shard_map/slice | solution.py:99
  131.5 6.3 %all-to-all-start.2 = ((bf16[64,4,4,1792]{3,2,1,0:T(4,128)(2,1)}), bf16[64,4,4,1792]{3,2,1,0:T(4,128)(2,1)}, u32[]{:S(2)}, u32[]{:S(2)}) async-start(bf16[64,4,4,1792]{3,2,1,0:T(4,128)(2,1)} %get-tuple-element.35), calls=%async_computation.2 | async-start | bytes 7340032 | tf_op jit(solution)/shard_map/all_to_all | solution.py:98
  137.9 0.2 copy.130
  138.1 2.9 copy.129
  141.0 0.7 slice_convert_fusion.1
  141.7 1.2 fusion.23
  142.9 79.6 %all-to-all-done.2 = bf16[64,4,4,1792]{3,2,1,0:T(4,128)(2,1)} async-done(((bf16[64,4,4,1792]{3,2,1,0:T(4,128)(2,1)}), bf16[64,4,4,1792]{3,2,1,0:T(4,128)(2,1)}, u32[]{:S(2)}, u32[]{:S(2)}) %all-to-all-start.2) | async-done | bytes 3670048 | tf_op jit(solution)/shard_map/all_to_all | solution.py:98
  222.5 5.9 %all-to-all-start.3 = ((bf16[64,4,4,1792]{3,2,1,0:T(4,128)(2,1)}), bf16[64,4,4,1792]{3,2,1,0:T(4,128)(2,1)}, u32[]{:S(2)}, u32[]{:S(2)}) async-start(bf16[64,4,4,1792]{3,2,1,0:T(4,128)(2,1)} %get-tuple-element.36), calls=%async_computation.4 | async-start | bytes 7340032 | tf_op jit(solution)/shard_map/all_to_all | solution.py:98
  228.5 3.3 copy.145
  231.8 1.1 fusion.34
  232.9 1.1 fusion.31
  234.1 1.1 fusion.28
  235.2 1.1 fusion.25
  236.4 2.3 pad_maximum_fusion
  238.7 0.3 reduce-scatter.5.cloned.1.call-start
  239.0 74.1 %all-to-all-done.3 = bf16[64,4,4,1792]{3,2,1,0:T(4,128)(2,1)} async-done(((bf16[64,4,4,1792]{3,2,1,0:T(4,128)(2,1)}), bf16[64,4,4,1792]{3,2,1,0:T(4,128)(2,1)}, u32[]{:S(2)}, u32[]{:S(2)}) %all-to-all-start.3) | async-done | bytes 3670048 | tf_op jit(solution)/shard_map/all_to_all | solution.py:98
  313.1 3.4 fusion.73
  316.5 1.1 fusion.37
  317.7 1.1 fusion.43
  318.8 1.1 fusion.40
  320.0 1.1 fusion.46
  321.1 2.3 pad_maximum_fusion.1
  323.5 44.0 %reduce-scatter.5.cloned.1.call-done = f32[1,64,4,1024]{3,1,2,0:T(8,128)} async-done(((f32[4,64,4,1024]{3,1,2,0:T(8,128)}), f32[1,64,4,1024]{3,1,2,0:T(8,128)}) %reduce-scatter.5.cloned.1.call-update) | async-done | bytes 1048592 | tf_op jit(solution)/shard_map/reduce_scatter | solution.py:116
  367.5 1.9 fusion.24
  370.0 1.6 concatenate.17
  371.6 1.7 copy.156
  373.3 11.1 %all-to-all-start.4 = ((bf16[64,8,1152]{2,1,0:T(8,128)(2,1)}), bf16[64,8,1152]{2,1,0:T(8,128)(2,1)S(1)}, u32[]{:S(2)}, u32[]{:S(2)}) async-start(bf16[64,8,1152]{2,1,0:T(8,128)(2,1)} %copy.156), calls=%async_computation.6 | async-start | bytes 2359296 | tf_op jit(solution)/shard_map/all_to_all | solution.py:129
  384.4 8.2 %fusion.18 = f32[1024,1792,1,1]{1,0,3,2:T(8,128)S(1)} fusion(bf16[4,64,8,1024]{3,1,0,2:T(8,128)(2,1)} %bitcast.186, bf16[64,4,4,1792]{3,2,1,0:T(4,128)(2,1)} %all-to-all-done.2), kind=kOutput, calls=%fused_computation.28 | convolution fusion | flops 3758096384 | bytes 15204352 | tf_op jit(solution)/shard_map/gscf,sgcd->fd/dot_general | solution.py:118
  392.6 10.2 %fusion.20 = bf16[1,1024,1792]{2,1,0:T(8,128)(2,1)} fusion(bf16[4,64,8,1024]{3,1,0,2:T(8,128)(2,1)S(1)} %bitcast.187, bf16[64,4,4,1792]{3,2,1,0:T(4,128)(2,1)} %all-to-all-done.3, f32[1024,1792,1,1]{1,0,3,2:T(8,128)S(1)} %fusion.18), kind=kOutput, calls=%fused_computation.30 | convolution fusion | flops 3761766400 | bytes 18874368 | tf_op jit(solution)/shard_map/gscf,sgcd->fd/dot_general | solution.py:118
  402.8 12.8 %all-to-all-done.4 = bf16[64,8,1152]{2,1,0:T(8,128)(2,1)S(1)} async-done(((bf16[64,8,1152]{2,1,0:T(8,128)(2,1)}), bf16[64,8,1152]{2,1,0:T(8,128)(2,1)S(1)}, u32[]{:S(2)}, u32[]{:S(2)}) %all-to-all-start.4) | async-done | bytes 1179680 | tf_op jit(solution)/shard_map/all_to_all | solution.py:129
  415.6 0.3 fusion.52
  416.1 1.2 gather_fusion.3
  417.3 1.9 gather_fusion.4
  419.2 1.0 reshape.260
  420.4 0.6 copy.159
  (89 shorter events, 4.2 us)
Async XLA Ops:
  15.1 8.1 %copy-start.2 = (s32[128,2]{0,1:T(2,128)S(1)}, s32[128,2]{0,1:T(2,128)}, u32[]{:S(2)}) copy-start(s32[128,2]{0,1:T(2,128)} %param.8) | copy-start | bytes 3076
  15.1 9.6 %copy-start.3 = (f32[128,2]{0,1:T(2,128)S(1)}, f32[128,2]{0,1:T(2,128)}, u32[]{:S(2)}) copy-start(f32[128,2]{0,1:T(2,128)} %param.9) | copy-start | bytes 3076
  18.1 14.6 %copy-start.1 = (bf16[128,2,1024]{2,1,0:T(2,128)(2,1)S(1)}, bf16[128,2,1024]{2,1,0:T(2,128)(2,1)}, u32[]{:S(2)}) copy-start(bf16[128,2,1024]{2,1,0:T(2,128)(2,1)} %param.7) | copy-start | bytes 1572868
  18.1 28.4 %all-to-all-start.1 = ((bf16[4,128,1920]{2,1,0:T(8,128)(2,1)}), bf16[4,128,1920]{2,1,0:T(8,128)(2,1)S(1)}, u32[]{:S(2)}, u32[]{:S(2)}) async-start(bf16[4,128,1920]{2,1,0:T(8,128)(2,1)} %pad_maximum_fusion.3), calls=%async_computation.1 | async-start | bytes 3932160 | tf_op jit(solution)/shard_map/all_to_all | solution.py:63
  46.5 48.0 %copy-start = (bf16[4,128,1920]{2,1,0:T(8,128)(2,1)}, bf16[4,128,1920]{2,1,0:T(8,128)(2,1)S(1)}, u32[]{:S(2)}) copy-start(bf16[4,128,1920]{2,1,0:T(8,128)(2,1)S(1)} %all-to-all-done.1) | copy-start | bytes 5898244
  46.5 45.4 %all-to-all-start = ((bf16[64,8,1152]{2,1,0:T(8,128)(2,1)}), bf16[64,8,1152]{2,1,0:T(8,128)(2,1)S(1)}, u32[]{:S(2)}, u32[]{:S(2)}) async-start(bf16[64,8,1152]{2,1,0:T(8,128)(2,1)} %concatenate.14), calls=%async_computation | async-start | bytes 2359296 | tf_op jit(solution)/shard_map/all_to_all | solution.py:71
  92.0 12.0 %copy-start.5 = (s32[2]{0:T(128)S(1)}, s32[2]{0:T(128)}, u32[]{:S(2)}) copy-start(s32[2]{0:T(128)} %constant.88) | copy-start | bytes 28
  92.0 12.1 %copy-start.4 = (s32[2]{0:T(128)S(1)}, s32[2]{0:T(128)}, u32[]{:S(2)}) copy-start(s32[2]{0:T(128)} %constant.85) | copy-start | bytes 28
  95.2 14.4 %slice-start = ((bf16[4,128,1920]{2,1,0:T(8,128)(2,1)}), bf16[4,128,1792]{2,1,0:T(8,128)(2,1)S(1)}, s32[]{:S(2)}) async-start(bf16[4,128,1920]{2,1,0:T(8,128)(2,1)} %copy-done), calls=%async_computation.10 | async-start | bytes 3670016 | tf_op jit(solution)/shard_map/slice | solution.py:84
  131.5 91.0 %all-to-all-start.2 = ((bf16[64,4,4,1792]{3,2,1,0:T(4,128)(2,1)}), bf16[64,4,4,1792]{3,2,1,0:T(4,128)(2,1)}, u32[]{:S(2)}, u32[]{:S(2)}) async-start(bf16[64,4,4,1792]{3,2,1,0:T(4,128)(2,1)} %get-tuple-element.35), calls=%async_computation.2 | async-start | bytes 7340032 | tf_op jit(solution)/shard_map/all_to_all | solution.py:98
  137.9 90.6 %all-gather.3.cloned.1.call-start = ((), (), s32[]{:S(2)}) async-start(), calls=%async_computation.9 | async-start | bytes 5242880 | tf_op jit(solution)/shard_map/all_gather | solution.py:82
  222.5 90.6 %all-to-all-start.3 = ((bf16[64,4,4,1792]{3,2,1,0:T(4,128)(2,1)}), bf16[64,4,4,1792]{3,2,1,0:T(4,128)(2,1)}, u32[]{:S(2)}, u32[]{:S(2)}) async-start(bf16[64,4,4,1792]{3,2,1,0:T(4,128)(2,1)} %get-tuple-element.36), calls=%async_computation.4 | async-start | bytes 7340032 | tf_op jit(solution)/shard_map/all_to_all | solution.py:98
  228.4 95.0 %reduce-scatter.3.cloned.1.call-start = ((), (), s32[]{:S(2)}) async-start(), calls=%async_computation.7 | async-start | bytes 5242880 | tf_op jit(solution)/shard_map/reduce_scatter | solution.py:116
  228.5 3.3 copy-start.7
  238.7 128.8 %reduce-scatter.5.cloned.1.call-start = ((), (), s32[]{:S(2)}) async-start(), calls=%async_computation.8 | async-start | bytes 5242880 | tf_op jit(solution)/shard_map/reduce_scatter | solution.py:116
  313.1 3.4 copy-start.8
  373.3 42.3 %all-to-all-start.4 = ((bf16[64,8,1152]{2,1,0:T(8,128)(2,1)}), bf16[64,8,1152]{2,1,0:T(8,128)(2,1)S(1)}, u32[]{:S(2)}, u32[]{:S(2)}) async-start(bf16[64,8,1152]{2,1,0:T(8,128)(2,1)} %copy.156), calls=%async_computation.6 | async-start | bytes 2359296 | tf_op jit(solution)/shard_map/all_to_all | solution.py:129
  384.4 8.2 %copy-start.6 = (bf16[256,8,1024]{2,0,1:T(8,128)(2,1)S(1)}, bf16[256,8,1024]{2,0,1:T(8,128)(2,1)}, u32[]{:S(2)}) copy-start(bf16[256,8,1024]{2,0,1:T(8,128)(2,1)} %all-gather.3.cloned.1.call-done) | copy-start | bytes 12582916
Sparse Core Ops, SparseCore 0:
  143.1 49.7 all-gather.2
  238.8 48.4 reduce-scatter.2
  323.5 43.9 reduce-scatter.4

commit v4 on v3

--- a/solution.py
+++ b/solution.py
@@ -61,49 +61,58 @@
         axis=2,
     )
     received = lax.all_to_all(cot_split, "dp", split_axis=0, concat_axis=0, tiled=True)
-    clamped = jnp.minimum(slot_of, slot_count - 1)
-    send_hidden = hidden.reshape(slot_count, hidden_width)[clamped].reshape(
-        columns, capacity, hidden_width
-    )
-    send_gates = jnp.where(slot_of < slot_count, gates.reshape(slot_count)[clamped], 0.0).reshape(
-        columns, capacity
-    )
-    got = lax.all_to_all(
-        jnp.concatenate([send_hidden, split3(send_gates)], axis=2),
-        "expert",
-        split_axis=0,
-        concat_axis=0,
-        tiled=True,
-    )
-    got, received = lax.optimization_barrier((got, received))
-    got_hidden = got[:, :, :hidden_width]
-    got_gates = join3(got[:, :, hidden_width:])
-    scaled = (got_gates[:, :, None] * got_hidden.astype(jnp.float32)).astype(jnp.bfloat16)
-    rows_all = lax.all_gather(scaled, "dp", axis=0, tiled=False)
-
-    cot_q = received[:, :, :quarter]
     routes_all = received[:, :, quarter : quarter + top_count].astype(jnp.int32)
     _, slot_of_all = jax.vmap(lambda r: slots_for(r, columns, capacity))(
         routes_all.reshape(groups, slot_count)
     )
-    token_of = jnp.minimum(slot_of_all // top_count, local_tokens - 1)
+
+    gate_lanes = split3(gates.reshape(slot_count))
+    hidden_rows = jnp.concatenate(
+        [
+            hidden.reshape(slot_count, hidden_width),
+            gate_lanes,
+            jnp.zeros((slot_count, quarter - hidden_width - LANES), jnp.bfloat16),
+        ],
+        axis=1,
+    )
+    cot_rows = groups * local_tokens
+    zero_row = cot_rows + slot_count
+    table = jnp.concatenate(
+        [
+            received[:, :, :quarter].reshape(cot_rows, quarter),
+            hidden_rows,
+            jnp.zeros((8, quarter), jnp.bfloat16),
+        ],
+        axis=0,
+    )
+    token_of = slot_of_all // top_count + (jnp.arange(groups, dtype=jnp.int32) * local_tokens)[
+        :, None
+    ]
+    token_of = jnp.where(slot_of_all < slot_count, token_of, zero_row)
     token_of = token_of.reshape(groups, columns, capacity).transpose(1, 0, 2)
-    flat_token = token_of + (jnp.arange(groups, dtype=jnp.int32) * local_tokens)[None, :, None]
-    send_cot = cot_q.reshape(groups * local_tokens, quarter)[flat_token]
+    hidden_of = jnp.where(slot_of < slot_count, slot_of + cot_rows, zero_row).reshape(
+        columns, capacity
+    )
 
     matrix = weight[0]
-    step = capacity // CHUNKS
+    bounds = [0, capacity // 2, capacity]
     backs, got_chunks = [], []
-    for c in range(CHUNKS):
-        got_cot = lax.all_to_all(
-            send_cot[:, :, c * step : (c + 1) * step],
-            "expert",
-            split_axis=0,
-            concat_axis=0,
-            tiled=True,
-        )
+    for c in range(len(bounds) - 1):
+        step = bounds[c + 1] - bounds[c]
+        index = token_of[:, :, bounds[c] : bounds[c + 1]].reshape(columns, groups * step)
         if c == 0:
-            rows_all, got_cot = lax.optimization_barrier((rows_all, got_cot))
+            index = jnp.concatenate([index, hidden_of], axis=1)
+        got_rows = lax.all_to_all(table[index], "expert", split_axis=0, concat_axis=0, tiled=True)
+        if c == 0:
+            got_hidden = got_rows[:, groups * step :, :hidden_width]
+            got_gates = join3(got_rows[:, groups * step :, hidden_width : hidden_width + LANES])
+            scaled = (got_gates[:, :, None] * got_hidden.astype(jnp.float32)).astype(
+                jnp.bfloat16
+            )
+            rows_all = lax.all_gather(scaled, "dp", axis=0, tiled=False)
+        if c == 1:
+            rows_all, got_rows = lax.optimization_barrier((rows_all, got_rows))
+        got_cot = got_rows[:, : groups * step].reshape(columns, groups, step, quarter)
         got_chunks.append(got_cot)
         partial_back = jnp.stack(
             [
@@ -117,13 +126,14 @@
     grad_matrix = sum(
         jnp.einsum(
             "gscf,sgcd->fd",
-            rows_all[:, :, c * step : (c + 1) * step],
+            rows_all[:, :, bounds[c] : bounds[c + 1]],
             got_chunks[c],
             preferred_element_type=jnp.float32,
         )
-        for c in range(CHUNKS)
+        for c in range(len(bounds) - 1)
     )
     back = jnp.concatenate(backs, axis=1)
+    grad_matrix, back = lax.optimization_barrier((grad_matrix, back))
     grad_hidden_rows = (got_gates[:, :, None] * back).astype(jnp.bfloat16)
     grad_gates_rows = jnp.sum(got_hidden.astype(jnp.float32) * back, axis=2)
     returned = lax.all_to_all(

time: 435 us -> 421 us (0.968); the launches traced: 428 us -> 420 us
  blocking collectives: 0 us -> 138 us
  waiting for transfers between devices: 251 us -> 153 us
  starting transfers between devices: 42.9 us -> 22.3 us
  local copies, waits for them, and re-layouts: 70.6 us -> 50.9 us
  matrix products: 27.5 us -> 22.3 us
    all_to_all x0 -> x1, blocking collectives: none -> 138 us  [per_device(): lax.all_to_all(table[index], 'expert', split_axis=0, concat_axis=0, tiled...]
    all_to_all x3 -> x1, waiting for transfers between devices: 185 us -> 73.1 us  [per_device(): lax.all_to_all(table[index], 'expert', split_axis=0, concat_axis=0, tiled...]
    all_to_all x3 -> x1, starting transfers between devices: 26.4 us -> 6.34 us  [per_device(): lax.all_to_all(table[index], 'expert', split_axis=0, concat_axis=0, tiled...]
    all_to_all x1, waiting for transfers between devices: 12.8 us -> 31.3 us  [per_device(): lax.all_to_all(jnp.concatenate([grad_hidden_rows, split3(grad_gates_rows)...]
    reduce_scatter x2, waiting for transfers between devices: 44.1 us -> 30.9 us  [per_device(): lax.psum_scatter(partial_back, 'dp', scatter_dimension=0, tiled=True)[0]]
    slice x4 -> x9, local copies, waits for them, and re-layouts: 14.7 us -> 3.77 us  [the longest x2 2.03 us: per_device(): got_rows[:, :groups * step].reshape(columns, groups, step, quarter)]
    all_to_all x1, waiting for transfers between devices: 8.6 us -> 17.8 us  [per_device(): lax.all_to_all(cot_split, 'dp', split_axis=0, concat_axis=0, tiled=True)]
    unnamed x31 -> x44, local copies, waits for them, and re-layouts: 9.23 us -> 15 us
  transfers between devices with their start and end apart: 8 -> 6, of which waited for: 6 -> 4; matrix products, arithmetic and copies ran while one was open for 14% -> 10% of each run, Pallas kernels for 0% -> 0%
where the time goes in v4:
time: 421 us; the launch traced here: 420 us
  waiting for transfers between devices  153 us (36%)
  blocking collectives  138 us (33%)
  local copies, waits for them, and re-layouts  50.9 us (12%)
  starting transfers between devices  22.3 us (5%)
  matrix products  22.3 us (5%)
  other arithmetic  19.1 us (5%)
  between operations  14.4 us (3%)
    all_to_all x1, blocking collectives, per_device(): lax.all_to_all(table[index], 'expert', split_axis=0, concat_axis=0, tiled...  138 us
    all_to_all x1, waiting for transfers between devices, per_device(): lax.all_to_all(table[index], 'expert', split_axis=0, concat_axis=0, tiled...  73.1 us
    all_to_all x1, waiting for transfers between devices, per_device(): lax.all_to_all(jnp.concatenate([grad_hidden_rows, split3(grad_gates_rows)...  31.3 us
    reduce_scatter x2, waiting for transfers between devices, per_device(): lax.psum_scatter(partial_back, 'dp', scatter_dimension=0, tiled=True)[0]  30.9 us
    all_to_all x1, waiting for transfers between devices, per_device(): lax.all_to_all(cot_split, 'dp', split_axis=0, concat_axis=0, tiled=True)  17.8 us
    unnamed x44, local copies, waits for them, and re-layouts  15 us
    dot_general x2, matrix products, per_device(): jnp.einsum('gscf,sgcd->fd', rows_all[:, :, bounds[c]:bounds[c + 1]], got_...  13.2 us
    gather x2, local copies, waits for them, and re-layouts, per_device(): table[index]  12.5 us
  transfers between devices with their start and end apart: 6, of which 4 were waited for; matrix products, arithmetic and copies ran while one was open for 10% of the time, Pallas kernels for 0%

profile of v4, /device:TPU:1, one launch (start us, length us, event | category | flops | bytes accessed | tf_op | source)
XLA Modules:
  0.0 420.4 jit_solution(13790050036530061677)
XLA Ops:
  7.2 0.6 compare_reduce_fusion
  7.8 3.3 copy.113
  11.1 2.5 copy.115
  13.6 0.6 broadcast_select_fusion.1
  14.5 3.0 pad_maximum_fusion.3
  17.5 5.0 %all-to-all-start = ((bf16[4,128,1920]{2,1,0:T(8,128)(2,1)}), bf16[4,128,1920]{2,1,0:T(8,128)(2,1)S(1)}, u32[]{:S(2)}, u32[]{:S(2)}) async-start(bf16[4,128,1920]{2,1,0:T(8,128)(2,1)} %pad_maximum_fusion.3), calls=%async_computation | async-start | bytes 3932160 | tf_op jit(solution)/shard_map/all_to_all | solution.py:63
  23.0 0.6 reduce-window.16
  23.6 0.2 slice_reduce_fusion
  24.2 1.4 scatter_custom_fusion
  26.0 0.1 copy.117
  26.2 0.1 copy.118
  26.3 0.1 copy.119
  26.5 0.2 reshape.370
  26.8 1.1 concatenate.44
  27.9 17.8 %all-to-all-done = bf16[4,128,1920]{2,1,0:T(8,128)(2,1)S(1)} async-done(((bf16[4,128,1920]{2,1,0:T(8,128)(2,1)}), bf16[4,128,1920]{2,1,0:T(8,128)(2,1)S(1)}, u32[]{:S(2)}, u32[]{:S(2)}) %all-to-all-start) | async-done | bytes 1966112 | tf_op jit(solution)/shard_map/all_to_all | solution.py:63
  45.9 0.2 copy.122
  46.2 2.4 reduce-window.14
  49.0 0.2 copy.121
  49.2 0.2 fusion.47
  49.7 0.2 copy.155
  50.0 4.3 %scatter_custom_fusion.1 = s32[2048]{0:T(1024)S(1)} fusion(s32[1024]{0:T(1024)S(1)} %bitcast.198, s32[1024]{0:T(1024)S(1)} %bitcast.197, s32[]{:T(128)} %constant.73.clone.1), kind=kCustom, calls=%fused_computation.106 | custom fusion | bytes 8196
  55.1 1.7 maximum_maximum_fusion
  56.8 6.7 %gather_fusion = bf16[1536,1792]{1,0:T(8,128)(2,1)} fusion(bf16[776,1792]{1,0:T(8,128)(2,1)S(1)} %maximum_maximum_fusion, s32[2048]{0:T(1024)S(1)} %pad_clamp_fusion), kind=kCustom, calls=%fused_computation | custom fusion | bytes 11016192 | tf_op jit(solution)/shard_map/gather | solution.py:105
  63.5 138.1 %all_to_all.20 = bf16[64,24,1792]{2,1,0:T(8,128)(2,1)S(1)} all-to-all(bf16[64,24,1792]{2,1,0:T(8,128)(2,1)} %bitcast.171), channel_id=1, replica_groups=mesh['dp'=4,'expert'=64] {'expert'}, dimensions={0} | all-to-all | bytes 11010048 | tf_op jit(solution)/shard_map/all_to_all | solution.py:105
  201.7 2.4 copy-done
  204.1 0.2 copy.158
  204.3 1.3 slice.154
  205.6 1.0 copy-done.1
  206.6 1.7 fusion.19
  208.5 5.8 %gather_fusion.1 = bf16[1024,1792]{1,0:T(8,128)(2,1)} fusion(bf16[776,1792]{1,0:T(8,128)(2,1)S(1)} %maximum_maximum_fusion, s32[1024]{0:T(1024)S(1)} %broadcast_clamp_fusion), kind=kCustom, calls=%fused_computation.1 | custom fusion | bytes 7344128 | tf_op jit(solution)/shard_map/gather | solution.py:105
  214.3 6.3 %all-to-all-start.2 = ((bf16[64,16,1792]{2,1,0:T(8,128)(2,1)}), bf16[64,16,1792]{2,1,0:T(8,128)(2,1)}, u32[]{:S(2)}, u32[]{:S(2)}) async-start(bf16[64,16,1792]{2,1,0:T(8,128)(2,1)} %bitcast.172), calls=%async_computation.2 | async-start | bytes 7340032 | tf_op jit(solution)/shard_map/all_to_all | solution.py:105
  220.7 0.2 reduce-scatter.3.cloned.1.call-start
  220.9 2.0 slice-done
  222.9 1.1 copy.160
  224.1 1.1 copy-done.12
  225.2 1.1 fusion.21
  226.3 1.1 fusion.24
  227.5 1.1 fusion.27
  228.6 1.1 fusion.30
  229.8 2.3 pad_maximum_fusion
  232.2 73.1 %all-to-all-done.2 = bf16[64,16,1792]{2,1,0:T(8,128)(2,1)} async-done(((bf16[64,16,1792]{2,1,0:T(8,128)(2,1)}), bf16[64,16,1792]{2,1,0:T(8,128)(2,1)}, u32[]{:S(2)}, u32[]{:S(2)}) %all-to-all-start.2) | async-done | bytes 3670048 | tf_op jit(solution)/shard_map/all_to_all | solution.py:105
  305.3 3.4 copy.146
  308.7 1.1 fusion.33
  309.8 1.1 fusion.36
  311.0 1.1 fusion.39
  312.1 1.1 fusion.42
  313.3 2.3 pad_maximum_fusion.1
  315.6 7.1 %fusion.17 = f32[1024,1792,1,1]{1,0,3,2:T(8,128)S(1)} fusion(bf16[4,64,8,1024]{3,1,0,2:T(8,128)(2,1)} %bitcast.199, bf16[64,4,4,1792]{3,0,2,1:T(8,128)(2,1)} %bitcast.179), kind=kOutput, calls=%fused_computation.26 | convolution fusion | flops 3758096384 | bytes 15204352 | tf_op jit(solution)/shard_map/gscf,sgcd->fd/dot_general | solution.py:127
  322.7 6.1 %bitcast_add_fusion = bf16[1024,1792]{1,0:T(8,128)(2,1)} fusion(f32[1024,1792,1,1]{1,0,3,2:T(8,128)S(1)} %fusion.17, bf16[4,64,8,1024]{3,1,0,2:T(8,128)(2,1)S(1)} %bitcast.200, bf16[64,4,4,1792]{3,0,2,1:T(8,128)(2,1)S(1)} %bitcast.184), kind=kOutput, calls=%fused_computation.6 | convolution fusion | flops 3761766400 | bytes 18874368 | tf_op jit(solution)/shard_map/gscf,sgcd->fd/dot_general | solution.py:127
  328.8 30.9 %reduce-scatter.5.cloned.1.call-done = f32[1,64,4,1024]{3,1,2,0:T(8,128)} async-done(((f32[4,64,4,1024]{3,1,2,0:T(8,128)}), f32[1,64,4,1024]{3,1,2,0:T(8,128)}) %reduce-scatter.5.cloned.1.call-update) | async-done | bytes 1048592 | tf_op jit(solution)/shard_map/reduce_scatter | solution.py:125
  359.7 1.7 pad_maximum_fusion.2
  361.4 1.1 fusion.20
  362.5 0.2 copy.148
  362.7 0.2 copy.149
  362.8 0.2 copy.150
  363.0 1.6 concatenate.50
  364.6 1.7 copy.151
  366.3 10.7 %all-to-all-start.3 = ((bf16[64,8,1152]{2,1,0:T(8,128)(2,1)}), bf16[64,8,1152]{2,1,0:T(8,128)(2,1)S(1)}, u32[]{:S(2)}, u32[]{:S(2)}) async-start(bf16[64,8,1152]{2,1,0:T(8,128)(2,1)} %copy.151), calls=%async_computation.5 | async-start | bytes 2359296 | tf_op jit(solution)/shard_map/all_to_all | solution.py:139
  377.1 31.3 %all-to-all-done.3 = bf16[64,8,1152]{2,1,0:T(8,128)(2,1)S(1)} async-done(((bf16[64,8,1152]{2,1,0:T(8,128)(2,1)}), bf16[64,8,1152]{2,1,0:T(8,128)(2,1)S(1)}, u32[]{:S(2)}, u32[]{:S(2)}) %all-to-all-start.3) | async-done | bytes 1179680 | tf_op jit(solution)/shard_map/all_to_all | solution.py:139
  408.5 1.2 gather_fusion.2
  409.7 1.0 reshape.379
  410.7 0.3 fusion.48
  411.1 1.9 gather_fusion.3
  413.2 0.6 copy.152
  (107 shorter events, 4.1 us)
Async XLA Ops:
  7.8 5.8 %copy-start.7 = (s32[128,2]{0,1:T(2,128)S(1)}, s32[128,2]{0,1:T(2,128)}, u32[]{:S(2)}) copy-start(s32[128,2]{0,1:T(2,128)} %param.8) | copy-start | bytes 3076
  14.4 11.3 %copy-start.8 = (f32[128,2]{0,1:T(2,128)S(1)}, f32[128,2]{0,1:T(2,128)}, u32[]{:S(2)}) copy-start(f32[128,2]{0,1:T(2,128)} %param.9) | copy-start | bytes 3076
  14.5 12.0 %copy-start.6 = (bf16[128,2,1024]{2,1,0:T(2,128)(2,1)S(1)}, bf16[128,2,1024]{2,1,0:T(2,128)(2,1)}, u32[]{:S(2)}) copy-start(bf16[128,2,1024]{2,1,0:T(2,128)(2,1)} %param.7) | copy-start | bytes 1572868
  17.5 28.3 %all-to-all-start = ((bf16[4,128,1920]{2,1,0:T(8,128)(2,1)}), bf16[4,128,1920]{2,1,0:T(8,128)(2,1)S(1)}, u32[]{:S(2)}, u32[]{:S(2)}) async-start(bf16[4,128,1920]{2,1,0:T(8,128)(2,1)} %pad_maximum_fusion.3), calls=%async_computation | async-start | bytes 3932160 | tf_op jit(solution)/shard_map/all_to_all | solution.py:63
  22.5 282.8 %all-gather.3.cloned.1.call-start = ((), (), s32[]{:S(2)}) async-start(), calls=%async_computation.8 | async-start | bytes 5242880 | tf_op jit(solution)/shard_map/all_gather | solution.py:112
  22.9 26.5 %copy-start.10 = (s32[2]{0:T(128)S(1)}, s32[2]{0:T(128)}, u32[]{:S(2)}) copy-start(s32[2]{0:T(128)} %constant.89) | copy-start | bytes 28
  23.6 26.1 %copy-start.9 = (s32[2]{0:T(128)S(1)}, s32[2]{0:T(128)}, u32[]{:S(2)}) copy-start(s32[2]{0:T(128)} %constant.92) | copy-start | bytes 28
  201.7 2.4 copy-start
  205.6 1.0 copy-start.1
  214.3 91.0 %all-to-all-start.2 = ((bf16[64,16,1792]{2,1,0:T(8,128)(2,1)}), bf16[64,16,1792]{2,1,0:T(8,128)(2,1)}, u32[]{:S(2)}, u32[]{:S(2)}) async-start(bf16[64,16,1792]{2,1,0:T(8,128)(2,1)} %bitcast.172), calls=%async_computation.2 | async-start | bytes 7340032 | tf_op jit(solution)/shard_map/all_to_all | solution.py:105
  220.7 108.2 %reduce-scatter.3.cloned.1.call-start = ((), (), s32[]{:S(2)}) async-start(), calls=%async_computation.6 | async-start | bytes 5242880 | tf_op jit(solution)/shard_map/reduce_scatter | solution.py:125
  220.9 2.0 slice-start
  222.9 2.2 copy-start.12
  224.0 4.6 %copy-start.3 = (bf16[64,16,1792]{2,0,1:T(8,128)(2,1)}, bf16[64,16,1792]{2,0,1:T(8,128)(2,1)S(1)}, u32[]{:S(2)}) copy-start(bf16[64,16,1792]{2,0,1:T(8,128)(2,1)S(1)} %copy.160) | copy-start | bytes 11010052
  232.1 127.6 %reduce-scatter.5.cloned.1.call-start = ((), (), s32[]{:S(2)}) async-start(), calls=%async_computation.7 | async-start | bytes 5242880 | tf_op jit(solution)/shard_map/reduce_scatter | solution.py:125
  305.3 3.4 copy-start.13
  308.7 3.5 copy-start.4
  315.6 7.1 %copy-start.5 = (bf16[64,16,1792]{2,0,1:T(8,128)(2,1)S(1)}, bf16[64,16,1792]{2,0,1:T(8,128)(2,1)}, u32[]{:S(2)}) copy-start(bf16[64,16,1792]{2,0,1:T(8,128)(2,1)} %copy-done.4) | copy-start | bytes 11010052
  315.6 7.1 %copy-start.11 = (bf16[256,8,1024]{2,0,1:T(8,128)(2,1)S(1)}, bf16[256,8,1024]{2,0,1:T(8,128)(2,1)}, u32[]{:S(2)}) copy-start(bf16[256,8,1024]{2,0,1:T(8,128)(2,1)} %all-gather.3.cloned.1.call-done) | copy-start | bytes 12582916
  328.8 32.5 %copy-start.2 = (bf16[64,8,1024]{2,1,0:T(8,128)(2,1)S(1)}, bf16[64,8,1024]{2,1,0:T(8,128)(2,1)}, u32[]{:S(2)}) copy-start(bf16[64,8,1024]{2,1,0:T(8,128)(2,1)} %copy-done.1) | copy-start | bytes 3145732
  366.3 42.1 %all-to-all-start.3 = ((bf16[64,8,1152]{2,1,0:T(8,128)(2,1)}), bf16[64,8,1152]{2,1,0:T(8,128)(2,1)S(1)}, u32[]{:S(2)}, u32[]{:S(2)}) async-start(bf16[64,8,1152]{2,1,0:T(8,128)(2,1)} %copy.151), calls=%async_computation.5 | async-start | bytes 2359296 | tf_op jit(solution)/shard_map/all_to_all | solution.py:139
Sparse Core Ops, SparseCore 0:
  208.4 45.5 all-gather.2
  256.5 49.8 reduce-scatter.2
  315.7 43.9 reduce-scatter.4

commit v5 on v4

--- a/solution.py
+++ b/solution.py
@@ -24,15 +24,18 @@
 CHUNKS = 2
 
 
-def split3(values):
+def split3(values, lanes=LANES):
     pieces = []
     rest = values
     for _ in range(3):
         head = lax.reduce_precision(rest, exponent_bits=8, mantissa_bits=7)
         pieces.append(head.astype(jnp.bfloat16))
         rest = rest - head
-    pad = jnp.zeros(values.shape + (LANES - 3,), jnp.bfloat16)
-    return jnp.concatenate([jnp.stack(pieces, axis=-1), pad], axis=-1)
+    terms = jnp.stack(pieces, axis=-1)
+    if lanes == 3:
+        return terms
+    pad = jnp.zeros(values.shape + (lanes - 3,), jnp.bfloat16)
+    return jnp.concatenate([terms, pad], axis=-1)
 
 
 def join3(lanes):
@@ -66,33 +69,33 @@
         routes_all.reshape(groups, slot_count)
     )
 
-    gate_lanes = split3(gates.reshape(slot_count))
-    hidden_rows = jnp.concatenate(
-        [
-            hidden.reshape(slot_count, hidden_width),
-            gate_lanes,
-            jnp.zeros((slot_count, quarter - hidden_width - LANES), jnp.bfloat16),
-        ],
-        axis=1,
-    )
     cot_rows = groups * local_tokens
-    zero_row = cot_rows + slot_count
     table = jnp.concatenate(
-        [
-            received[:, :, :quarter].reshape(cot_rows, quarter),
-            hidden_rows,
-            jnp.zeros((8, quarter), jnp.bfloat16),
-        ],
+        [received[:, :, :quarter].reshape(cot_rows, quarter), jnp.zeros((8, quarter), jnp.bfloat16)],
         axis=0,
     )
     token_of = slot_of_all // top_count + (jnp.arange(groups, dtype=jnp.int32) * local_tokens)[
         :, None
     ]
-    token_of = jnp.where(slot_of_all < slot_count, token_of, zero_row)
+    token_of = jnp.where(slot_of_all < slot_count, token_of, cot_rows)
     token_of = token_of.reshape(groups, columns, capacity).transpose(1, 0, 2)
-    hidden_of = jnp.where(slot_of < slot_count, slot_of + cot_rows, zero_row).reshape(
-        columns, capacity
+
+    clamped = jnp.minimum(slot_of, slot_count - 1)
+    send_hidden = hidden.reshape(slot_count, hidden_width)[clamped].reshape(
+        columns, capacity * hidden_width
     )
+    send_gates = jnp.where(slot_of < slot_count, gates.reshape(slot_count)[clamped], 0.0)
+    gate_terms = split3(send_gates, 3).reshape(columns, capacity * 3)
+    packed = capacity * hidden_width + capacity * 3
+    packed_rows = -(-packed // quarter)
+    hidden_rows = jnp.concatenate(
+        [
+            send_hidden,
+            gate_terms,
+            jnp.zeros((columns, packed_rows * quarter - packed), jnp.bfloat16),
+        ],
+        axis=1,
+    ).reshape(columns, packed_rows, quarter)
 
     matrix = weight[0]
     bounds = [0, capacity // 2, capacity]
@@ -100,12 +103,18 @@
     for c in range(len(bounds) - 1):
         step = bounds[c + 1] - bounds[c]
         index = token_of[:, :, bounds[c] : bounds[c + 1]].reshape(columns, groups * step)
+        payload = table[index]
         if c == 0:
-            index = jnp.concatenate([index, hidden_of], axis=1)
-        got_rows = lax.all_to_all(table[index], "expert", split_axis=0, concat_axis=0, tiled=True)
+            payload = jnp.concatenate([payload, hidden_rows], axis=1)
+        got_rows = lax.all_to_all(payload, "expert", split_axis=0, concat_axis=0, tiled=True)
         if c == 0:
-            got_hidden = got_rows[:, groups * step :, :hidden_width]
-            got_gates = join3(got_rows[:, groups * step :, hidden_width : hidden_width + LANES])
+            got_packed = got_rows[:, groups * step :].reshape(columns, packed_rows * quarter)
+            got_hidden = got_packed[:, : capacity * hidden_width].reshape(
+                columns, capacity, hidden_width
+            )
+            got_gates = join3(
+                got_packed[:, capacity * hidden_width : packed].reshape(columns, capacity, 3)
+            )
             scaled = (got_gates[:, :, None] * got_hidden.astype(jnp.float32)).astype(
                 jnp.bfloat16
             )

time: 421 us -> 425 us (level)
  local copies, waits for them, and re-layouts: 50.9 us -> 64.2 us
  waiting for transfers between devices: 153 us -> 140 us
    all_to_all x1, waiting for transfers between devices: 17.8 us -> 5.04 us  [per_device(): lax.all_to_all(cot_split, 'dp', split_axis=0, concat_axis=0, tiled=True)]
    reshape x2 -> x5, local copies, waits for them, and re-layouts: 0.34 us -> 5.86 us  [the longest x1 4.08 us: per_device(): hidden_rows = jnp.concatenate([send_hidden, gate_terms, jnp.zeros((column...]
    gather x2 -> x4, local copies, waits for them, and re-layouts: 12.5 us -> 17.3 us  [the longest x2 11.6 us: per_device(): payload = table[index]]
    unnamed x44 -> x52, local copies, waits for them, and re-layouts: 15 us -> 17.5 us
  transfers between devices with their start and end apart: 6 -> 6, of which waited for: 4 -> 4; matrix products, arithmetic and copies ran while one was open for 10% -> 13% of each run, Pallas kernels for 0% -> 0%
where the time goes in v5:
time: 425 us; the launch traced here: 424 us
  waiting for transfers between devices  140 us (33%)
  blocking collectives  138 us (32%)
  local copies, waits for them, and re-layouts  64.2 us (15%)
  starting transfers between devices  22.5 us (5%)
  matrix products  22.3 us (5%)
  other arithmetic  22.2 us (5%)
  between operations  14.4 us (3%)
    all_to_all x1, blocking collectives, per_device(): lax.all_to_all(payload, 'expert', split_axis=0, concat_axis=0, tiled=True)  138 us
    all_to_all x1, waiting for transfers between devices, per_device(): lax.all_to_all(payload, 'expert', split_axis=0, concat_axis=0, tiled=True)  73.1 us
    all_to_all x1, waiting for transfers between devices, per_device(): lax.all_to_all(jnp.concatenate([grad_hidden_rows, split3(grad_gates_rows)...  31.3 us
    reduce_scatter x2, waiting for transfers between devices, per_device(): lax.psum_scatter(partial_back, 'dp', scatter_dimension=0, tiled=True)[0]  30.8 us
    unnamed x52, local copies, waits for them, and re-layouts  17.5 us
    dot_general x2, matrix products, per_device(): jnp.einsum('gscf,sgcd->fd', rows_all[:, :, bounds[c]:bounds[c + 1]], got_...  13.2 us
    gather x2, local copies, waits for them, and re-layouts, per_device(): payload = table[index]  11.6 us
    all_to_all x1, starting transfers between devices, per_device(): lax.all_to_all(jnp.concatenate([grad_hidden_rows, split3(grad_gates_rows)...  10.7 us
  transfers between devices with their start and end apart: 6, of which 4 were waited for; matrix products, arithmetic and copies ran while one was open for 13% of the time, Pallas kernels for 0%

profile of v5, /device:TPU:1, one launch (start us, length us, event | category | flops | bytes accessed | tf_op | source)
XLA Modules:
  0.0 423.9 jit_solution(2606452769684609341)
XLA Ops:
  7.2 0.6 compare_reduce_fusion
  7.8 3.3 copy.113
  11.1 2.5 copy.115
  13.6 0.6 broadcast_select_fusion.1
  14.5 3.0 pad_maximum_fusion.4
  17.4 5.1 %all-to-all-start = ((bf16[4,128,1920]{2,1,0:T(8,128)(2,1)}), bf16[4,128,1920]{2,1,0:T(8,128)(2,1)S(1)}, u32[]{:S(2)}, u32[]{:S(2)}) async-start(bf16[4,128,1920]{2,1,0:T(8,128)(2,1)} %pad_maximum_fusion.4), calls=%async_computation | async-start | bytes 3932160 | tf_op jit(solution)/shard_map/all_to_all | solution.py:66
  22.8 0.6 reduce-window.16
  23.5 0.2 slice_reduce_fusion
  24.5 1.4 scatter_custom_fusion
  25.9 3.5 gather_fusion.2
  29.5 0.2 copy.136
  29.9 0.2 reshape.305
  30.1 2.2 gather_fusion.1
  32.3 1.3 reshape.307
  33.6 3.1 concatenate.22
  36.7 4.1 reshape.310
  40.8 5.0 %all-to-all-done = bf16[4,128,1920]{2,1,0:T(8,128)(2,1)S(1)} async-done(((bf16[4,128,1920]{2,1,0:T(8,128)(2,1)}), bf16[4,128,1920]{2,1,0:T(8,128)(2,1)S(1)}, u32[]{:S(2)}, u32[]{:S(2)}) %all-to-all-start) | async-done | bytes 1966112 | tf_op jit(solution)/shard_map/all_to_all | solution.py:66
  46.3 2.4 reduce-window.14
  49.0 0.2 copy.117
  49.8 0.2 copy.153
  50.1 4.3 %scatter_custom_fusion.1 = s32[2048]{0:T(1024)S(1)} fusion(s32[1024]{0:T(1024)S(1)} %bitcast.216, s32[1024]{0:T(1024)S(1)} %bitcast.215, s32[]{:T(128)} %constant.71.clone.1), kind=kCustom, calls=%fused_computation.110 | custom fusion | bytes 8196
  55.3 5.8 %gather_fusion = bf16[1024,1792]{1,0:T(8,128)(2,1)} fusion(bf16[520,1792]{1,0:T(8,128)(2,1)S(1)} %concatenate.21, s32[1024]{0:T(1024)S(1)} %broadcast_clamp_fusion.1), kind=kCustom, calls=%fused_computation | custom fusion | bytes 7344128 | tf_op jit(solution)/shard_map/gather | solution.py:106
  61.1 3.1 pad_maximum_fusion
  64.2 137.9 %all_to_all.20 = bf16[64,21,1792]{2,1,0:T(8,128)(2,1)S(1)} all-to-all(bf16[64,21,1792]{2,1,0:T(8,128)(2,1)S(1)} %pad_maximum_fusion), channel_id=1, replica_groups=mesh['dp'=4,'expert'=64] {'expert'}, dimensions={0} | all-to-all | bytes 9633792 | tf_op jit(solution)/shard_map/all_to_all | solution.py:109
  202.2 0.2 copy.164
  202.6 1.9 copy-done
  204.6 1.3 copy-done.1
  205.9 2.5 copy.165
  208.6 3.9 fusion.20
  212.7 5.8 %gather_fusion.3 = bf16[1024,1792]{1,0:T(8,128)(2,1)} fusion(bf16[520,1792]{1,0:T(8,128)(2,1)S(1)} %concatenate.21, s32[1024]{0:T(1024)S(1)} %broadcast_clamp_fusion), kind=kCustom, calls=%fused_computation.3 | custom fusion | bytes 7344128 | tf_op jit(solution)/shard_map/gather | solution.py:106
  218.5 6.3 %all-to-all-start.2 = ((bf16[64,16,1792]{2,1,0:T(8,128)(2,1)}), bf16[64,16,1792]{2,1,0:T(8,128)(2,1)}, u32[]{:S(2)}, u32[]{:S(2)}) async-start(bf16[64,16,1792]{2,1,0:T(8,128)(2,1)} %bitcast.183), calls=%async_computation.2 | async-start | bytes 7340032 | tf_op jit(solution)/shard_map/all_to_all | solution.py:109
  224.9 2.0 slice-done
  227.0 1.1 copy.157
  228.1 1.1 copy-done.15
  229.1 1.1 fusion.21
  230.3 1.1 fusion.24
  231.4 1.1 fusion.27
  232.6 1.1 fusion.30
  233.7 2.4 pad_maximum_fusion.1
  236.1 0.3 reduce-scatter.5.cloned.1.call-start
  236.4 73.1 %all-to-all-done.2 = bf16[64,16,1792]{2,1,0:T(8,128)(2,1)} async-done(((bf16[64,16,1792]{2,1,0:T(8,128)(2,1)}), bf16[64,16,1792]{2,1,0:T(8,128)(2,1)}, u32[]{:S(2)}, u32[]{:S(2)}) %all-to-all-start.2) | async-done | bytes 3670048 | tf_op jit(solution)/shard_map/all_to_all | solution.py:109
  309.5 3.4 copy.143
  312.9 1.1 fusion.33
  314.0 1.1 fusion.36
  315.2 1.1 fusion.39
  316.3 1.1 fusion.42
  317.5 2.3 pad_maximum_fusion.2
  319.8 7.1 %fusion.17 = f32[1024,1792,1,1]{1,0,3,2:T(8,128)S(1)} fusion(bf16[4,64,8,1024]{3,1,0,2:T(8,128)(2,1)} %all-gather.2.cloned.1.call-done, bf16[64,4,4,1792]{3,0,2,1:T(8,128)(2,1)} %bitcast.195), kind=kOutput, calls=%fused_computation.29 | convolution fusion | flops 3758096384 | bytes 15204352 | tf_op jit(solution)/shard_map/gscf,sgcd->fd/dot_general | solution.py:136
  326.9 6.2 %bitcast_add_fusion = bf16[1024,1792]{1,0:T(8,128)(2,1)} fusion(f32[1024,1792,1,1]{1,0,3,2:T(8,128)S(1)} %fusion.17, bf16[4,64,8,1024]{3,1,0,2:T(8,128)(2,1)S(1)} %copy-done.14, bf16[64,4,4,1792]{3,0,2,1:T(8,128)(2,1)S(1)} %bitcast.200), kind=kOutput, calls=%fused_computation.8 | convolution fusion | flops 3761766400 | bytes 18874368 | tf_op jit(solution)/shard_map/gscf,sgcd->fd/dot_general | solution.py:136
  333.0 30.8 %reduce-scatter.5.cloned.1.call-done = f32[1,64,4,1024]{3,1,2,0:T(8,128)} async-done(((f32[4,64,4,1024]{3,1,2,0:T(8,128)}), f32[1,64,4,1024]{3,1,2,0:T(8,128)}) %reduce-scatter.5.cloned.1.call-update) | async-done | bytes 1048592 | tf_op jit(solution)/shard_map/reduce_scatter | solution.py:134
  363.8 1.7 pad_maximum_fusion.3
  365.5 0.5 fusion.19
  366.0 0.2 copy.146
  366.2 0.2 copy.147
  366.3 0.2 copy.148
  366.6 1.6 concatenate.25
  368.2 1.7 copy.149
  369.8 10.7 %all-to-all-start.3 = ((bf16[64,8,1152]{2,1,0:T(8,128)(2,1)}), bf16[64,8,1152]{2,1,0:T(8,128)(2,1)S(1)}, u32[]{:S(2)}, u32[]{:S(2)}) async-start(bf16[64,8,1152]{2,1,0:T(8,128)(2,1)} %copy.149), calls=%async_computation.5 | async-start | bytes 2359296 | tf_op jit(solution)/shard_map/all_to_all | solution.py:148
  380.6 31.3 %all-to-all-done.3 = bf16[64,8,1152]{2,1,0:T(8,128)(2,1)S(1)} async-done(((bf16[64,8,1152]{2,1,0:T(8,128)(2,1)}), bf16[64,8,1152]{2,1,0:T(8,128)(2,1)S(1)}, u32[]{:S(2)}, u32[]{:S(2)}) %all-to-all-start.3) | async-done | bytes 1179680 | tf_op jit(solution)/shard_map/all_to_all | solution.py:148
  412.0 1.2 gather_fusion.4
  413.2 1.0 reshape.316
  414.2 0.3 fusion.48
  414.6 1.9 gather_fusion.5
  416.7 0.6 copy.150
  (120 shorter events, 4.9 us)
Async XLA Ops:
  7.8 5.8 %copy-start.8 = (s32[128,2]{0,1:T(2,128)S(1)}, s32[128,2]{0,1:T(2,128)}, u32[]{:S(2)}) copy-start(s32[128,2]{0,1:T(2,128)} %param.8) | copy-start | bytes 3076
  14.4 9.7 %copy-start.11 = (f32[128,2]{0,1:T(2,128)S(1)}, f32[128,2]{0,1:T(2,128)}, u32[]{:S(2)}) copy-start(f32[128,2]{0,1:T(2,128)} %param.9) | copy-start | bytes 3076
  17.4 12.4 %copy-start.6 = (bf16[128,2,1024]{2,1,0:T(2,128)(2,1)S(1)}, bf16[128,2,1024]{2,1,0:T(2,128)(2,1)}, u32[]{:S(2)}) copy-start(bf16[128,2,1024]{2,1,0:T(2,128)(2,1)} %param.7) | copy-start | bytes 1572868
  17.4 28.4 %all-to-all-start = ((bf16[4,128,1920]{2,1,0:T(8,128)(2,1)}), bf16[4,128,1920]{2,1,0:T(8,128)(2,1)S(1)}, u32[]{:S(2)}, u32[]{:S(2)}) async-start(bf16[4,128,1920]{2,1,0:T(8,128)(2,1)} %pad_maximum_fusion.4), calls=%async_computation | async-start | bytes 3932160 | tf_op jit(solution)/shard_map/all_to_all | solution.py:66
  22.6 286.9 %all-gather.2.cloned.1.call-start = ((), (), s32[]{:S(2)}) async-start(), calls=%async_computation.6 | async-start | bytes 5242880 | tf_op jit(solution)/shard_map/all_gather | solution.py:121
  24.5 1.4 copy-start.9
  25.9 3.6 copy-start.7
  33.6 15.9 %copy-start.13 = (s32[2]{0:T(128)S(1)}, s32[2]{0:T(128)}, u32[]{:S(2)}) copy-start(s32[2]{0:T(128)} %constant.89) | copy-start | bytes 28
  33.6 16.1 %copy-start.12 = (s32[2]{0:T(128)S(1)}, s32[2]{0:T(128)}, u32[]{:S(2)}) copy-start(s32[2]{0:T(128)} %constant.92) | copy-start | bytes 28
  202.1 2.5 copy-start
  204.6 1.4 copy-start.1
  218.5 91.0 %all-to-all-start.2 = ((bf16[64,16,1792]{2,1,0:T(8,128)(2,1)}), bf16[64,16,1792]{2,1,0:T(8,128)(2,1)}, u32[]{:S(2)}, u32[]{:S(2)}) async-start(bf16[64,16,1792]{2,1,0:T(8,128)(2,1)} %bitcast.183), calls=%async_computation.2 | async-start | bytes 7340032 | tf_op jit(solution)/shard_map/all_to_all | solution.py:109
  224.9 108.2 %reduce-scatter.3.cloned.1.call-start = ((), (), s32[]{:S(2)}) async-start(), calls=%async_computation.7 | async-start | bytes 5242880 | tf_op jit(solution)/shard_map/reduce_scatter | solution.py:134
  224.9 2.0 slice-start
  226.9 2.2 copy-start.15
  228.0 4.5 %copy-start.3 = (bf16[64,16,1792]{2,0,1:T(8,128)(2,1)}, bf16[64,16,1792]{2,0,1:T(8,128)(2,1)S(1)}, u32[]{:S(2)}) copy-start(bf16[64,16,1792]{2,0,1:T(8,128)(2,1)S(1)} %copy.157) | copy-start | bytes 11010052
  236.1 127.7 %reduce-scatter.5.cloned.1.call-start = ((), (), s32[]{:S(2)}) async-start(), calls=%async_computation.8 | async-start | bytes 5242880 | tf_op jit(solution)/shard_map/reduce_scatter | solution.py:134
  309.5 3.4 copy-start.16
  312.9 3.5 copy-start.4
  319.8 7.1 %copy-start.5 = (bf16[64,16,1792]{2,0,1:T(8,128)(2,1)S(1)}, bf16[64,16,1792]{2,0,1:T(8,128)(2,1)}, u32[]{:S(2)}) copy-start(bf16[64,16,1792]{2,0,1:T(8,128)(2,1)} %copy-done.4) | copy-start | bytes 11010052
  319.8 7.1 %copy-start.14 = (bf16[4,64,8,1024]{3,1,0,2:T(8,128)(2,1)S(1)}, bf16[4,64,8,1024]{3,1,0,2:T(8,128)(2,1)}, u32[]{:S(2)}) copy-start(bf16[4,64,8,1024]{3,1,0,2:T(8,128)(2,1)} %all-gather.2.cloned.1.call-done) | copy-start | bytes 12582916
  333.0 32.5 %copy-start.2 = (f32[64,8192]{1,0:T(8,128)S(1)}, f32[64,8192]{1,0:T(8,128)}, u32[]{:S(2)}) copy-start(f32[64,8192]{1,0:T(8,128)} %copy-done.1) | copy-start | bytes 6291460
  366.5 14.0 %copy-start.10 = (s32[256,1]{0,1:T(1,128)S(1)}, s32[256,1]{0,1:T(1,128)}, u32[]{:S(2)}) copy-start(s32[256,1]{0,1:T(1,128)} %copy-done.9) | copy-start | bytes 3076
  369.8 42.0 %all-to-all-start.3 = ((bf16[64,8,1152]{2,1,0:T(8,128)(2,1)}), bf16[64,8,1152]{2,1,0:T(8,128)(2,1)S(1)}, u32[]{:S(2)}, u32[]{:S(2)}) async-start(bf16[64,8,1152]{2,1,0:T(8,128)(2,1)} %copy.149), calls=%async_computation.5 | async-start | bytes 2359296 | tf_op jit(solution)/shard_map/all_to_all | solution.py:148
Sparse Core Ops, SparseCore 0:
  212.6 45.5 all-gather.1
  260.7 49.8 reduce-scatter.2
  319.9 43.9 reduce-scatter.4

commit v6 on v1

--- a/solution.py
+++ b/solution.py
@@ -59,7 +59,10 @@
             for g in range(groups)
         ]
     )
-    back = lax.psum_scatter(partial_back, "dp", scatter_dimension=0, tiled=True)[0]
+    parts = lax.all_to_all(
+        partial_back.astype(jnp.bfloat16), "dp", split_axis=0, concat_axis=0, tiled=True
+    )
+    back = jnp.sum(parts.astype(jnp.float32), axis=0)
     grad_matrix = jnp.einsum(
         "gscf,sgcd->fd", rows_all, got_cot, preferred_element_type=jnp.float32
     )

time: 405 us -> 443 us (1.094)
  blocking collectives: 254 us -> 38.6 us
  waiting for transfers between devices: 54 us -> 251 us
  starting transfers between devices: 16.4 us -> 47.2 us
  matrix products: 21.5 us -> 40.8 us
  local copies, waits for them, and re-layouts: 33.1 us -> 38.5 us
    all_to_all x0 -> x3, waiting for transfers between devices: none -> 226 us  [the longest x1 156 us: per_device(): lax.all_to_all(send_cot, 'expert', split_axis=0, concat_axis=0, tiled=True)]
    all_to_all x2 -> x0, blocking collectives: 211 us -> none  [the longest x1 178 us: per_device(): lax.all_to_all(send_cot, 'expert', split_axis=0, concat_axis=0, tiled=True)]
    all_to_all x0 -> x3, starting transfers between devices: none -> 31.3 us  [the longest x1 14.9 us: per_device(): lax.all_to_all(send_cot, 'expert', split_axis=0, concat_axis=0, tiled=True)]
    reduce_scatter x1 -> x0, waiting for transfers between devices: 22.8 us -> none  [per_device(): lax.psum_scatter(partial_back, 'dp', scatter_dimension=0, tiled=True)[0]]
    dot_general x1, matrix products: 13.1 us -> 25.1 us  [per_device(): jnp.einsum('gscf,sgcd->fd', rows_all, got_cot, preferred_element_type=jnp...]
    dot_general x4, matrix products: 8.36 us -> 15.7 us  [per_device(): jnp.einsum('scd,fd->scf', got_cot[:, g], matrix, preferred_element_type=j...]
    all_to_all x1, waiting for transfers between devices: 6.69 us -> 0.01 us  [per_device(): lax.all_to_all(send_gates, 'expert', split_axis=0, concat_axis=0, tiled=T...]
    all_gather x0 -> x1, local copies, waits for them, and re-layouts: none -> 4.51 us  [per_device(): rows_all = lax.all_gather(scaled, 'dp', axis=0, tiled=False)]
  transfers between devices with their start and end apart: 5 -> 7, of which waited for: 3 -> 4; matrix products, arithmetic and copies ran while one was open for 6% -> 10% of each run, Pallas kernels for 0% -> 0%
where the time goes in v6:
time: 443 us; the launch traced here: 442 us
  waiting for transfers between devices  251 us (57%)
  starting transfers between devices  47.2 us (11%)
  matrix products  40.8 us (9%)
  blocking collectives  38.6 us (9%)
  local copies, waits for them, and re-layouts  38.5 us (9%)
  between operations  14.4 us (3%)
  other arithmetic  11.8 us (3%)
    all_to_all x1, waiting for transfers between devices, per_device(): lax.all_to_all(send_cot, 'expert', split_axis=0, concat_axis=0, tiled=True)  156 us
    all_to_all x1, waiting for transfers between devices, per_device(): lax.all_to_all(partial_back.astype(jnp.bfloat16), 'dp', split_axis=0, con...  45.3 us
    dot_general x1, matrix products, per_device(): jnp.einsum('gscf,sgcd->fd', rows_all, got_cot, preferred_element_type=jnp...  25.1 us
    all_to_all x1, waiting for transfers between devices, per_device(): lax.all_to_all(send_hidden, 'expert', split_axis=0, concat_axis=0, tiled=...  24.9 us
    all_to_all x1, waiting for transfers between devices, per_device(): lax.all_to_all(grad_hidden_rows, 'expert', split_axis=0, concat_axis=0, t...  24.5 us
    all_gather x1, blocking collectives, per_device(): lax.all_gather(routes.reshape(slot_count), 'dp', axis=0, tiled=False)  23.3 us
    dot_general x4, matrix products, per_device(): jnp.einsum('scd,fd->scf', got_cot[:, g], matrix, preferred_element_type=j...  15.7 us
    all_to_all x1, blocking collectives, per_device(): lax.all_to_all(grad_gates_rows, 'expert', split_axis=0, concat_axis=0, ti...  15.3 us
  transfers between devices with their start and end apart: 7, of which 4 were waited for; matrix products, arithmetic and copies ran while one was open for 10% of the time, Pallas kernels for 0%

profile of v6, /device:TPU:1, one launch (start us, length us, event | category | flops | bytes accessed | tf_op | source)
XLA Modules:
  0.0 441.8 jit_solution(6574943071834621323)
XLA Ops:
  7.2 2.9 copy.95
  10.0 5.1 %all-to-all-start.1 = ((bf16[4,128,1792]{2,1,0:T(8,128)(2,1)}), bf16[4,128,1792]{2,1,0:T(8,128)(2,1)S(1)}, u32[]{:S(2)}, u32[]{:S(2)}) async-start(bf16[4,128,1792]{2,1,0:T(8,128)(2,1)} %bitcast.156), calls=%async_computation.1 | async-start | bytes 3670016 | tf_op jit(solution)/shard_map/all_to_all | solution.py:36
  15.2 0.1 copy.51
  15.3 0.1 reshape.181
  15.4 23.3 %all-gather.1 = s32[4,1,256]{2,1,0:T(1,128)S(1)} all-gather(s32[1,1,256]{2,1,0:T(1,128)S(1)} %reshape.181), channel_id=1, replica_groups=mesh['dp'=4,'expert'=64] {'dp'}, dimensions={0}, use_global_device_ids=true | all-gather | bytes 5120 | tf_op jit(solution)/shard_map/all_gather | solution.py:31
  38.7 2.4 reduce-window.16
  41.1 0.1 slice.43
  41.3 0.1 copy.58
  41.4 0.2 fusion.43
  41.6 0.1 multiply_reduce_fusion
  41.7 0.1 and_reduce_fusion
  41.8 4.3 scatter_custom_fusion.1
  46.2 0.1 reshape.111
  46.3 0.1 compare_select_fusion
  46.4 0.1 copy.61
  46.5 0.2 reshape.132
  46.6 0.0 all-to-all-done.1
  46.7 10.7 %gather_fusion.1 = bf16[2048,1792]{1,0:T(8,128)(2,1)} fusion(bf16[512,1792]{1,0:T(8,128)(2,1)S(1)} %bitcast.153, s32[2048]{0:T(1024)S(1)} %broadcast_clamp_fusion), kind=kCustom, calls=%fused_computation.1 | custom fusion | bytes 14688256 | tf_op jit(solution)/shard_map/gather | solution.py:40
  57.3 14.9 %all-to-all-start.2 = ((bf16[64,4,8,1792]{3,2,1,0:T(8,128)(2,1)}), bf16[64,4,8,1792]{3,2,1,0:T(8,128)(2,1)}, u32[]{:S(2)}, u32[]{:S(2)}) async-start(bf16[64,4,8,1792]{3,2,1,0:T(8,128)(2,1)} %bitcast.154), calls=%async_computation.2 | async-start | bytes 14680064 | tf_op jit(solution)/shard_map/all_to_all | solution.py:41
  72.2 0.1 eq.48
  72.3 0.1 eq.52
  72.5 0.1 copy.50
  72.6 0.1 mul.56
  72.8 0.6 reduce-window.14
  73.4 0.2 slice_reduce_fusion
  73.6 0.1 copy.54
  73.7 0.1 reshape.107
  73.9 0.1 fusion.47
  74.0 1.4 scatter_custom_fusion
  75.4 3.5 gather_fusion
  79.0 0.7 all_to_all.27
  79.7 155.8 %all-to-all-done.2 = bf16[64,4,8,1792]{3,2,1,0:T(8,128)(2,1)} async-done(((bf16[64,4,8,1792]{3,2,1,0:T(8,128)(2,1)}), bf16[64,4,8,1792]{3,2,1,0:T(8,128)(2,1)}, u32[]{:S(2)}, u32[]{:S(2)}) %all-to-all-start.2) | async-done | bytes 7340064 | tf_op jit(solution)/shard_map/all_to_all | solution.py:41
  235.5 5.8 %all-to-all-start = ((f32[64,1,8]{2,1,0:T(1,128)}), f32[64,1,8]{2,1,0:T(1,128)S(1)}, u32[]{:S(2)}, u32[]{:S(2)}) async-start(f32[64,1,8]{2,1,0:T(1,128)} %bitcast.3), calls=%async_computation | async-start | bytes 65536 | tf_op jit(solution)/shard_map/all_to_all | solution.py:51
  241.3 0.0 copy-start.5
  241.3 4.8 %fusion.29 = bf16[1,64,8,1024]{3,2,1,0:T(8,128)(2,1)S(1)} fusion(bf16[1,1024,1792]{2,1,0:T(8,128)(2,1)} %param.9, bf16[64,4,8,1792]{3,2,1,0:T(8,128)(2,1)} %all-to-all-done.2), kind=kOutput, calls=%fused_computation.35 | convolution fusion | flops 1879572480 | bytes 6553600 | tf_op jit(solution)/shard_map/scd,fd->scf/dot_general | solution.py:58
  246.2 3.6 fusion.32
  249.8 3.6 fusion.35
  253.4 3.6 fusion.38
  257.1 2.3 pad_maximum_fusion
  259.4 5.0 %all-to-all-start.3 = ((bf16[4,64,8,1024]{3,2,1,0:T(8,128)(2,1)}), bf16[4,64,8,1024]{3,2,1,0:T(8,128)(2,1)}, u32[]{:S(2)}, u32[]{:S(2)}) async-start(bf16[4,64,8,1024]{3,2,1,0:T(8,128)(2,1)} %pad_maximum_fusion), calls=%async_computation.3 | async-start | bytes 8388608 | tf_op jit(solution)/shard_map/all_to_all | solution.py:62
  264.4 0.2 reshape.114
  264.6 2.8 gather_fusion.3
  267.4 45.3 %all-to-all-done.3 = bf16[4,64,8,1024]{3,2,1,0:T(8,128)(2,1)} async-done(((bf16[4,64,8,1024]{3,2,1,0:T(8,128)(2,1)}), bf16[4,64,8,1024]{3,2,1,0:T(8,128)(2,1)}, u32[]{:S(2)}, u32[]{:S(2)}) %all-to-all-start.3) | async-done | bytes 4194336 | tf_op jit(solution)/shard_map/all_to_all | solution.py:62
  312.7 11.4 %all-to-all-start.5 = ((bf16[64,8,1024]{2,1,0:T(8,128)(2,1)}), bf16[64,8,1024]{2,1,0:T(8,128)(2,1)S(1)}, u32[]{:S(2)}, u32[]{:S(2)}) async-start(bf16[64,8,1024]{2,1,0:T(8,128)(2,1)} %bitcast.24), calls=%async_computation.5 | async-start | bytes 2097152 | tf_op jit(solution)/shard_map/all_to_all | solution.py:50
  324.1 0.3 all-gather.4.cloned.1.call-start
  324.4 3.3 convert_reduce_fusion
  327.7 24.9 %all-to-all-done.5 = bf16[64,8,1024]{2,1,0:T(8,128)(2,1)S(1)} async-done(((bf16[64,8,1024]{2,1,0:T(8,128)(2,1)}), bf16[64,8,1024]{2,1,0:T(8,128)(2,1)S(1)}, u32[]{:S(2)}, u32[]{:S(2)}) %all-to-all-start.5) | async-done | bytes 1048608 | tf_op jit(solution)/shard_map/all_to_all | solution.py:50
  352.7 1.8 fusion.15
  354.4 0.0 all-gather.4.cloned.1.call-update
  354.4 0.1 copy.73
  354.5 0.1 copy.67
  354.6 15.3 %all_to_all.43 = f32[64,1,8]{2,1,0:T(1,128)S(1)} all-to-all(f32[64,1,8]{2,1,0:T(1,128)S(1)} %copy.67), channel_id=1, replica_groups=mesh['dp'=4,'expert'=64] {'expert'}, dimensions={0} | all-to-all | bytes 4096 | tf_op jit(solution)/shard_map/all_to_all | solution.py:74
  369.9 4.8 %all-to-all-start.4 = ((bf16[64,8,1024]{2,1,0:T(8,128)(2,1)}), bf16[64,8,1024]{2,1,0:T(8,128)(2,1)S(1)}, u32[]{:S(2)}, u32[]{:S(2)}) async-start(bf16[64,8,1024]{2,1,0:T(8,128)(2,1)} %get-tuple-element.13), calls=%async_computation.4 | async-start | bytes 2097152 | tf_op jit(solution)/shard_map/all_to_all | solution.py:71
  374.7 0.5 broadcast.133
  375.2 0.7 reduce.9
  375.9 0.1 reshape.116
  376.0 1.9 gather_fusion.4
  378.0 0.1 reshape.117
  378.1 0.6 copy.70
  378.8 24.5 %all-to-all-done.4 = bf16[64,8,1024]{2,1,0:T(8,128)(2,1)S(1)} async-done(((bf16[64,8,1024]{2,1,0:T(8,128)(2,1)}), bf16[64,8,1024]{2,1,0:T(8,128)(2,1)S(1)}, u32[]{:S(2)}, u32[]{:S(2)}) %all-to-all-start.4) | async-done | bytes 1048608 | tf_op jit(solution)/shard_map/all_to_all | solution.py:71
  403.2 1.2 gather_fusion.2
  404.4 1.0 reshape.113
  405.4 4.5 %copy.68 = bf16[256,8,1024]{2,0,1:T(8,128)(2,1)S(1)} copy(bf16[256,8,1024]{2,1,0:T(8,128)(2,1)} %all-gather.4.cloned.1.call-done) | data formatting | bytes 8388608 | tf_op jit(solution)/shard_map/all_gather | solution.py:54
  409.9 25.1 %fusion.12 = bf16[1,1024,1792]{2,1,0:T(8,128)(2,1)} fusion(bf16[4,64,8,1024]{3,1,0,2:T(8,128)(2,1)S(1)} %bitcast.157, bf16[64,4,8,1792]{3,2,1,0:T(8,128)(2,1)} %all-to-all-done.2), kind=kOutput, calls=%fused_computation.20 | convolution fusion | flops 7518027776 | bytes 15204352 | tf_op jit(solution)/shard_map/gscf,sgcd->fd/dot_general | solution.py:66
  (38 shorter events, 0.2 us)
Async XLA Ops:
  7.2 8.0 %copy-start.1 = (s32[128,2]{0,1:T(2,128)S(1)}, s32[128,2]{0,1:T(2,128)}, u32[]{:S(2)}) copy-start(s32[128,2]{0,1:T(2,128)} %param.6) | copy-start | bytes 3076
  10.0 31.6 %copy-start.4 = (s32[2]{0:T(128)S(1)}, s32[2]{0:T(128)}, u32[]{:S(2)}) copy-start(s32[2]{0:T(128)} %constant.50) | copy-start | bytes 28
  10.0 31.7 %copy-start.3 = (s32[2]{0:T(128)S(1)}, s32[2]{0:T(128)}, u32[]{:S(2)}) copy-start(s32[2]{0:T(128)} %constant.53) | copy-start | bytes 28
  10.0 36.6 %all-to-all-start.1 = ((bf16[4,128,1792]{2,1,0:T(8,128)(2,1)}), bf16[4,128,1792]{2,1,0:T(8,128)(2,1)S(1)}, u32[]{:S(2)}, u32[]{:S(2)}) async-start(bf16[4,128,1792]{2,1,0:T(8,128)(2,1)} %bitcast.156), calls=%async_computation.1 | async-start | bytes 3670016 | tf_op jit(solution)/shard_map/all_to_all | solution.py:36
  57.3 16.3 %copy-start.2 = (f32[128,2]{0,1:T(2,128)S(1)}, f32[128,2]{0,1:T(2,128)}, u32[]{:S(2)}) copy-start(f32[128,2]{0,1:T(2,128)} %param.7) | copy-start | bytes 3076
  57.3 178.2 %all-to-all-start.2 = ((bf16[64,4,8,1792]{3,2,1,0:T(8,128)(2,1)}), bf16[64,4,8,1792]{3,2,1,0:T(8,128)(2,1)}, u32[]{:S(2)}, u32[]{:S(2)}) async-start(bf16[64,4,8,1792]{3,2,1,0:T(8,128)(2,1)} %bitcast.154), calls=%async_computation.2 | async-start | bytes 14680064 | tf_op jit(solution)/shard_map/all_to_all | solution.py:41
  235.5 23.9 %all-to-all-start = ((f32[64,1,8]{2,1,0:T(1,128)}), f32[64,1,8]{2,1,0:T(1,128)S(1)}, u32[]{:S(2)}, u32[]{:S(2)}) async-start(f32[64,1,8]{2,1,0:T(1,128)} %bitcast.3), calls=%async_computation | async-start | bytes 65536 | tf_op jit(solution)/shard_map/all_to_all | solution.py:51
  241.3 4.9 %copy-start.5 = (bf16[1,1024,1792]{2,1,0:T(8,128)(2,1)S(1)}, bf16[1,1024,1792]{2,1,0:T(8,128)(2,1)}, u32[]{:S(2)}) copy-start(bf16[1,1024,1792]{2,1,0:T(8,128)(2,1)} %param.9) | copy-start | bytes 11010052
  259.4 5.0 %copy-start = (bf16[128,2,1024]{2,1,0:T(2,128)(2,1)S(1)}, bf16[128,2,1024]{2,1,0:T(2,128)(2,1)}, u32[]{:S(2)}) copy-start(bf16[128,2,1024]{2,1,0:T(2,128)(2,1)} %param.5) | copy-start | bytes 1572868
  259.4 53.3 %all-to-all-start.3 = ((bf16[4,64,8,1024]{3,2,1,0:T(8,128)(2,1)}), bf16[4,64,8,1024]{3,2,1,0:T(8,128)(2,1)}, u32[]{:S(2)}, u32[]{:S(2)}) async-start(bf16[4,64,8,1024]{3,2,1,0:T(8,128)(2,1)} %pad_maximum_fusion), calls=%async_computation.3 | async-start | bytes 8388608 | tf_op jit(solution)/shard_map/all_to_all | solution.py:62
  312.7 40.0 %all-to-all-start.5 = ((bf16[64,8,1024]{2,1,0:T(8,128)(2,1)}), bf16[64,8,1024]{2,1,0:T(8,128)(2,1)S(1)}, u32[]{:S(2)}, u32[]{:S(2)}) async-start(bf16[64,8,1024]{2,1,0:T(8,128)(2,1)} %bitcast.24), calls=%async_computation.5 | async-start | bytes 2097152 | tf_op jit(solution)/shard_map/all_to_all | solution.py:50
  324.1 81.3 %all-gather.4.cloned.1.call-start = ((), (), s32[]{:S(2)}) async-start(), calls=%async_computation.7 | async-start | bytes 5242880 | tf_op jit(solution)/shard_map/all_gather | solution.py:54
  369.9 33.3 %all-to-all-start.4 = ((bf16[64,8,1024]{2,1,0:T(8,128)(2,1)}), bf16[64,8,1024]{2,1,0:T(8,128)(2,1)S(1)}, u32[]{:S(2)}, u32[]{:S(2)}) async-start(bf16[64,8,1024]{2,1,0:T(8,128)(2,1)} %get-tuple-element.13), calls=%async_computation.4 | async-start | bytes 2097152 | tf_op jit(solution)/shard_map/all_to_all | solution.py:71
Sparse Core Ops, SparseCore 0:
  354.6 45.5 all-gather.3

commit v7 on v4

--- a/solution.py
+++ b/solution.py
@@ -95,14 +95,18 @@
     )
 
     matrix = weight[0]
-    bounds = [0, capacity // 2, capacity]
+    bounds = [0, capacity // 2, capacity * 3 // 4, capacity]
     backs, got_chunks = [], []
     for c in range(len(bounds) - 1):
         step = bounds[c + 1] - bounds[c]
         index = token_of[:, :, bounds[c] : bounds[c + 1]].reshape(columns, groups * step)
         if c == 0:
             index = jnp.concatenate([index, hidden_of], axis=1)
-        got_rows = lax.all_to_all(table[index], "expert", split_axis=0, concat_axis=0, tiled=True)
+        payload = table[index]
+        if c > 0:
+            payload, pending = lax.optimization_barrier((payload, pending))
+            backs.append(lax.psum_scatter(pending, "dp", scatter_dimension=0, tiled=True)[0])
+        got_rows = lax.all_to_all(payload, "expert", split_axis=0, concat_axis=0, tiled=True)
         if c == 0:
             got_hidden = got_rows[:, groups * step :, :hidden_width]
             got_gates = join3(got_rows[:, groups * step :, hidden_width : hidden_width + LANES])
@@ -122,7 +126,8 @@
                 for g in range(groups)
             ]
         )
-        backs.append(lax.psum_scatter(partial_back, "dp", scatter_dimension=0, tiled=True)[0])
+        pending = partial_back
+    backs.append(lax.psum_scatter(pending, "dp", scatter_dimension=0, tiled=True)[0])
     grad_matrix = sum(
         jnp.einsum(
             "gscf,sgcd->fd",

time: 421 us -> 437 us (1.038)
  matrix products: 22.3 us -> 32.1 us
  starting transfers between devices: 22.3 us -> 28 us
    reduce_scatter x2 -> x3, waiting for transfers between devices: 30.9 us -> 12.9 us  [per_device(): lax.psum_scatter(pending, 'dp', scatter_dimension=0, tiled=True)[0]]
    all_to_all x1 -> x2, waiting for transfers between devices: 73.1 us -> 86.1 us  [per_device(): lax.all_to_all(payload, 'expert', split_axis=0, concat_axis=0, tiled=True)]
    dot_general x8 -> x12, matrix products: 9.1 us -> 14.9 us  [per_device(): jnp.einsum('scd,fd->scf', got_cot[:, g], matrix, preferred_element_type=j...]
    all_to_all x1 -> x2, starting transfers between devices: 6.34 us -> 11.7 us  [per_device(): lax.all_to_all(payload, 'expert', split_axis=0, concat_axis=0, tiled=True)]
    dot_general x2 -> x3, matrix products: 13.2 us -> 17.2 us  [per_device(): jnp.einsum('gscf,sgcd->fd', rows_all[:, :, bounds[c]:bounds[c + 1]], got_...]
    unnamed x44 -> x47, local copies, waits for them, and re-layouts: 15 us -> 15.9 us
    gather x2 -> x3, local copies, waits for them, and re-layouts: 12.5 us -> 13 us  [per_device(): payload = table[index]]
  transfers between devices with their start and end apart: 6 -> 8, of which waited for: 4 -> 5; matrix products, arithmetic and copies ran while one was open for 10% -> 13% of each run, Pallas kernels for 0% -> 0%
where the time goes in v7:
time: 437 us; the launch traced here: 436 us
  waiting for transfers between devices  149 us (34%)
  blocking collectives  138 us (32%)
  local copies, waits for them, and re-layouts  54.4 us (12%)
  matrix products  32.1 us (7%)
  starting transfers between devices  28 us (6%)
  other arithmetic  20.1 us (5%)
  between operations  14.4 us (3%)
    all_to_all x1, blocking collectives, per_device(): lax.all_to_all(payload, 'expert', split_axis=0, concat_axis=0, tiled=True)  138 us
    all_to_all x2, waiting for transfers between devices, per_device(): lax.all_to_all(payload, 'expert', split_axis=0, concat_axis=0, tiled=True)  86.1 us
    all_to_all x1, waiting for transfers between devices, per_device(): lax.all_to_all(jnp.concatenate([grad_hidden_rows, split3(grad_gates_rows)...  31.3 us
    all_to_all x1, waiting for transfers between devices, per_device(): lax.all_to_all(cot_split, 'dp', split_axis=0, concat_axis=0, tiled=True)  17.8 us
    dot_general x3, matrix products, per_device(): jnp.einsum('gscf,sgcd->fd', rows_all[:, :, bounds[c]:bounds[c + 1]], got_...  17.2 us
    unnamed x47, local copies, waits for them, and re-layouts  15.9 us
    dot_general x12, matrix products, per_device(): jnp.einsum('scd,fd->scf', got_cot[:, g], matrix, preferred_element_type=j...  14.9 us
    gather x3, local copies, waits for them, and re-layouts, per_device(): payload = table[index]  13 us
  transfers between devices with their start and end apart: 8, of which 5 were waited for; matrix products, arithmetic and copies ran while one was open for 13% of the time, Pallas kernels for 0%

profile of v7, /device:TPU:1, one launch (start us, length us, event | category | flops | bytes accessed | tf_op | source)
XLA Modules:
  0.0 436.1 jit_solution(3693281850836192245)
XLA Ops:
  7.2 0.6 compare_reduce_fusion
  7.8 3.3 copy.126
  11.1 2.5 copy.128
  13.6 0.6 broadcast_select_fusion.1
  14.5 3.0 pad_maximum_fusion.4
  17.5 5.0 %all-to-all-start = ((bf16[4,128,1920]{2,1,0:T(8,128)(2,1)}), bf16[4,128,1920]{2,1,0:T(8,128)(2,1)S(1)}, u32[]{:S(2)}, u32[]{:S(2)}) async-start(bf16[4,128,1920]{2,1,0:T(8,128)(2,1)} %pad_maximum_fusion.4), calls=%async_computation | async-start | bytes 3932160 | tf_op jit(solution)/shard_map/all_to_all | solution.py:63
  23.0 0.6 reduce-window.16
  24.2 1.4 scatter_custom_fusion
  26.8 1.1 concatenate.44
  27.9 17.8 %all-to-all-done = bf16[4,128,1920]{2,1,0:T(8,128)(2,1)S(1)} async-done(((bf16[4,128,1920]{2,1,0:T(8,128)(2,1)}), bf16[4,128,1920]{2,1,0:T(8,128)(2,1)S(1)}, u32[]{:S(2)}, u32[]{:S(2)}) %all-to-all-start) | async-done | bytes 1966112 | tf_op jit(solution)/shard_map/all_to_all | solution.py:63
  46.2 2.4 reduce-window.14
  50.0 4.3 scatter_custom_fusion.1
  55.0 1.7 maximum_maximum_fusion
  56.7 6.7 %gather_fusion = bf16[1536,1792]{1,0:T(8,128)(2,1)} fusion(bf16[776,1792]{1,0:T(8,128)(2,1)S(1)} %maximum_maximum_fusion, s32[2048]{0:T(1024)S(1)} %pad_clamp_fusion), kind=kCustom, calls=%fused_computation | custom fusion | bytes 11016192 | tf_op jit(solution)/shard_map/gather | solution.py:105
  63.4 138.1 %all_to_all.25 = bf16[64,24,1792]{2,1,0:T(8,128)(2,1)S(1)} all-to-all(bf16[64,24,1792]{2,1,0:T(8,128)(2,1)} %bitcast.221), channel_id=1, replica_groups=mesh['dp'=4,'expert'=64] {'expert'}, dimensions={0} | all-to-all | bytes 11010048 | tf_op jit(solution)/shard_map/all_to_all | solution.py:109
  201.6 2.4 copy-done.3
  204.1 1.3 slice.180
  205.4 1.0 copy-done.4
  206.4 1.7 fusion.25
  208.8 3.2 gather_fusion.1
  212.0 2.0 slice-done
  214.0 1.1 copy.157
  215.1 1.9 copy-done
  217.0 1.1 fusion.31
  218.1 1.1 fusion.34
  219.3 1.1 fusion.37
  220.4 1.1 fusion.40
  221.6 2.6 pad_maximum_fusion
  224.2 5.6 %all-to-all-start.2 = ((bf16[64,8,1792]{2,1,0:T(8,128)(2,1)}), bf16[64,8,1792]{2,1,0:T(8,128)(2,1)}, u32[]{:S(2)}, u32[]{:S(2)}) async-start(bf16[64,8,1792]{2,1,0:T(8,128)(2,1)} %bitcast.234), calls=%async_computation.2 | async-start | bytes 3670016 | tf_op jit(solution)/shard_map/all_to_all | solution.py:109
  230.1 3.2 gather_fusion.2
  233.3 41.8 %all-to-all-done.2 = bf16[64,8,1792]{2,1,0:T(8,128)(2,1)} async-done(((bf16[64,8,1792]{2,1,0:T(8,128)(2,1)}), bf16[64,8,1792]{2,1,0:T(8,128)(2,1)}, u32[]{:S(2)}, u32[]{:S(2)}) %all-to-all-start.2) | async-done | bytes 1835040 | tf_op jit(solution)/shard_map/all_to_all | solution.py:109
  275.1 2.0 copy.159
  277.1 0.6 copy-done.1
  277.7 1.3 fusion.43
  279.0 1.3 fusion.46
  280.3 1.3 fusion.49
  281.7 1.3 fusion.52
  283.0 1.4 pad_maximum_fusion.1
  284.4 6.1 %all-to-all-start.3 = ((bf16[64,8,1792]{2,1,0:T(8,128)(2,1)}), bf16[64,8,1792]{2,1,0:T(8,128)(2,1)}, u32[]{:S(2)}, u32[]{:S(2)}) async-start(bf16[64,8,1792]{2,1,0:T(8,128)(2,1)} %bitcast.235), calls=%async_computation.3 | async-start | bytes 3670016 | tf_op jit(solution)/shard_map/all_to_all | solution.py:109
  290.6 0.7 reduce-scatter.6.cloned.1.call-update
  291.3 0.3 reduce-scatter.8.cloned.1.call-start
  291.6 44.3 %all-to-all-done.3 = bf16[64,8,1792]{2,1,0:T(8,128)(2,1)} async-done(((bf16[64,8,1792]{2,1,0:T(8,128)(2,1)}), bf16[64,8,1792]{2,1,0:T(8,128)(2,1)}, u32[]{:S(2)}, u32[]{:S(2)}) %all-to-all-start.3) | async-done | bytes 1835040 | tf_op jit(solution)/shard_map/all_to_all | solution.py:109
  335.9 2.0 copy.163
  337.9 0.7 copy-done.2
  338.5 1.3 fusion.55
  339.8 1.3 fusion.58
  341.1 1.3 fusion.61
  342.4 1.3 fusion.64
  343.7 1.4 pad_maximum_fusion.2
  345.2 3.5 fusion.29
  348.8 5.1 %fusion.27 = f32[1024,1792,1,1]{1,0,3,2:T(8,128)} fusion(bf16[4,64,8,1024]{3,1,0,2:T(8,128)(2,1)S(1)} %bitcast.259, bf16[64,4,2,1792]{3,0,2,1:T(8,128)(2,1)S(1)} %bitcast.231), kind=kOutput, calls=%fused_computation.46 | convolution fusion | flops 1879048192 | bytes 13369344 | tf_op jit(solution)/shard_map/gscf,sgcd->fd/dot_general | solution.py:132
  353.9 8.6 %bitcast_add_fusion = bf16[1024,1792]{1,0:T(8,128)(2,1)} fusion(f32[1024,1792,1,1]{1,0,3,2:T(8,128)} %fusion.27, f32[1024,1792,1,1]{1,0,3,2:T(8,128)S(1)} %fusion.29, bf16[4,64,8,1024]{3,1,0,2:T(8,128)(2,1)S(1)} %bitcast.260, bf16[64,4,4,1792]{3,0,2,1:T(8,128)(2,1)S(1)} %bitcast.240), kind=kOutput, calls=%fused_computation.7 | convolution fusion | flops 3763601408 | bytes 26214400 | tf_op jit(solution)/shard_map/gscf,sgcd->fd/dot_general | solution.py:132
  362.5 12.9 %reduce-scatter.8.cloned.1.call-done = f32[1,64,2,1024]{3,1,2,0:T(8,128)} async-done(((f32[4,64,2,1024]{3,1,2,0:T(8,128)}), f32[1,64,2,1024]{3,1,2,0:T(8,128)}) %reduce-scatter.8.cloned.1.call-update) | async-done | bytes 524304 | tf_op jit(solution)/shard_map/reduce_scatter | solution.py:130
  375.4 1.7 pad_maximum_fusion.3
  377.1 1.2 fusion.26
  378.8 1.6 concatenate.50
  380.4 1.7 copy.168
  382.0 10.7 %all-to-all-start.4 = ((bf16[64,8,1152]{2,1,0:T(8,128)(2,1)}), bf16[64,8,1152]{2,1,0:T(8,128)(2,1)S(1)}, u32[]{:S(2)}, u32[]{:S(2)}) async-start(bf16[64,8,1152]{2,1,0:T(8,128)(2,1)} %copy.168), calls=%async_computation.7 | async-start | bytes 2359296 | tf_op jit(solution)/shard_map/all_to_all | solution.py:144
  392.8 31.3 %all-to-all-done.4 = bf16[64,8,1152]{2,1,0:T(8,128)(2,1)S(1)} async-done(((bf16[64,8,1152]{2,1,0:T(8,128)(2,1)}), bf16[64,8,1152]{2,1,0:T(8,128)(2,1)S(1)}, u32[]{:S(2)}, u32[]{:S(2)}) %all-to-all-start.4) | async-done | bytes 1179680 | tf_op jit(solution)/shard_map/all_to_all | solution.py:144
  424.3 1.2 gather_fusion.3
  425.4 1.0 reshape.415
  426.4 0.3 fusion.70
  426.8 1.9 gather_fusion.4
  428.9 0.6 copy.169
  (129 shorter events, 6.8 us)
Async XLA Ops:
  7.8 5.8 %copy-start.11 = (s32[128,2]{0,1:T(2,128)S(1)}, s32[128,2]{0,1:T(2,128)}, u32[]{:S(2)}) copy-start(s32[128,2]{0,1:T(2,128)} %param.8) | copy-start | bytes 3076
  14.4 11.3 %copy-start.12 = (f32[128,2]{0,1:T(2,128)S(1)}, f32[128,2]{0,1:T(2,128)}, u32[]{:S(2)}) copy-start(f32[128,2]{0,1:T(2,128)} %param.9) | copy-start | bytes 3076
  14.5 12.0 %copy-start.10 = (bf16[128,2,1024]{2,1,0:T(2,128)(2,1)S(1)}, bf16[128,2,1024]{2,1,0:T(2,128)(2,1)}, u32[]{:S(2)}) copy-start(bf16[128,2,1024]{2,1,0:T(2,128)(2,1)} %param.7) | copy-start | bytes 1572868
  17.5 28.3 %all-to-all-start = ((bf16[4,128,1920]{2,1,0:T(8,128)(2,1)}), bf16[4,128,1920]{2,1,0:T(8,128)(2,1)S(1)}, u32[]{:S(2)}, u32[]{:S(2)}) async-start(bf16[4,128,1920]{2,1,0:T(8,128)(2,1)} %pad_maximum_fusion.4), calls=%async_computation | async-start | bytes 3932160 | tf_op jit(solution)/shard_map/all_to_all | solution.py:63
  22.5 252.6 %all-gather.3.cloned.1.call-start = ((), (), s32[]{:S(2)}) async-start(), calls=%async_computation.11 | async-start | bytes 5242880 | tf_op jit(solution)/shard_map/all_gather | solution.py:116
  22.9 26.5 %copy-start.14 = (s32[2]{0:T(128)S(1)}, s32[2]{0:T(128)}, u32[]{:S(2)}) copy-start(s32[2]{0:T(128)} %constant.89) | copy-start | bytes 28
  23.6 26.1 %copy-start.13 = (s32[2]{0:T(128)S(1)}, s32[2]{0:T(128)}, u32[]{:S(2)}) copy-start(s32[2]{0:T(128)} %constant.92) | copy-start | bytes 28
  201.6 2.4 copy-start.3
  205.4 1.0 copy-start.4
  208.1 154.3 %reduce-scatter.4.cloned.1.call-start = ((), (), s32[]{:S(2)}) async-start(), calls=%async_computation.8 | async-start | bytes 5242880 | tf_op jit(solution)/shard_map/reduce_scatter | solution.py:108
  212.0 2.0 slice-start
  214.0 3.0 copy-start
  215.1 5.3 %copy-start.8 = (bf16[64,16,1792]{2,0,1:T(8,128)(2,1)}, bf16[64,16,1792]{2,0,1:T(8,128)(2,1)S(1)}, u32[]{:S(2)}) copy-start(bf16[64,16,1792]{2,0,1:T(8,128)(2,1)S(1)} %copy.157) | copy-start | bytes 11010052
  224.2 50.9 %all-to-all-start.2 = ((bf16[64,8,1792]{2,1,0:T(8,128)(2,1)}), bf16[64,8,1792]{2,1,0:T(8,128)(2,1)}, u32[]{:S(2)}, u32[]{:S(2)}) async-start(bf16[64,8,1792]{2,1,0:T(8,128)(2,1)} %bitcast.234), calls=%async_computation.2 | async-start | bytes 3670016 | tf_op jit(solution)/shard_map/all_to_all | solution.py:109
  275.1 2.6 copy-start.1
  284.4 51.5 %all-to-all-start.3 = ((bf16[64,8,1792]{2,1,0:T(8,128)(2,1)}), bf16[64,8,1792]{2,1,0:T(8,128)(2,1)}, u32[]{:S(2)}, u32[]{:S(2)}) async-start(bf16[64,8,1792]{2,1,0:T(8,128)(2,1)} %bitcast.235), calls=%async_computation.3 | async-start | bytes 3670016 | tf_op jit(solution)/shard_map/all_to_all | solution.py:109
  290.6 71.9 %reduce-scatter.6.cloned.1.call-start = ((), (), s32[]{:S(2)}) async-start(), calls=%async_computation.9 | async-start | bytes 2621440 | tf_op jit(solution)/shard_map/reduce_scatter | solution.py:108
  291.3 84.1 %reduce-scatter.8.cloned.1.call-start = ((), (), s32[]{:S(2)}) async-start(), calls=%async_computation.10 | async-start | bytes 2621440 | tf_op jit(solution)/shard_map/reduce_scatter | solution.py:130
  335.9 2.7 copy-start.2
  337.9 4.6 %copy-start.6 = (bf16[64,8,1792]{2,0,1:T(8,128)(2,1)}, bf16[64,8,1792]{2,0,1:T(8,128)(2,1)S(1)}, u32[]{:S(2)}) copy-start(bf16[64,8,1792]{2,0,1:T(8,128)(2,1)S(1)} %copy.163) | copy-start | bytes 5505028
  345.2 3.5 copy-start.7
  345.2 3.5 copy-start.15
  348.7 5.1 %copy-start.9 = (bf16[64,16,1792]{2,0,1:T(8,128)(2,1)S(1)}, bf16[64,16,1792]{2,0,1:T(8,128)(2,1)}, u32[]{:S(2)}) copy-start(bf16[64,16,1792]{2,0,1:T(8,128)(2,1)} %copy-done.8) | copy-start | bytes 11010052
  362.5 14.6 %copy-start.5 = (bf16[64,8,1024]{2,1,0:T(8,128)(2,1)S(1)}, bf16[64,8,1024]{2,1,0:T(8,128)(2,1)}, u32[]{:S(2)}) copy-start(bf16[64,8,1024]{2,1,0:T(8,128)(2,1)} %copy-done.4) | copy-start | bytes 3145732
  382.0 42.1 %all-to-all-start.4 = ((bf16[64,8,1152]{2,1,0:T(8,128)(2,1)}), bf16[64,8,1152]{2,1,0:T(8,128)(2,1)S(1)}, u32[]{:S(2)}, u32[]{:S(2)}) async-start(bf16[64,8,1152]{2,1,0:T(8,128)(2,1)} %copy.168), calls=%async_computation.7 | async-start | bytes 2359296 | tf_op jit(solution)/shard_map/all_to_all | solution.py:144
Sparse Core Ops, SparseCore 0:
  208.3 45.5 all-gather.2
  256.4 49.8 reduce-scatter.3
  308.9 32.0 reduce-scatter.5
  345.3 30.0 reduce-scatter.7

commit v8 on v2

--- a/solution.py
+++ b/solution.py
@@ -89,7 +89,13 @@
     got_gates = join3(got[:, :, hidden_width:])
 
     scaled = (got_gates[:, :, None] * got_hidden.astype(jnp.float32)).astype(jnp.bfloat16)
-    rows_all = lax.all_gather(scaled, "dp", axis=0, tiled=False)
+    rows_all = lax.all_to_all(
+        jnp.broadcast_to(scaled[None], (groups,) + scaled.shape),
+        "dp",
+        split_axis=0,
+        concat_axis=0,
+        tiled=True,
+    )
     matrix = weight[0]
     partial_back = jnp.stack(
         [
@@ -98,13 +104,16 @@
         ]
     )
     back = lax.psum_scatter(partial_back, "dp", scatter_dimension=0, tiled=True)[0]
+    _, back = lax.optimization_barrier((rows_all, back))
     grad_matrix = jnp.einsum(
         "gscf,sgcd->fd", rows_all, got_cot, preferred_element_type=jnp.float32
     )
     grad_hidden_rows = (got_gates[:, :, None] * back).astype(jnp.bfloat16)
     grad_gates_rows = jnp.sum(got_hidden.astype(jnp.float32) * back, axis=2)
+    payload = jnp.concatenate([grad_hidden_rows, split3(grad_gates_rows)], axis=2)
+    grad_matrix, payload = lax.optimization_barrier((grad_matrix, payload))
     returned = lax.all_to_all(
-        jnp.concatenate([grad_hidden_rows, split3(grad_gates_rows)], axis=2),
+        payload,
         "expert",
         split_axis=0,
         concat_axis=0,

time: 409 us -> 496 us (1.21)
  blocking collectives: 215 us -> 296 us
  waiting for transfers between devices: 82 us -> 54.6 us
  local copies, waits for them, and re-layouts: 44.4 us -> 66.1 us
  matrix products: 21.5 us -> 33.1 us
    all_to_all x0 -> x1, blocking collectives: none -> 70 us  [per_device(): lax.all_to_all(jnp.broadcast_to(scaled[None], (groups,) + scaled.shape),...]
    reduce_scatter x1, waiting for transfers between devices: 27.1 us -> 0.01 us  [per_device(): lax.psum_scatter(partial_back, 'dp', scatter_dimension=0, tiled=True)[0]]
    dot_general x1, matrix products: 13.1 us -> 24.7 us  [per_device(): jnp.einsum('gscf,sgcd->fd', rows_all, got_cot, preferred_element_type=jnp...]
    all_to_all x1, blocking collectives: 178 us -> 188 us  [per_device(): lax.all_to_all(send_cot, 'expert', split_axis=0, concat_axis=0, tiled=True)]
    slice x0 -> x1, local copies, waits for them, and re-layouts: none -> 10.7 us  [per_device(): got_cot[:, g]]
    gather x1 -> x2, local copies, waits for them, and re-layouts: 10.7 us -> 20.6 us  [per_device(): send_cot = cot_q.reshape(groups * local_tokens, quarter)[flat_token]]
  transfers between devices with their start and end apart: 4 -> 3, of which waited for: 4 -> 2; matrix products, arithmetic and copies ran while one was open for 5% -> 8% of each run, Pallas kernels for 0% -> 0%
where the time goes in v8:
time: 496 us; the launch traced here: 495 us
  blocking collectives  296 us (60%)
  local copies, waits for them, and re-layouts  66.1 us (13%)
  waiting for transfers between devices  54.6 us (11%)
  matrix products  33.1 us (7%)
  starting transfers between devices  15.8 us (3%)
  between operations  15 us (3%)
  other arithmetic  14.4 us (3%)
    all_to_all x1, blocking collectives, per_device(): lax.all_to_all(send_cot, 'expert', split_axis=0, concat_axis=0, tiled=True)  188 us
    all_to_all x1, blocking collectives, per_device(): lax.all_to_all(jnp.broadcast_to(scaled[None], (groups,) + scaled.shape),...  70 us
    all_to_all x1, blocking collectives, per_device(): lax.all_to_all(jnp.concatenate([send_hidden, split3(send_gates)], axis=2)...  37.3 us
    all_to_all x1, waiting for transfers between devices, per_device(): lax.all_to_all(payload, 'expert', split_axis=0, concat_axis=0, tiled=True)  31.3 us
    dot_general x1, matrix products, per_device(): jnp.einsum('gscf,sgcd->fd', rows_all, got_cot, preferred_element_type=jnp...  24.7 us
    all_to_all x1, waiting for transfers between devices, per_device(): lax.all_to_all(cot_split, 'dp', split_axis=0, concat_axis=0, tiled=True)  23.2 us
    gather x2, local copies, waits for them, and re-layouts, per_device(): send_cot = cot_q.reshape(groups * local_tokens, quarter)[flat_token]  20.6 us
    slice x1, local copies, waits for them, and re-layouts, per_device(): got_cot[:, g]  10.7 us
  transfers between devices with their start and end apart: 3, of which 2 were waited for; matrix products, arithmetic and copies ran while one was open for 8% of the time, Pallas kernels for 0%

profile of v8, /device:TPU:1, one launch (start us, length us, event | category | flops | bytes accessed | tf_op | source)
XLA Modules:
  0.0 494.6 jit_solution(12468951348717367600)
XLA Ops:
  7.2 0.6 compare_reduce_fusion
  7.8 3.3 copy.126
  11.1 2.5 copy.128
  13.6 0.6 broadcast_select_fusion.1
  14.3 0.1 copy.164
  14.4 3.0 pad_maximum_fusion.1
  17.4 5.1 %all-to-all-start.2 = ((bf16[4,128,1920]{2,1,0:T(8,128)(2,1)}), bf16[4,128,1920]{2,1,0:T(8,128)(2,1)S(1)}, u32[]{:S(2)}, u32[]{:S(2)}) async-start(bf16[4,128,1920]{2,1,0:T(8,128)(2,1)} %pad_maximum_fusion.1), calls=%async_computation.2 | async-start | bytes 3932160 | tf_op jit(solution)/shard_map/all_to_all | solution.py:62
  22.6 23.2 %all-to-all-done.2 = bf16[4,128,1920]{2,1,0:T(8,128)(2,1)S(1)} async-done(((bf16[4,128,1920]{2,1,0:T(8,128)(2,1)}), bf16[4,128,1920]{2,1,0:T(8,128)(2,1)S(1)}, u32[]{:S(2)}, u32[]{:S(2)}) %all-to-all-start.2) | async-done | bytes 1966112 | tf_op jit(solution)/shard_map/all_to_all | solution.py:62
  46.0 0.2 copy.131
  46.3 2.4 reduce-window.16
  48.7 0.1 slice.118
  48.8 0.1 copy.135
  49.0 0.2 copy.130
  49.3 0.2 fusion.30
  49.6 0.1 copy.158
  49.8 0.2 copy.157
  50.1 4.3 scatter_custom_fusion.1
  54.8 0.2 reshape.285
  54.9 1.6 slice.116
  56.6 10.6 %gather_fusion.2 = bf16[2048,1792]{1,0:T(8,128)(2,1)} fusion(bf16[512,1792]{1,0:T(8,128)(2,1)S(1)} %bitcast.128, s32[2048]{0:T(1024)S(1)} %broadcast_clamp_fusion), kind=kCustom, calls=%fused_computation.2 | custom fusion | bytes 14688256 | tf_op jit(solution)/shard_map/gather | solution.py:71
  67.2 9.9 %copy.143 = bf16[64,4,8,1792]{3,1,2,0:T(4,128)(2,1)} copy(bf16[64,4,8,1792]{3,2,1,0:T(8,128)(2,1)} %bitcast.131) | data formatting | bytes 14680064 | tf_op jit(solution)/shard_map/gather | solution.py:71
  77.1 188.4 %all_to_all.25 = bf16[64,4,8,1792]{3,1,2,0:T(4,128)(2,1)S(1)} all-to-all(bf16[64,4,8,1792]{3,1,2,0:T(4,128)(2,1)} %copy.143), channel_id=1, replica_groups=mesh['dp'=4,'expert'=64] {'expert'}, dimensions={0} | all-to-all | bytes 14680064 | tf_op jit(solution)/shard_map/all_to_all | solution.py:72
  265.5 10.7 %fusion.50 = (bf16[64,1,8,1792]{3,1,2,0:T(2,128)(2,1)S(1)}, bf16[64,1,8,1792]{3,1,2,0:T(2,128)(2,1)S(1)}, bf16[64,1,8,1792]{3,1,2,0:T(2,128)(2,1)S(1)}, bf16[64,1,8,1792]{3,1,2,0:T(2,128)(2,1)S(1)}) fusion(bf16[64,4,8,1792]{3,1,2,0:T(4,128)(2,1)S(1)} %all_to_all.25), kind=kLoop, calls=%fused_computation.105 | loop fusion | bytes 14680064 | tf_op jit(solution)/shard_map/slice | solution.py:102
  276.2 2.1 fusion.16
  278.3 2.1 fusion.19
  280.4 2.1 fusion.22
  282.5 2.1 fusion.25
  284.6 3.6 pad_maximum_fusion
  288.4 0.1 eq.54
  288.5 0.1 eq.50
  288.7 0.6 reduce-window.14
  289.3 0.2 slice_reduce_fusion
  289.6 0.1 mul.66
  289.9 0.1 reshape.254
  290.2 1.4 scatter_custom_fusion
  291.6 3.5 gather_fusion.1
  295.3 0.2 copy.120
  295.5 0.8 copy.121
  296.3 0.8 copy.122
  297.1 0.2 reshape.251
  297.4 2.1 gather_fusion
  299.5 1.6 concatenate.11
  301.1 37.3 %all_to_all.26 = bf16[64,8,1152]{2,1,0:T(8,128)(2,1)S(1)} all-to-all(bf16[64,8,1152]{2,1,0:T(8,128)(2,1)S(1)} %concatenate.11), channel_id=1, replica_groups=mesh['dp'=4,'expert'=64] {'expert'}, dimensions={0} | all-to-all | bytes 2359296 | tf_op jit(solution)/shard_map/all_to_all | solution.py:81
  338.4 0.2 slice_add_fusion.2
  338.6 0.4 copy.156
  339.1 0.3 fusion.14
  339.3 0.6 copy.125
  339.9 0.5 broadcast_in_dim.22
  340.5 70.0 %all_to_all.27 = bf16[4,64,8,1024]{3,1,2,0:T(8,128)(2,1)S(1)} all-to-all(bf16[4,64,8,1024]{3,1,2,0:T(8,128)(2,1)S(1)} %broadcast_in_dim.22), channel_id=1, replica_groups=mesh['dp'=4,'expert'=64] {'dp'}, dimensions={0} | all-to-all | bytes 8388608 | tf_op jit(solution)/shard_map/all_to_all | solution.py:92
  410.5 24.7 %fusion.2 = bf16[1024,1792]{1,0:T(8,128)(2,1)} fusion(bf16[64,4,8,1792]{3,1,2,0:T(4,128)(2,1)S(1)} %bitcast.130, bf16[4,64,8,1024]{3,1,2,0:T(8,128)(2,1)S(1)} %all_to_all.27), kind=kOutput, calls=%fused_computation.10 | convolution fusion | flops 7516192768 | bytes 15204352 | tf_op jit(solution)/shard_map/gscf,sgcd->fd/dot_general | solution.py:108
  435.2 2.0 fusion.15
  437.3 0.2 copy.151
  437.5 0.2 copy.152
  437.6 0.2 copy.153
  437.8 2.1 concatenate.13
  439.9 10.6 %all-to-all-start.4 = ((bf16[64,8,1152]{2,1,0:T(8,128)(2,1)}), bf16[64,8,1152]{2,1,0:T(8,128)(2,1)S(1)}, u32[]{:S(2)}, u32[]{:S(2)}) async-start(bf16[64,8,1152]{2,1,0:T(8,128)(2,1)} %concatenate.13), calls=%async_computation.5 | async-start | bytes 2359296 | tf_op jit(solution)/shard_map/all_to_all | solution.py:115
  450.6 31.3 %all-to-all-done.4 = bf16[64,8,1152]{2,1,0:T(8,128)(2,1)S(1)} async-done(((bf16[64,8,1152]{2,1,0:T(8,128)(2,1)}), bf16[64,8,1152]{2,1,0:T(8,128)(2,1)S(1)}, u32[]{:S(2)}, u32[]{:S(2)}) %all-to-all-start.4) | async-done | bytes 1179680 | tf_op jit(solution)/shard_map/all_to_all | solution.py:115
  481.9 0.1 slice_bitcast_fusion
  482.0 1.2 gather_fusion.3
  483.2 1.0 reshape.261
  484.2 0.3 fusion.31
  484.6 1.9 gather_fusion.4
  486.6 0.1 reshape.262
  486.7 0.6 copy.154
  (80 shorter events, 2.0 us)
Async XLA Ops:
  7.8 5.8 %copy-start.5 = (s32[128,2]{0,1:T(2,128)S(1)}, s32[128,2]{0,1:T(2,128)}, u32[]{:S(2)}) copy-start(s32[128,2]{0,1:T(2,128)} %param.8) | copy-start | bytes 3076
  17.4 32.1 %copy-start.8 = (s32[2]{0:T(128)S(1)}, s32[2]{0:T(128)}, u32[]{:S(2)}) copy-start(s32[2]{0:T(128)} %constant.85) | copy-start | bytes 28
  17.4 32.3 %copy-start.7 = (s32[2]{0:T(128)S(1)}, s32[2]{0:T(128)}, u32[]{:S(2)}) copy-start(s32[2]{0:T(128)} %constant.88) | copy-start | bytes 28
  17.4 28.4 %all-to-all-start.2 = ((bf16[4,128,1920]{2,1,0:T(8,128)(2,1)}), bf16[4,128,1920]{2,1,0:T(8,128)(2,1)S(1)}, u32[]{:S(2)}, u32[]{:S(2)}) async-start(bf16[4,128,1920]{2,1,0:T(8,128)(2,1)} %pad_maximum_fusion.1), calls=%async_computation.2 | async-start | bytes 3932160 | tf_op jit(solution)/shard_map/all_to_all | solution.py:62
  22.6 412.6 %reduce-scatter.2.cloned.1.call-start = ((), (), s32[]{:S(2)}) async-start(), calls=%async_computation.6 | async-start | bytes 10485760 | tf_op jit(solution)/shard_map/reduce_scatter | solution.py:106
  45.8 9.1 %copy-start.1 = (bf16[4,128,1920]{2,1,0:T(8,128)(2,1)}, bf16[4,128,1920]{2,1,0:T(8,128)(2,1)S(1)}, u32[]{:S(2)}) copy-start(bf16[4,128,1920]{2,1,0:T(8,128)(2,1)S(1)} %all-to-all-done.2) | copy-start | bytes 5898244
  265.5 10.7 %copy-start = (bf16[64,4,8,1792]{3,1,2,0:T(4,128)(2,1)}, bf16[64,4,8,1792]{3,1,2,0:T(4,128)(2,1)S(1)}, u32[]{:S(2)}) copy-start(bf16[64,4,8,1792]{3,1,2,0:T(4,128)(2,1)S(1)} %all_to_all.25) | copy-start | bytes 22020100
  265.5 10.7 %copy-start.9 = (bf16[1,1024,1792]{2,1,0:T(8,128)(2,1)S(1)}, bf16[1,1024,1792]{2,1,0:T(8,128)(2,1)}, u32[]{:S(2)}) copy-start(bf16[1,1024,1792]{2,1,0:T(8,128)(2,1)} %param.11) | copy-start | bytes 11010052
  288.2 1.6 copy-start.6
  288.3 8.9 %copy-start.2 = (bf16[128,2,1024]{2,1,0:T(2,128)(2,1)S(1)}, bf16[128,2,1024]{2,1,0:T(2,128)(2,1)}, u32[]{:S(2)}) copy-start(bf16[128,2,1024]{2,1,0:T(2,128)(2,1)} %param.7) | copy-start | bytes 1572868
  297.3 2.1 copy-start.3
  297.4 2.1 copy-start.4
  339.9 70.6 %slice-start = ((s8[7340032]{0:T(1024)(128)(4,1)}), s8[4194304]{0:T(1024)(128)(4,1)S(1)}, s32[]{:S(2)}) async-start(s8[7340032]{0:T(1024)(128)(4,1)} %bitcast.129), calls=%async_computation.7 | async-start | bytes 8388608
  340.5 70.0 %slice-start.1 = ((s8[7340032]{0:T(1024)(128)(4,1)}), s8[3145728]{0:T(1024)(128)(4,1)S(1)}, s32[]{:S(2)}) async-start(s8[7340032]{0:T(1024)(128)(4,1)} %bitcast.129), calls=%async_computation.8 | async-start | bytes 6291456
  439.9 42.0 %all-to-all-start.4 = ((bf16[64,8,1152]{2,1,0:T(8,128)(2,1)}), bf16[64,8,1152]{2,1,0:T(8,128)(2,1)S(1)}, u32[]{:S(2)}, u32[]{:S(2)}) async-start(bf16[64,8,1152]{2,1,0:T(8,128)(2,1)} %concatenate.13), calls=%async_computation.5 | async-start | bytes 2359296 | tf_op jit(solution)/shard_map/all_to_all | solution.py:115
Sparse Core Ops, SparseCore 0:
  288.4 111.3 reduce-scatter.1

commit v9 on v2

--- a/solution.py
+++ b/solution.py
@@ -47,24 +47,12 @@
     slot_count = local_tokens * top_count
     quarter = cotangent.shape[1] // groups
 
+    routes_all = lax.all_gather(routes.reshape(slot_count), "dp", axis=0, tiled=False)
+    _, slot_of_all = jax.vmap(lambda r: slots_for(r, columns, capacity))(routes_all)
     destination, slot_of = slots_for(routes.reshape(slot_count), columns, capacity)
 
-    route_lanes = jnp.zeros((local_tokens, LANES), jnp.bfloat16).at[:, :top_count].set(
-        routes.astype(jnp.bfloat16)
-    )
-    cot_split = jnp.concatenate(
-        [
-            cotangent.reshape(local_tokens, groups, quarter).transpose(1, 0, 2),
-            jnp.broadcast_to(route_lanes[None], (groups, local_tokens, LANES)),
-        ],
-        axis=2,
-    )
-    received = lax.all_to_all(cot_split, "dp", split_axis=0, concat_axis=0, tiled=True)
-    cot_q = received[:, :, :quarter]
-    routes_all = received[:, :, quarter : quarter + top_count].astype(jnp.int32)
-    _, slot_of_all = jax.vmap(lambda r: slots_for(r, columns, capacity))(
-        routes_all.reshape(groups, slot_count)
-    )
+    cot_split = cotangent.reshape(local_tokens, groups, quarter).transpose(1, 0, 2)
+    cot_q = lax.all_to_all(cot_split, "dp", split_axis=0, concat_axis=0, tiled=True)
     token_of = jnp.minimum(slot_of_all // top_count, local_tokens - 1)
     token_of = token_of.reshape(groups, columns, capacity).transpose(1, 0, 2)
     flat_token = token_of + (jnp.arange(groups, dtype=jnp.int32) * local_tokens)[None, :, None]

time: 409 us -> 400 us (0.978)
  blocking collectives: 215 us -> 239 us
  waiting for transfers between devices: 82 us -> 58.9 us
  local copies, waits for them, and re-layouts: 44.4 us -> 38.7 us
  other arithmetic: 15.4 us -> 11.1 us
    all_gather x0 -> x1, blocking collectives: none -> 23.3 us  [per_device(): lax.all_gather(routes.reshape(slot_count), 'dp', axis=0, tiled=False)]
    all_to_all x1, waiting for transfers between devices: 23.2 us -> 0.01 us  [per_device(): lax.all_to_all(cot_split, 'dp', split_axis=0, concat_axis=0, tiled=True)]
    unnamed x34 -> x28, local copies, waits for them, and re-layouts: 9.18 us -> 5.38 us
  transfers between devices with their start and end apart: 4 -> 4, of which waited for: 4 -> 3; matrix products, arithmetic and copies ran while one was open for 5% -> 7% of each run, Pallas kernels for 0% -> 0%
where the time goes in v9:
time: 400 us; the launch traced here: 399 us
  blocking collectives  239 us (60%)
  waiting for transfers between devices  58.9 us (15%)
  local copies, waits for them, and re-layouts  38.7 us (10%)
  matrix products  21.5 us (5%)
  starting transfers between devices  15.9 us (4%)
  between operations  14.4 us (4%)
  other arithmetic  11.1 us (3%)
    all_to_all x1, blocking collectives, per_device(): lax.all_to_all(send_cot, 'expert', split_axis=0, concat_axis=0, tiled=True)  178 us
    all_to_all x1, blocking collectives, per_device(): lax.all_to_all(jnp.concatenate([send_hidden, split3(send_gates)], axis=2)...  37.6 us
    all_to_all x1, waiting for transfers between devices, per_device(): lax.all_to_all(jnp.concatenate([grad_hidden_rows, split3(grad_gates_rows)...  31.3 us
    reduce_scatter x1, waiting for transfers between devices, per_device(): lax.psum_scatter(partial_back, 'dp', scatter_dimension=0, tiled=True)[0]  27.2 us
    all_gather x1, blocking collectives, per_device(): lax.all_gather(routes.reshape(slot_count), 'dp', axis=0, tiled=False)  23.3 us
    dot_general x1, matrix products, per_device(): jnp.einsum('gscf,sgcd->fd', rows_all, got_cot, preferred_element_type=jnp...  13.1 us
    all_to_all x1, starting transfers between devices, per_device(): lax.all_to_all(jnp.concatenate([grad_hidden_rows, split3(grad_gates_rows)...  10.7 us
    gather x1, local copies, waits for them, and re-layouts, per_device(): send_cot = cot_q.reshape(groups * local_tokens, quarter)[flat_token]  10.6 us
  transfers between devices with their start and end apart: 4, of which 3 were waited for; matrix products, arithmetic and copies ran while one was open for 7% of the time, Pallas kernels for 0%

profile of v9, /device:TPU:1, one launch (start us, length us, event | category | flops | bytes accessed | tf_op | source)
XLA Modules:
  0.0 399.5 jit_solution(3503107045734127546)
XLA Ops:
  7.2 2.9 copy.112
  10.0 5.1 %all-to-all-start.1 = ((bf16[4,128,1792]{2,1,0:T(8,128)(2,1)}), bf16[4,128,1792]{2,1,0:T(8,128)(2,1)S(1)}, u32[]{:S(2)}, u32[]{:S(2)}) async-start(bf16[4,128,1792]{2,1,0:T(8,128)(2,1)} %bitcast.143), calls=%async_computation.1 | async-start | bytes 3670016 | tf_op jit(solution)/shard_map/all_to_all | solution.py:55
  15.2 0.1 copy.57
  15.3 0.1 reshape.262
  15.4 23.3 %all-gather.1 = s32[4,1,256]{2,1,0:T(1,128)S(1)} all-gather(s32[1,1,256]{2,1,0:T(1,128)S(1)} %reshape.262), channel_id=1, replica_groups=mesh['dp'=4,'expert'=64] {'dp'}, dimensions={0}, use_global_device_ids=true | all-gather | bytes 5120 | tf_op jit(solution)/shard_map/all_gather | solution.py:50
  38.7 2.4 reduce-window.16
  41.1 0.1 slice.91
  41.3 0.1 copy.70
  41.4 0.2 fusion.26
  41.6 0.1 multiply_reduce_fusion
  41.7 0.1 and_reduce_fusion
  41.8 4.3 %scatter_custom_fusion.1 = s32[2048]{0:T(1024)S(1)} fusion(s32[1024]{0:T(1024)S(1)} %bitcast.152, s32[1024]{0:T(1024)S(1)} %bitcast.153, s32[]{:T(128)} %constant.14.clone.1), kind=kCustom, calls=%fused_computation.92 | custom fusion | bytes 8196
  46.2 0.1 reshape.195
  46.3 0.1 compare_select_fusion
  46.4 0.1 copy.73
  46.5 0.2 reshape.221
  46.7 10.6 %gather_fusion.2 = bf16[2048,1792]{1,0:T(8,128)(2,1)} fusion(bf16[512,1792]{1,0:T(8,128)(2,1)S(1)} %bitcast.141, s32[2048]{0:T(1024)S(1)} %broadcast_clamp_fusion), kind=kCustom, calls=%fused_computation.2 | custom fusion | bytes 14688256 | tf_op jit(solution)/shard_map/gather | solution.py:59
  57.3 178.2 %all_to_all.20 = bf16[64,4,8,1792]{3,2,1,0:T(8,128)(2,1)S(1)} all-to-all(bf16[64,4,8,1792]{3,2,1,0:T(8,128)(2,1)} %bitcast.142), channel_id=1, replica_groups=mesh['dp'=4,'expert'=64] {'expert'}, dimensions={0} | all-to-all | bytes 14680064 | tf_op jit(solution)/shard_map/all_to_all | solution.py:60
  235.5 2.1 fusion.12
  237.6 2.1 fusion.15
  239.7 2.1 fusion.18
  241.8 2.1 fusion.21
  243.9 3.8 pad_maximum_fusion
  247.8 0.1 eq.52
  247.9 0.1 eq.48
  248.1 0.6 reduce-window.14
  248.7 0.2 slice_reduce_fusion
  248.9 0.1 copy.56
  249.1 0.1 mul.56
  249.2 0.1 copy.60
  249.3 0.1 reshape.190
  249.5 0.1 fusion.31
  249.6 1.4 scatter_custom_fusion
  251.0 3.5 gather_fusion.1
  254.6 0.1 reshape.191
  254.6 0.1 copy.61
  254.7 0.2 copy.63
  254.9 0.8 copy.64
  255.7 0.8 copy.65
  256.6 0.2 reshape.187
  256.8 2.1 gather_fusion
  258.9 1.6 concatenate.6
  260.5 37.6 %all_to_all.21 = bf16[64,8,1152]{2,1,0:T(8,128)(2,1)S(1)} all-to-all(bf16[64,8,1152]{2,1,0:T(8,128)(2,1)S(1)} %concatenate.6), channel_id=1, replica_groups=mesh['dp'=4,'expert'=64] {'expert'}, dimensions={0} | all-to-all | bytes 2359296 | tf_op jit(solution)/shard_map/all_to_all | solution.py:69
  298.1 0.2 slice_add_fusion.2
  298.3 0.4 copy.85
  298.7 27.2 %reduce-scatter.2.cloned.1.call-done = f32[1,64,8,1024]{3,2,1,0:T(8,128)} async-done(((f32[4,64,8,1024]{3,2,1,0:T(8,128)}), f32[1,64,8,1024]{3,2,1,0:T(8,128)}) %reduce-scatter.2.cloned.1.call-update) | async-done | bytes 2097168 | tf_op jit(solution)/shard_map/reduce_scatter | solution.py:88
  326.0 3.0 fusion.9
  329.0 0.1 copy.78
  329.1 0.2 copy.79
  329.3 0.2 copy.80
  329.4 0.2 copy.81
  329.6 2.1 concatenate.7
  331.7 10.7 %all-to-all-start.3 = ((bf16[64,8,1152]{2,1,0:T(8,128)(2,1)}), bf16[64,8,1152]{2,1,0:T(8,128)(2,1)S(1)}, u32[]{:S(2)}, u32[]{:S(2)}) async-start(bf16[64,8,1152]{2,1,0:T(8,128)(2,1)} %concatenate.7), calls=%async_computation.4 | async-start | bytes 2359296 | tf_op jit(solution)/shard_map/all_to_all | solution.py:94
  342.4 31.3 %all-to-all-done.3 = bf16[64,8,1152]{2,1,0:T(8,128)(2,1)S(1)} async-done(((bf16[64,8,1152]{2,1,0:T(8,128)(2,1)}), bf16[64,8,1152]{2,1,0:T(8,128)(2,1)S(1)}, u32[]{:S(2)}, u32[]{:S(2)}) %all-to-all-start.3) | async-done | bytes 1179680 | tf_op jit(solution)/shard_map/all_to_all | solution.py:94
  373.7 0.1 slice_bitcast_fusion.16
  373.9 1.2 gather_fusion.3
  375.1 1.0 reshape.197
  376.1 0.3 fusion.27
  376.4 0.1 add.90
  376.5 1.9 gather_fusion.4
  378.4 0.1 reshape.198
  378.6 0.6 copy.83
  379.2 0.3 all-gather.4.cloned.1.call-done
  379.5 13.1 %fusion.8 = bf16[1,1024,1792]{2,1,0:T(8,128)(2,1)} fusion(bf16[4,64,8,1024]{3,2,1,0:T(8,128)(2,1)} %bitcast.154, bf16[64,4,8,1792]{3,2,1,0:T(8,128)(2,1)} %copy-done), kind=kOutput, calls=%fused_computation.17 | convolution fusion | flops 7518027776 | bytes 15204352 | tf_op jit(solution)/shard_map/gscf,sgcd->fd/dot_general | solution.py:89
  (53 shorter events, 0.4 us)
Async XLA Ops:
  7.2 8.0 %copy-start.4 = (s32[128,2]{0,1:T(2,128)S(1)}, s32[128,2]{0,1:T(2,128)}, u32[]{:S(2)}) copy-start(s32[128,2]{0,1:T(2,128)} %param.6) | copy-start | bytes 3076
  10.0 31.6 %copy-start.7 = (s32[2]{0:T(128)S(1)}, s32[2]{0:T(128)}, u32[]{:S(2)}) copy-start(s32[2]{0:T(128)} %constant.52) | copy-start | bytes 28
  10.0 31.7 %copy-start.6 = (s32[2]{0:T(128)S(1)}, s32[2]{0:T(128)}, u32[]{:S(2)}) copy-start(s32[2]{0:T(128)} %constant.55) | copy-start | bytes 28
  10.0 36.6 %all-to-all-start.1 = ((bf16[4,128,1792]{2,1,0:T(8,128)(2,1)}), bf16[4,128,1792]{2,1,0:T(8,128)(2,1)S(1)}, u32[]{:S(2)}, u32[]{:S(2)}) async-start(bf16[4,128,1792]{2,1,0:T(8,128)(2,1)} %bitcast.143), calls=%async_computation.1 | async-start | bytes 3670016 | tf_op jit(solution)/shard_map/all_to_all | solution.py:55
  15.2 310.8 %reduce-scatter.2.cloned.1.call-start = ((), (), s32[]{:S(2)}) async-start(), calls=%async_computation.5 | async-start | bytes 10485760 | tf_op jit(solution)/shard_map/reduce_scatter | solution.py:88
  57.3 178.2 %copy-start.8 = (bf16[1,1024,1792]{2,1,0:T(8,128)(2,1)S(1)}, bf16[1,1024,1792]{2,1,0:T(8,128)(2,1)}, u32[]{:S(2)}) copy-start(bf16[1,1024,1792]{2,1,0:T(8,128)(2,1)} %param.9) | copy-start | bytes 11010052
  235.5 6.3 %copy-start = (bf16[64,4,8,1792]{3,2,1,0:T(8,128)(2,1)}, bf16[64,4,8,1792]{3,2,1,0:T(8,128)(2,1)S(1)}, u32[]{:S(2)}) copy-start(bf16[64,4,8,1792]{3,2,1,0:T(8,128)(2,1)S(1)} %all_to_all.20) | copy-start | bytes 22020100
  247.7 1.5 copy-start.5
  247.7 8.8 %copy-start.1 = (bf16[128,2,1024]{2,1,0:T(2,128)(2,1)S(1)}, bf16[128,2,1024]{2,1,0:T(2,128)(2,1)}, u32[]{:S(2)}) copy-start(bf16[128,2,1024]{2,1,0:T(2,128)(2,1)} %param.5) | copy-start | bytes 1572868
  247.8 131.8 %all-gather.4.cloned.1.call-start = ((), (), s32[]{:S(2)}) async-start(), calls=%async_computation.6 | async-start | bytes 5242880 | tf_op jit(solution)/shard_map/all_gather | solution.py:80
  256.8 2.1 copy-start.2
  256.8 2.1 copy-start.3
  331.7 42.0 %all-to-all-start.3 = ((bf16[64,8,1152]{2,1,0:T(8,128)(2,1)}), bf16[64,8,1152]{2,1,0:T(8,128)(2,1)S(1)}, u32[]{:S(2)}, u32[]{:S(2)}) async-start(bf16[64,8,1152]{2,1,0:T(8,128)(2,1)} %concatenate.7), calls=%async_computation.4 | async-start | bytes 2359296 | tf_op jit(solution)/shard_map/all_to_all | solution.py:94
Sparse Core Ops, SparseCore 0:
  247.9 78.0 reduce-scatter.1
  329.1 50.3 all-gather.3

commit v10 on v9

--- a/solution.py
+++ b/solution.py
@@ -47,7 +47,13 @@
     slot_count = local_tokens * top_count
     quarter = cotangent.shape[1] // groups
 
-    routes_all = lax.all_gather(routes.reshape(slot_count), "dp", axis=0, tiled=False)
+    routes_all = lax.all_to_all(
+        jnp.broadcast_to(routes.reshape(1, slot_count), (groups, slot_count)),
+        "dp",
+        split_axis=0,
+        concat_axis=0,
+        tiled=True,
+    )
     _, slot_of_all = jax.vmap(lambda r: slots_for(r, columns, capacity))(routes_all)
     destination, slot_of = slots_for(routes.reshape(slot_count), columns, capacity)
 

time: 400 us -> 396 us (0.990)
  blocking collectives: 239 us -> 216 us
  waiting for transfers between devices: 58.9 us -> 73.4 us
    all_gather x1 -> x0, blocking collectives: 23.3 us -> none  [per_device(): lax.all_gather(routes.reshape(slot_count), 'dp', axis=0, tiled=False)]
    all_to_all x1, waiting for transfers between devices: 0.01 us -> 13 us  [per_device(): lax.all_to_all(cot_split, 'dp', split_axis=0, concat_axis=0, tiled=True)]
    all_to_all x0 -> x1, starting transfers between devices: none -> 5 us  [per_device(): lax.all_to_all(jnp.broadcast_to(routes.reshape(1, slot_count), (groups, s...]
  transfers between devices with their start and end apart: 4 -> 5, of which waited for: 3 -> 5; matrix products, arithmetic and copies ran while one was open for 7% -> 8% of each run, Pallas kernels for 0% -> 0%
where the time goes in v10:
time: 396 us
  blocking collectives  216 us (55%)
  waiting for transfers between devices  73.4 us (19%)
  local copies, waits for them, and re-layouts  39.8 us (10%)
  matrix products  21.5 us (5%)
  starting transfers between devices  19.4 us (5%)
  between operations  14.5 us (4%)
  other arithmetic  11.1 us (3%)
    all_to_all x1, blocking collectives, per_device(): lax.all_to_all(send_cot, 'expert', split_axis=0, concat_axis=0, tiled=True)  179 us
    all_to_all x1, blocking collectives, per_device(): lax.all_to_all(jnp.concatenate([send_hidden, split3(send_gates)], axis=2)...  37.6 us
    all_to_all x1, waiting for transfers between devices, per_device(): lax.all_to_all(jnp.concatenate([grad_hidden_rows, split3(grad_gates_rows)...  31.3 us
    reduce_scatter x1, waiting for transfers between devices, per_device(): lax.psum_scatter(partial_back, 'dp', scatter_dimension=0, tiled=True)[0]  27.4 us
    dot_general x1, matrix products, per_device(): jnp.einsum('gscf,sgcd->fd', rows_all, got_cot, preferred_element_type=jnp...  13.1 us
    all_to_all x1, waiting for transfers between devices, per_device(): lax.all_to_all(cot_split, 'dp', split_axis=0, concat_axis=0, tiled=True)  13 us
    all_to_all x1, starting transfers between devices, per_device(): lax.all_to_all(jnp.concatenate([grad_hidden_rows, split3(grad_gates_rows)...  10.7 us
    gather x1, local copies, waits for them, and re-layouts, per_device(): send_cot = cot_q.reshape(groups * local_tokens, quarter)[flat_token]  10.6 us
  transfers between devices with their start and end apart: 5, of which 5 were waited for; matrix products, arithmetic and copies ran while one was open for 8% of the time, Pallas kernels for 0%

profile of v10, /device:TPU:1, one launch (start us, length us, event | category | flops | bytes accessed | tf_op | source)
XLA Modules:
  0.0 395.6 jit_solution(759111447614625458)
XLA Ops:
  7.2 0.8 copy.55
  8.0 0.1 eq.50
  8.1 0.6 broadcast_in_dim.19
  8.7 5.0 %all-to-all-start.2 = ((s32[4,1,256]{2,1,0:T(1,128)}), s32[4,1,256]{2,1,0:T(1,128)S(1)}, u32[]{:S(2)}, u32[]{:S(2)}) async-start(s32[4,1,256]{2,1,0:T(1,128)} %broadcast_in_dim.19), calls=%async_computation.2 | async-start | bytes 8192 | tf_op jit(solution)/shard_map/all_to_all | solution.py:50
  13.7 2.9 copy.107
  16.6 1.3 all-to-all-done.2
  17.8 3.6 all-to-all-start.1
  21.5 2.4 reduce-window.16
  23.9 0.1 slice.91
  24.1 0.1 copy.67
  24.2 0.2 fusion.26
  24.4 0.1 multiply_reduce_fusion
  24.5 0.1 and_reduce_fusion
  24.6 4.3 %scatter_custom_fusion.1 = s32[2048]{0:T(1024)S(1)} fusion(s32[1024]{0:T(1024)S(1)} %bitcast.153, s32[1024]{0:T(1024)S(1)} %bitcast.152, s32[]{:T(128)} %constant.14.clone.1), kind=kCustom, calls=%fused_computation.92 | custom fusion | bytes 8196
  29.0 0.1 reshape.234
  29.1 0.1 compare_select_fusion
  29.2 0.1 copy.70
  29.3 0.2 reshape.260
  29.4 13.0 %all-to-all-done.1 = bf16[4,128,1792]{2,1,0:T(8,128)(2,1)S(1)} async-done(((bf16[4,128,1792]{2,1,0:T(8,128)(2,1)}), bf16[4,128,1792]{2,1,0:T(8,128)(2,1)S(1)}, u32[]{:S(2)}, u32[]{:S(2)}) %all-to-all-start.1) | async-done | bytes 1835040 | tf_op jit(solution)/shard_map/all_to_all | solution.py:61
  42.5 10.6 %gather_fusion.2 = bf16[2048,1792]{1,0:T(8,128)(2,1)} fusion(bf16[512,1792]{1,0:T(8,128)(2,1)S(1)} %bitcast.141, s32[2048]{0:T(1024)S(1)} %broadcast_clamp_fusion), kind=kCustom, calls=%fused_computation.2 | custom fusion | bytes 14688256 | tf_op jit(solution)/shard_map/gather | solution.py:65
  53.1 178.5 %all_to_all.26 = bf16[64,4,8,1792]{3,2,1,0:T(8,128)(2,1)S(1)} all-to-all(bf16[64,4,8,1792]{3,2,1,0:T(8,128)(2,1)} %bitcast.142), channel_id=1, replica_groups=mesh['dp'=4,'expert'=64] {'expert'}, dimensions={0} | all-to-all | bytes 14680064 | tf_op jit(solution)/shard_map/all_to_all | solution.py:66
  231.6 2.1 fusion.12
  233.7 2.1 fusion.15
  235.8 2.1 fusion.18
  237.9 2.1 fusion.21
  240.0 3.8 pad_maximum_fusion
  243.9 0.1 eq.54
  244.1 0.6 reduce-window.14
  244.7 0.2 slice_reduce_fusion
  244.9 0.1 copy.54
  245.0 0.1 mul.66
  245.2 0.1 copy.58
  245.3 0.1 reshape.229
  245.5 0.1 fusion.31
  245.6 1.4 scatter_custom_fusion
  247.0 3.5 gather_fusion.1
  250.5 0.1 reshape.230
  250.7 0.2 copy.61
  250.9 0.8 copy.62
  251.7 0.8 copy.63
  252.5 0.2 reshape.226
  252.8 2.1 gather_fusion
  254.9 1.6 concatenate.6
  256.5 37.6 %all_to_all.27 = bf16[64,8,1152]{2,1,0:T(8,128)(2,1)S(1)} all-to-all(bf16[64,8,1152]{2,1,0:T(8,128)(2,1)S(1)} %concatenate.6), channel_id=1, replica_groups=mesh['dp'=4,'expert'=64] {'expert'}, dimensions={0} | all-to-all | bytes 2359296 | tf_op jit(solution)/shard_map/all_to_all | solution.py:75
  294.1 0.2 slice_add_fusion.2
  294.3 0.4 copy.82
  294.7 27.4 %reduce-scatter.2.cloned.1.call-done = f32[1,64,8,1024]{3,2,1,0:T(8,128)} async-done(((f32[4,64,8,1024]{3,2,1,0:T(8,128)}), f32[1,64,8,1024]{3,2,1,0:T(8,128)}) %reduce-scatter.2.cloned.1.call-update) | async-done | bytes 2097168 | tf_op jit(solution)/shard_map/reduce_scatter | solution.py:94
  322.1 3.0 fusion.9
  325.2 0.2 copy.76
  325.4 0.2 copy.77
  325.6 0.2 copy.78
  325.7 2.1 concatenate.7
  327.8 10.7 %all-to-all-start.4 = ((bf16[64,8,1152]{2,1,0:T(8,128)(2,1)}), bf16[64,8,1152]{2,1,0:T(8,128)(2,1)S(1)}, u32[]{:S(2)}, u32[]{:S(2)}) async-start(bf16[64,8,1152]{2,1,0:T(8,128)(2,1)} %concatenate.7), calls=%async_computation.5 | async-start | bytes 2359296 | tf_op jit(solution)/shard_map/all_to_all | solution.py:100
  338.6 31.3 %all-to-all-done.4 = bf16[64,8,1152]{2,1,0:T(8,128)(2,1)S(1)} async-done(((bf16[64,8,1152]{2,1,0:T(8,128)(2,1)}), bf16[64,8,1152]{2,1,0:T(8,128)(2,1)S(1)}, u32[]{:S(2)}, u32[]{:S(2)}) %all-to-all-start.4) | async-done | bytes 1179680 | tf_op jit(solution)/shard_map/all_to_all | solution.py:100
  369.9 0.1 slice_bitcast_fusion.16
  370.0 1.2 gather_fusion.3
  371.2 1.0 reshape.236
  372.2 0.3 fusion.27
  372.5 0.1 add.104
  372.6 1.9 gather_fusion.4
  374.6 0.1 reshape.237
  374.7 0.6 copy.80
  375.4 0.3 all-gather.3.cloned.1.call-done
  375.7 13.1 %fusion.8 = bf16[1,1024,1792]{2,1,0:T(8,128)(2,1)} fusion(bf16[4,64,8,1024]{3,2,1,0:T(8,128)(2,1)} %bitcast.154, bf16[64,4,8,1792]{3,2,1,0:T(8,128)(2,1)} %copy-done), kind=kOutput, calls=%fused_computation.17 | convolution fusion | flops 7518027776 | bytes 15204352 | tf_op jit(solution)/shard_map/gscf,sgcd->fd/dot_general | solution.py:95
  (54 shorter events, 0.5 us)
Async XLA Ops:
  8.7 9.1 %all-to-all-start.2 = ((s32[4,1,256]{2,1,0:T(1,128)}), s32[4,1,256]{2,1,0:T(1,128)S(1)}, u32[]{:S(2)}, u32[]{:S(2)}) async-start(s32[4,1,256]{2,1,0:T(1,128)} %broadcast_in_dim.19), calls=%async_computation.2 | async-start | bytes 8192 | tf_op jit(solution)/shard_map/all_to_all | solution.py:50
  16.6 7.8 %copy-start.7 = (s32[2]{0:T(128)S(1)}, s32[2]{0:T(128)}, u32[]{:S(2)}) copy-start(s32[2]{0:T(128)} %constant.52) | copy-start | bytes 28
  16.6 7.9 %copy-start.6 = (s32[2]{0:T(128)S(1)}, s32[2]{0:T(128)}, u32[]{:S(2)}) copy-start(s32[2]{0:T(128)} %constant.55) | copy-start | bytes 28
  17.8 24.6 %all-to-all-start.1 = ((bf16[4,128,1792]{2,1,0:T(8,128)(2,1)}), bf16[4,128,1792]{2,1,0:T(8,128)(2,1)S(1)}, u32[]{:S(2)}, u32[]{:S(2)}) async-start(bf16[4,128,1792]{2,1,0:T(8,128)(2,1)} %bitcast.143), calls=%async_computation.1 | async-start | bytes 3670016 | tf_op jit(solution)/shard_map/all_to_all | solution.py:61
  21.4 300.6 %reduce-scatter.2.cloned.1.call-start = ((), (), s32[]{:S(2)}) async-start(), calls=%async_computation.6 | async-start | bytes 10485760 | tf_op jit(solution)/shard_map/reduce_scatter | solution.py:94
  53.1 178.5 %copy-start.8 = (bf16[1,1024,1792]{2,1,0:T(8,128)(2,1)S(1)}, bf16[1,1024,1792]{2,1,0:T(8,128)(2,1)}, u32[]{:S(2)}) copy-start(bf16[1,1024,1792]{2,1,0:T(8,128)(2,1)} %param.9) | copy-start | bytes 11010052
  231.6 6.3 %copy-start = (bf16[64,4,8,1792]{3,2,1,0:T(8,128)(2,1)}, bf16[64,4,8,1792]{3,2,1,0:T(8,128)(2,1)S(1)}, u32[]{:S(2)}) copy-start(bf16[64,4,8,1792]{3,2,1,0:T(8,128)(2,1)S(1)} %all_to_all.26) | copy-start | bytes 22020100
  243.8 1.1 copy-start.4
  243.8 1.3 copy-start.5
  243.8 8.7 %copy-start.1 = (bf16[128,2,1024]{2,1,0:T(2,128)(2,1)S(1)}, bf16[128,2,1024]{2,1,0:T(2,128)(2,1)}, u32[]{:S(2)}) copy-start(bf16[128,2,1024]{2,1,0:T(2,128)(2,1)} %param.5) | copy-start | bytes 1572868
  243.9 131.8 %all-gather.3.cloned.1.call-start = ((), (), s32[]{:S(2)}) async-start(), calls=%async_computation.7 | async-start | bytes 5242880 | tf_op jit(solution)/shard_map/all_gather | solution.py:86
  252.7 2.1 copy-start.2
  252.7 2.1 copy-start.3
  327.8 42.1 %all-to-all-start.4 = ((bf16[64,8,1152]{2,1,0:T(8,128)(2,1)}), bf16[64,8,1152]{2,1,0:T(8,128)(2,1)S(1)}, u32[]{:S(2)}, u32[]{:S(2)}) async-start(bf16[64,8,1152]{2,1,0:T(8,128)(2,1)} %concatenate.7), calls=%async_computation.5 | async-start | bytes 2359296 | tf_op jit(solution)/shard_map/all_to_all | solution.py:100
Sparse Core Ops, SparseCore 0:
  244.0 78.0 reduce-scatter.1
  325.2 50.4 all-gather.2
